TPU v7x, 768 devices: a whole 4x8x12 slice. The times are simulated.
768 devices in a mesh: slab: 48 (over x, z), tile: 16 (over y, core).
Axes of the slice: x: 4, y: 8, z: 12, core: 2. Of those that a mesh axis runs over, the one named last changes fastest.
Arguments:
- old_fine: float32 [49152, 5, 512], P(('slab', 'tile')), may hold values from -6 to 6
- coarse_fine: float32 [49152, 5, 64], P(('slab', 'tile')), may hold values from -6 to 6
- old_owner: int32 [48, 16, 64], P('slab', 'tile'), may hold values from 0 to 15, as said below
- new_refine: int32 [48, 16, 64], P('slab', 'tile'), may hold values from 0 to 1
- parent_map: int32 [48, 16, 64], P('slab', 'tile'), may hold values from 0 to 63
- courant: float32 [3, 5], replicated, may hold values from 0.05 to 0.3
Outputs:
- fine_next: float32 [5, 384, 512, 128], P(None, 'slab', 'tile')
Inputs may be any that keep to these rules, and one draw needn't show every extreme that they name: `old_owner`: in each slab, old block k of tile t goes to tile (t + o_k) mod 16 with offsets o_k of the slab; every device sends exactly 4 blocks to each tile, and new slot k receives old slot k.
All inputs are finite; a program needn't handle non-finite values.
Results may differ from a plain program's by a relative error of at most 0.0003.
Values sent between devices are 32-bit elements; how exact they have to be, the bound alone decides.
No kernel may reach another device: no remote copies, remote signals or barrier semaphores. Data moves between devices by JAX's collectives and lax.ppermute only.
A program may use at most 64 MiB of HBM per device.

v0:
```python
import jax
import jax.numpy as jnp
from jax import lax
from jax.sharding import PartitionSpec as P

E = 8
BX = 16
BY = 4


def shifted_2(x, axis, by):
    peers = lax.axis_size(axis)
    return lax.ppermute(x, axis, [(i, (i + by) % peers) for i in range(peers)])


def with_halo(block, sides, width):
    for axis, dim in sides:
        count = lax.axis_size(axis)
        forward = [(i, i + 1) for i in range(count - 1)]
        backward = [(target, source) for source, target in forward]
        low = lax.ppermute(
            lax.slice_in_dim(block, block.shape[dim] - width, None, axis=dim), axis, forward
        )
        high = lax.ppermute(lax.slice_in_dim(block, 0, width, axis=dim), axis, backward)
        block = jnp.concatenate([low, block, high], axis=dim)
    return block


def minmod(left, right):
    return 0.5 * (jnp.sign(left) + jnp.sign(right)) * jnp.minimum(jnp.abs(left), jnp.abs(right))


def slopes(cells, axis):
    width = [(0, 0)] * cells.ndim
    width[axis] = (1, 1)
    padded = jnp.pad(cells, width, mode="edge")
    size = cells.shape[axis]
    below = lax.slice_in_dim(padded, 0, size, axis=axis)
    above = lax.slice_in_dim(padded, 2, size + 2, axis=axis)
    return minmod(cells - below, above - cells)


def refine_block(cells):
    nd = cells.ndim
    slope_z = slopes(cells, nd - 3)
    slope_y = slopes(cells, nd - 2)
    slope_x = slopes(cells, nd - 1)
    sigma = jnp.array([-0.25, 0.25], jnp.float32)

    def spread(value):
        return value[..., :, None, :, None, :, None]

    offset = (
        spread(slope_z) * sigma[:, None, None, None, None]
        + spread(slope_y) * sigma[:, None, None]
        + spread(slope_x) * sigma
    )
    fine = spread(cells) + offset
    half = cells.shape[-1]
    return fine.reshape(cells.shape[:-3] + (2 * half, 2 * half, 2 * half))


def advance(padded, courant):
    fields, zp, yp, xp = padded.shape
    zn, yn, xn = (zp - 4, yp - 4, xp - 4)

    def cut(dz, dy, dx):
        return padded[:, 2 + dz : 2 + dz + zn, 2 + dy : 2 + dy + yn, 2 + dx : 2 + dx + xn]

    center = cut(0, 0, 0)
    total = jnp.zeros_like(center)
    for axis, unit in enumerate(((1, 0, 0), (0, 1, 0), (0, 0, 1))):
        lower1 = cut(-unit[0], -unit[1], -unit[2])
        lower2 = cut(-2 * unit[0], -2 * unit[1], -2 * unit[2])
        upper1 = cut(unit[0], unit[1], unit[2])
        face_hi = center + 0.5 * minmod(center - lower1, upper1 - center)
        face_lo = lower1 + 0.5 * minmod(lower1 - lower2, center - lower1)
        total = total + courant[axis][:, None, None, None] * (face_hi - face_lo)
    return center - total


def local(old_fine, coarse_fine, old_owner, new_refine, parent_map, courant):
    tiles = lax.axis_size("tile")
    myself = lax.axis_index("tile")
    blocks, fields, cells = old_fine.shape
    per_peer = blocks // tiles
    half = E // 2
    owner = old_owner.reshape(-1)
    send_order = jnp.argsort(owner, stable=True)
    outgoing = old_fine[send_order].reshape(tiles, per_peer, fields, cells)
    arrived = lax.all_to_all(outgoing, "tile", split_axis=0, concat_axis=0, tiled=True).reshape(
        blocks, fields, cells
    )
    source = (2 * myself - owner) % tiles
    recv_order = jnp.argsort(source, stable=True)
    moved = arrived[jnp.argsort(recv_order)]
    parents = parent_map.reshape(-1)
    interp_all = refine_block(coarse_fine.reshape(blocks, fields, half, half, half)).reshape(
        blocks, fields, cells
    )
    shifted = shifted_2(interp_all, "slab", 1)
    filled = shifted[parents]
    flags = new_refine.reshape(-1)
    refilled = jnp.where((flags == 1)[:, None, None], filled, moved)
    region = (
        refilled.reshape(BY, BX, fields, E, E, E)
        .transpose(2, 3, 0, 4, 1, 5)
        .reshape(fields, E, BY * E, BX * E)
    )
    padded = with_halo(region, (("slab", 1), ("tile", 2)), 2)
    padded = jnp.pad(padded, ((0, 0), (0, 0), (0, 0), (2, 2)))
    return advance(padded, courant)


def solution(mesh):
    in_specs = (
        P(("slab", "tile"), None, None),
        P(("slab", "tile"), None, None),
        P("slab", "tile", None),
        P("slab", "tile", None),
        P("slab", "tile", None),
        P(),
    )
    out_specs = P(None, "slab", "tile", None)
    return jax.shard_map(local, mesh=mesh, in_specs=in_specs, out_specs=out_specs, check_vma=False)
```

profile of v0, /device:TPU:31, one launch (start us, length us, event | category | flops | bytes accessed | tf_op | source)
XLA Modules:
  0.0 112.0 jit_solution(444980356381514003)
XLA Ops:
  0.0 2.8 %sort.48 = (s32[64]{0:T(128)}, s32[64]{0:T(128)S(1)}) sort(s32[64]{0:T(128)} %bitcast.32, s32[64]{0:T(128)S(1)} %iota.11), dimensions={0}, to_apply=%region_0.0 | sort | flops 384 | bytes 1024 | tf_op jit(solution)/shard_map/jit(argsort)/sort | solution.py:89
  2.8 1.5 %gather_fusion.1 = f32[64,5,512]{2,0,1:T(8,128)S(1)} fusion(f32[64,5,512]{2,0,1:T(8,128)S(1)} %copy-done, s32[1024]{0:T(1024)S(1)} %pad_clamp_fusion.1), kind=kCustom, calls=%fused_computation.1 | custom fusion | bytes 1310976 | tf_op jit(solution)/shard_map/gather | solution.py:90
  4.6 0.9 copy.26
  5.4 7.6 %all-to-all-start = ((f32[16,4,5,512]{3,1,2,0:T(4,128)}), f32[16,4,5,512]{3,1,2,0:T(4,128)}, u32[]{:S(2)}, u32[]{:S(2)}) async-start(f32[16,4,5,512]{3,1,2,0:T(4,128)} %copy.26), calls=%async_computation | async-start | bytes 1310720 | tf_op jit(solution)/shard_map/all_to_all | solution.py:91
  13.3 0.9 minimum_multiply_fusion.2
  14.5 0.2 broadcast_multiply_fusion
  15.0 0.8 add_add_fusion
  15.8 0.4 copy.23
  16.2 4.2 %collective-permute-start = (f32[64,5,512]{2,0,1:T(8,128)S(1)}, f32[64,5,512]{2,0,1:T(8,128)S(1)}, u32[]{:S(2)}, u32[]{:S(2)}) collective-permute-start(f32[64,5,512]{2,0,1:T(8,128)S(1)} %copy.23), channel_id=1, source_target_pairs={{0,16},{16,32},{32,48},{48,64},{64,80},{80,96},{96,112},{112,128},... | collective-permute-start | bytes 1966088 | tf_op jit(solution)/shard_map/ppermute | solution.py:13
  20.5 2.0 %sort.49 = (s32[64]{0:T(128)}, s32[64]{0:T(128)S(1)}) sort(s32[64]{0:T(128)S(1)} %and_select_fusion, s32[64]{0:T(128)S(1)} %iota.12), dimensions={0}, to_apply=%region_1.2 | sort | flops 384 | bytes 1024 | tf_op jit(solution)/shard_map/jit(argsort)/sort | solution.py:95
  22.6 2.0 %sort.50 = (s32[64]{0:T(128)}, s32[64]{0:T(128)S(1)}) sort(s32[64]{0:T(128)S(1)} %get-tuple-element.9, s32[64]{0:T(128)S(1)} %iota.13), dimensions={0}, to_apply=%region_2.3 | sort | flops 384 | bytes 1024 | tf_op jit(solution)/shard_map/jit(argsort)/sort | solution.py:96
  24.7 20.8 %collective-permute-done = f32[64,5,512]{2,0,1:T(8,128)S(1)} collective-permute-done((f32[64,5,512]{2,0,1:T(8,128)S(1)}, f32[64,5,512]{2,0,1:T(8,128)S(1)}, u32[]{:S(2)}, u32[]{:S(2)}) %collective-permute-start) | collective-permute-done | bytes 655392 | tf_op jit(solution)/shard_map/ppermute | solution.py:13
  45.5 0.4 copy.24
  45.9 0.6 gather_fusion
  46.5 0.5 copy.25
  47.1 3.8 %gather.14 = f32[4,16,5,8,8,8]{1,0,5,4,3,2:T(4,128)} reshape(f32[64,5,512]{0,2,1:T(8,128)S(1)} %copy.25) | data formatting | bytes 1310720 | tf_op jit(solution)/shard_map/gather | solution.py:102
  50.8 1.3 %copy.27 = f32[16,4,5,512]{3,2,1,0:T(8,128)S(1)} copy(f32[16,4,5,512]{3,1,2,0:T(4,128)} %all-to-all-done) | data formatting | bytes 1310720 | tf_op jit(solution)/shard_map/all_to_all | solution.py:91
  52.2 0.6 gather_fusion.2
  52.8 0.5 copy.28
  53.3 3.8 %gather.17 = f32[4,16,5,8,8,8]{1,0,5,4,3,2:T(4,128)} reshape(f32[64,5,512]{0,2,1:T(8,128)S(1)} %copy.28) | data formatting | bytes 1310720 | tf_op jit(solution)/shard_map/gather | solution.py:96
  57.2 9.9 %select_bitcast_fusion = f32[5,8,4,8,16,8]{4,2,5,3,1,0:T(4,128)} fusion(f32[4,16,5,8,8,8]{1,0,5,4,3,2:T(4,128)} %gather.14, f32[4,16,5,8,8,8]{1,0,5,4,3,2:T(4,128)} %gather.17, pred[4,16]{1,0:T(4,128)(4,1)S(1)} %eq.17), kind=kLoop, calls=%fused_computation.3 | loop fusion | flops 163840 | bytes 1966144 | tf_op jit(solution)/shard_map/transpose | solution.py:107
  67.1 9.4 %copy.29 = f32[5,8,4,8,16,8]{5,4,3,2,1,0:T(8,128)} copy(f32[5,8,4,8,16,8]{4,2,5,3,1,0:T(4,128)} %select_bitcast_fusion) | data formatting | bytes 1310720 | tf_op jit(solution)/shard_map/transpose | solution.py:107
  76.5 7.8 %reshape.100 = f32[5,8,32,128]{3,2,1,0:T(8,128)S(1)} reshape(f32[5,8,4,8,16,8]{5,4,3,2,1,0:T(8,128)} %copy.29) | data formatting | bytes 1310720 | tf_op jit(solution)/shard_map/reshape | solution.py:108
  84.4 1.9 %collective-permute-start.1 = (f32[5,2,32,128]{3,2,1,0:T(8,128)S(1)}, f32[5,2,32,128]{3,2,1,0:T(8,128)S(1)}, u32[]{:S(2)}, u32[]{:S(2)}) collective-permute-start(f32[5,2,32,128]{3,2,1,0:T(8,128)S(1)} %get-tuple-element.16), channel_id=1, source_target_pairs={{0,16},{16,32},{32,48},{48,64},{64,80},{80,96},{96,112},{112,128},... | collective-permute-start | bytes 491528 | tf_op jit(solution)/shard_map/ppermute | solution.py:21
  86.3 5.5 %collective-permute-start.2 = (f32[5,2,32,128]{3,2,1,0:T(8,128)S(1)}, f32[5,2,32,128]{3,2,1,0:T(8,128)S(1)}, u32[]{:S(2)}, u32[]{:S(2)}) collective-permute-start(f32[5,2,32,128]{3,2,1,0:T(8,128)S(1)} %get-tuple-element.15), channel_id=1, source_target_pairs={{16,0},{32,16},{48,32},{64,48},{80,64},{96,80},{112,96},{128,112},... | collective-permute-start | bytes 491528 | tf_op jit(solution)/shard_map/ppermute | solution.py:24
  91.8 1.4 %collective-permute-done.1 = f32[5,2,32,128]{3,2,1,0:T(8,128)S(1)} collective-permute-done((f32[5,2,32,128]{3,2,1,0:T(8,128)S(1)}, f32[5,2,32,128]{3,2,1,0:T(8,128)S(1)}, u32[]{:S(2)}, u32[]{:S(2)}) %collective-permute-start.1) | collective-permute-done | bytes 163872 | tf_op jit(solution)/shard_map/ppermute | solution.py:21
  93.3 0.7 collective-permute-done.2
  94.1 6.3 %collective-permute-start.3 = (f32[5,12,2,128]{3,2,1,0:T(2,128)S(1)}, f32[5,12,2,128]{3,2,1,0:T(2,128)S(1)}, u32[]{:S(2)}, u32[]{:S(2)}) collective-permute-start(f32[5,12,2,128]{3,2,1,0:T(2,128)S(1)} %get-tuple-element.11), channel_id=1, source_target_pairs={{0,1},{1,2},{2,3},{3,4},{4,5},{5,6},{6,7},{7,8},{8,9},{9,10},{10,1... | collective-permute-start | bytes 184328 | tf_op jit(solution)/shard_map/ppermute | solution.py:21
  100.4 2.1 %collective-permute-start.4 = (f32[5,12,2,128]{3,2,1,0:T(2,128)S(1)}, f32[5,12,2,128]{3,2,1,0:T(2,128)S(1)}, u32[]{:S(2)}, u32[]{:S(2)}) collective-permute-start(f32[5,12,2,128]{3,2,1,0:T(2,128)S(1)} %get-tuple-element.12), channel_id=1, source_target_pairs={{1,0},{2,1},{3,2},{4,3},{5,4},{6,5},{7,6},{8,7},{9,8},{10,9},{11,1... | collective-permute-start | bytes 184328 | tf_op jit(solution)/shard_map/ppermute | solution.py:24
  102.6 4.6 %collective-permute-done.4 = f32[5,12,2,128]{3,2,1,0:T(2,128)S(1)} collective-permute-done((f32[5,12,2,128]{3,2,1,0:T(2,128)S(1)}, f32[5,12,2,128]{3,2,1,0:T(2,128)S(1)}, u32[]{:S(2)}, u32[]{:S(2)}) %collective-permute-start.4) | collective-permute-done | bytes 61472 | tf_op jit(solution)/shard_map/ppermute | solution.py:24
  107.2 1.0 select_maximum_fusion
  108.2 3.9 %add_subtract_fusion = f32[5,8,32,128]{3,2,1,0:T(8,128)} fusion(f32[5,8,32,128]{3,2,1,0:T(8,128)S(1)} %reshape.100, f32[5,12,36,132]{3,2,1,0:T(8,128)S(1)} %select_maximum_fusion, f32[5,12,32,128]{3,2,1,0:T(8,128)S(1)} %constant_dynamic-update-slice_fusion.2, f32[5,12,2,128]{3,2,1,0:T(2,128)S(1)} %collective-permute-done.3, ...), kind=kLoop, calls=%fused_computation.22 | loop fusion | flops 12451840 | bytes 5857340 | tf_op jit(solution)/shard_map/sub | solution.py:79
  (42 shorter events, 1.3 us)
Async XLA Ops:
  0.0 2.8 %copy-start = (f32[64,5,512]{2,0,1:T(8,128)S(1)}, f32[64,5,512]{2,0,1:T(8,128)}, u32[]{:S(2)}) copy-start(f32[64,5,512]{2,0,1:T(8,128)} %param.7) | copy-start | bytes 1966084
  4.3 8.7 %copy-start.1 = (f32[64,5,64]{2,0,1:T(8,128)S(1)}, f32[64,5,64]{2,0,1:T(8,128)}, u32[]{:S(2)}) copy-start(f32[64,5,64]{2,0,1:T(8,128)} %param.8) | copy-start | bytes 245764
  4.5 9.7 %copy-start.2 = (f32[2]{0:T(128)S(1)}, f32[2]{0:T(128)}, u32[]{:S(2)}) copy-start(f32[2]{0:T(128)} %constant.34.clone) | copy-start | bytes 28
  5.4 45.4 %all-to-all-start = ((f32[16,4,5,512]{3,1,2,0:T(4,128)}), f32[16,4,5,512]{3,1,2,0:T(4,128)}, u32[]{:S(2)}, u32[]{:S(2)}) async-start(f32[16,4,5,512]{3,1,2,0:T(4,128)} %copy.26), calls=%async_computation | async-start | bytes 1310720 | tf_op jit(solution)/shard_map/all_to_all | solution.py:91
  15.0 5.4 %copy-start.4 = (s32[1,1,64]{2,1,0:T(1,128)S(1)}, s32[1,1,64]{2,1,0:T(1,128)}, u32[]{:S(2)}) copy-start(s32[1,1,64]{2,1,0:T(1,128)} %param.10) | copy-start | bytes 772
  15.0 5.6 %copy-start.5 = (s32[1,1,64]{2,1,0:T(1,128)S(1)}, s32[1,1,64]{2,1,0:T(1,128)}, u32[]{:S(2)}) copy-start(s32[1,1,64]{2,1,0:T(1,128)} %param.9) | copy-start | bytes 772
  15.0 9.7 %copy-start.6 = (s32[1,1,64]{2,1,0:T(1,128)S(1)}, s32[1,1,64]{2,1,0:T(1,128)}, u32[]{:S(2)}) copy-start(s32[1,1,64]{2,1,0:T(1,128)} %param.11) | copy-start | bytes 772
  16.2 29.3 %collective-permute-start = (f32[64,5,512]{2,0,1:T(8,128)S(1)}, f32[64,5,512]{2,0,1:T(8,128)S(1)}, u32[]{:S(2)}, u32[]{:S(2)}) collective-permute-start(f32[64,5,512]{2,0,1:T(8,128)S(1)} %copy.23), channel_id=1, source_target_pairs={{0,16},{16,32},{32,48},{48,64},{64,80},{80,96},{96,112},{112,128},... | collective-permute-start | bytes 1966088 | tf_op jit(solution)/shard_map/ppermute | solution.py:13
  84.3 18.3 %copy-start.3 = (f32[3,5]{1,0:T(4,128)S(1)}, f32[3,5]{1,0:T(4,128)}, u32[]{:S(2)}) copy-start(f32[3,5]{1,0:T(4,128)} %param.12) | copy-start | bytes 184
  84.4 8.8 %collective-permute-start.1 = (f32[5,2,32,128]{3,2,1,0:T(8,128)S(1)}, f32[5,2,32,128]{3,2,1,0:T(8,128)S(1)}, u32[]{:S(2)}, u32[]{:S(2)}) collective-permute-start(f32[5,2,32,128]{3,2,1,0:T(8,128)S(1)} %get-tuple-element.16), channel_id=1, source_target_pairs={{0,16},{16,32},{32,48},{48,64},{64,80},{80,96},{96,112},{112,128},... | collective-permute-start | bytes 491528 | tf_op jit(solution)/shard_map/ppermute | solution.py:21
  86.3 7.7 %collective-permute-start.2 = (f32[5,2,32,128]{3,2,1,0:T(8,128)S(1)}, f32[5,2,32,128]{3,2,1,0:T(8,128)S(1)}, u32[]{:S(2)}, u32[]{:S(2)}) collective-permute-start(f32[5,2,32,128]{3,2,1,0:T(8,128)S(1)} %get-tuple-element.15), channel_id=1, source_target_pairs={{16,0},{32,16},{48,32},{64,48},{80,64},{96,80},{112,96},{128,112},... | collective-permute-start | bytes 491528 | tf_op jit(solution)/shard_map/ppermute | solution.py:24
  94.1 8.5 %collective-permute-start.3 = (f32[5,12,2,128]{3,2,1,0:T(2,128)S(1)}, f32[5,12,2,128]{3,2,1,0:T(2,128)S(1)}, u32[]{:S(2)}, u32[]{:S(2)}) collective-permute-start(f32[5,12,2,128]{3,2,1,0:T(2,128)S(1)} %get-tuple-element.11), channel_id=1, source_target_pairs={{0,1},{1,2},{2,3},{3,4},{4,5},{5,6},{6,7},{7,8},{8,9},{9,10},{10,1... | collective-permute-start | bytes 184328 | tf_op jit(solution)/shard_map/ppermute | solution.py:21
  100.4 6.8 %collective-permute-start.4 = (f32[5,12,2,128]{3,2,1,0:T(2,128)S(1)}, f32[5,12,2,128]{3,2,1,0:T(2,128)S(1)}, u32[]{:S(2)}, u32[]{:S(2)}) collective-permute-start(f32[5,12,2,128]{3,2,1,0:T(2,128)S(1)} %get-tuple-element.12), channel_id=1, source_target_pairs={{1,0},{2,1},{3,2},{4,3},{5,4},{6,5},{7,6},{8,7},{9,8},{10,9},{11,1... | collective-permute-start | bytes 184328 | tf_op jit(solution)/shard_map/ppermute | solution.py:24
where the time goes:
time: 113 us; the launch traced here: 112 us
  local copies, waits for them, and re-layouts  32.5 us (29%)
  starting transfers between devices  27.7 us (25%)
  waiting for transfers between devices  27.4 us (24%)
  other arithmetic  24.1 us (21%)
    ppermute x1, waiting for transfers between devices, shifted_2(): return lax.ppermute(x, axis, [(i, (i + by) % peers) for i in range(peers)])  20.8 us
    transpose x1, other arithmetic, local(): region = refilled.reshape(BY, BX, fields, E, E, E).transpose(2, 3, 0, 4,...  9.9 us
    transpose x1, local copies, waits for them, and re-layouts, local(): region = refilled.reshape(BY, BX, fields, E, E, E).transpose(2, 3, 0, 4,...  9.38 us
    ppermute x2, starting transfers between devices, with_halo(): lax.ppermute(lax.slice_in_dim(block, block.shape[dim] - width, None, axis...  8.26 us
    reshape x1, local copies, waits for them, and re-layouts, local(): region = refilled.reshape(BY, BX, fields, E, E, E).transpose(2, 3, 0, 4,...  7.85 us
    all_to_all x1, starting transfers between devices, local(): lax.all_to_all(outgoing, 'tile', split_axis=0, concat_axis=0, tiled=True)  7.62 us
    ppermute x2, starting transfers between devices, with_halo(): lax.ppermute(lax.slice_in_dim(block, 0, width, axis=dim), axis, backward)  7.61 us
    ppermute x2, waiting for transfers between devices, with_halo(): lax.ppermute(lax.slice_in_dim(block, 0, width, axis=dim), axis, backward)  5.23 us
  transfers between devices with their start and end apart: 6, of which 4 were waited for; matrix products, arithmetic and copies ran while one was open for 11% of the time, Pallas kernels for 0%

commit v1 on v0

v1 whole, which is shorter than its diff:
```python
import jax
import jax.numpy as jnp
from jax import lax
from jax.experimental import pallas as pl
from jax.experimental.pallas import tpu as pltpu
from jax.sharding import PartitionSpec as P

E = 8
BX = 16
BY = 4
INTERPRET = False


def minmod(left, right):
    return 0.5 * (jnp.sign(left) + jnp.sign(right)) * jnp.minimum(jnp.abs(left), jnp.abs(right))


def slopes(cells, axis):
    width = [(0, 0)] * cells.ndim
    width[axis] = (1, 1)
    padded = jnp.pad(cells, width, mode="edge")
    size = cells.shape[axis]
    below = lax.slice_in_dim(padded, 0, size, axis=axis)
    above = lax.slice_in_dim(padded, 2, size + 2, axis=axis)
    return minmod(cells - below, above - cells)


def refine_block(cells):
    nd = cells.ndim
    slope_z = slopes(cells, nd - 3)
    slope_y = slopes(cells, nd - 2)
    slope_x = slopes(cells, nd - 1)
    sigma = jnp.array([-0.25, 0.25], jnp.float32)

    def spread(value):
        return value[..., :, None, :, None, :, None]

    offset = (
        spread(slope_z) * sigma[:, None, None, None, None]
        + spread(slope_y) * sigma[:, None, None]
        + spread(slope_x) * sigma
    )
    fine = spread(cells) + offset
    half = cells.shape[-1]
    return fine.reshape(cells.shape[:-3] + (2 * half, 2 * half, 2 * half))


def assemble_kernel(arr_ref, int_ref, src_ref, o_ref, at_ref, p_ref):
    rows = at_ref.shape[1]
    lanes = src_ref.shape[1]

    @pl.when(pl.program_id(0) == 0)
    def _():
        row = lax.broadcasted_iota(jnp.int32, (rows, lanes), 0)
        lane = lax.broadcasted_iota(jnp.int32, (rows, lanes), 1)
        hit = row == src_ref[...]
        for x in range(E):
            sel = hit & (lane % E == x)
            p_ref[x * rows:(x + 1) * rows, :] = jnp.where(sel, 1.0, 0.0).astype(jnp.bfloat16)

    a = jnp.concatenate([arr_ref[0], int_ref[0]], axis=0)
    at_ref[...] = a.T
    zy = at_ref.shape[0] // E
    w = jnp.concatenate([at_ref[pl.ds(x, zy, stride=E), :] for x in range(E)], axis=1)
    hi = w.astype(jnp.bfloat16)
    rest = w - hi.astype(jnp.float32)
    mid = rest.astype(jnp.bfloat16)
    lo = (rest - mid.astype(jnp.float32)).astype(jnp.bfloat16)
    pm = p_ref[...]
    out = jnp.dot(hi, pm, preferred_element_type=jnp.float32)
    out = out + jnp.dot(mid, pm, preferred_element_type=jnp.float32)
    out = out + jnp.dot(lo, pm, preferred_element_type=jnp.float32)
    width = o_ref.shape[3]
    for by in range(o_ref.shape[2] // E):
        o_ref[0, :, by * E:(by + 1) * E, :] = out[:, by * width:(by + 1) * width].reshape(E, E, width)


def assemble(arrived, interp, srcrow):
    fields, blocks, cells = arrived.shape
    lanes = srcrow.shape[1]
    return pl.pallas_call(
        assemble_kernel,
        grid=(fields,),
        in_specs=[
            pl.BlockSpec((1, blocks, cells), lambda f: (f, 0, 0)),
            pl.BlockSpec((1, blocks, cells), lambda f: (f, 0, 0)),
            pl.BlockSpec((1, lanes), lambda f: (0, 0)),
        ],
        out_specs=pl.BlockSpec((1, E, BY * E, BX * E), lambda f: (f, 0, 0, 0)),
        out_shape=jax.ShapeDtypeStruct((fields, E, BY * E, BX * E), jnp.float32),
        scratch_shapes=[
            pltpu.VMEM((cells, 2 * blocks), jnp.float32),
            pltpu.VMEM((E * 2 * blocks, lanes), jnp.bfloat16),
        ],
        compiler_params=pltpu.CompilerParams(dimension_semantics=("arbitrary",)),
        interpret=INTERPRET,
    )(arrived, interp, srcrow)


def axis_terms(padded, axis, coef):
    size = padded.shape[axis] - 4

    def cut(d):
        return lax.slice_in_dim(padded, 2 + d, 2 + d + size, axis=axis)

    center = cut(0)
    lower1 = cut(-1)
    lower2 = cut(-2)
    upper1 = cut(1)
    face_hi = center + 0.5 * minmod(center - lower1, upper1 - center)
    face_lo = lower1 + 0.5 * minmod(lower1 - lower2, center - lower1)
    return coef[:, None, None, None] * (face_hi - face_lo)


def halo(block, axis, dim, width):
    count = lax.axis_size(axis)
    forward = [(i, i + 1) for i in range(count - 1)]
    backward = [(target, source) for source, target in forward]
    size = block.shape[dim]
    low = lax.ppermute(lax.slice_in_dim(block, size - width, size, axis=dim), axis, forward)
    high = lax.ppermute(lax.slice_in_dim(block, 0, width, axis=dim), axis, backward)
    return jnp.concatenate([low, block, high], axis=dim)


def local(old_fine, coarse_fine, old_owner, new_refine, parent_map, courant):
    slabs = lax.axis_size("slab")
    tiles = lax.axis_size("tile")
    myself = lax.axis_index("tile")
    blocks, fields, cells = old_fine.shape
    per_peer = blocks // tiles
    half = E // 2

    coarse_prev = lax.ppermute(coarse_fine, "slab", [(i, (i + 1) % slabs) for i in range(slabs)])

    owner = old_owner.reshape(-1)
    slot = jnp.arange(blocks, dtype=jnp.int32)
    same = owner[:, None] == owner[None, :]
    rank = jnp.sum((same & (slot[None, :] < slot[:, None])).astype(jnp.int32), axis=1)
    position = owner * per_peer + rank
    send_idx = jnp.sum(jnp.where(position[None, :] == slot[:, None], slot[None, :], 0), axis=1)
    outgoing = old_fine[send_idx]
    arrived = lax.all_to_all(outgoing, "tile", split_axis=0, concat_axis=0, tiled=True)
    source = (2 * myself - owner) % tiles
    inverse = source * per_peer + rank

    parents = coarse_prev[parent_map.reshape(-1)]
    interp = refine_block(parents.reshape(blocks, fields, half, half, half)).reshape(blocks, fields, cells)

    flags = new_refine.reshape(-1)
    src = jnp.where(flags == 1, blocks + slot, inverse)
    srcrow = jnp.repeat(src, E)[None, :]
    region = assemble(arrived.transpose(1, 0, 2), interp.transpose(1, 0, 2), srcrow)

    zpad = halo(region, "slab", 1, 2)
    ypad = halo(region, "tile", 2, 2)
    xpad = jnp.pad(region, ((0, 0), (0, 0), (0, 0), (2, 2)))
    total = axis_terms(zpad, 1, courant[0])
    total = total + axis_terms(ypad, 2, courant[1])
    total = total + axis_terms(xpad, 3, courant[2])
    return region - total


def solution(mesh):
    in_specs = (
        P(("slab", "tile"), None, None),
        P(("slab", "tile"), None, None),
        P("slab", "tile", None),
        P("slab", "tile", None),
        P("slab", "tile", None),
        P(),
    )
    out_specs = P(None, "slab", "tile", None)
    return jax.shard_map(local, mesh=mesh, in_specs=in_specs, out_specs=out_specs, check_vma=False)
```

time: 113 us -> 84.3 us (0.75)
  the two profiles are of different devices: /device:TPU:31 before, /device:TPU:7 now
where the time goes in v1:
time: 84.3 us; the launch traced here: 83.6 us
  starting transfers between devices  30.7 us (36%)
  waiting for transfers between devices  25.5 us (30%)
  other arithmetic  11 us (13%)
  local copies, waits for them, and re-layouts  10.1 us (12%)
  Pallas kernels  6.19 us (7%)
    all_to_all x1, waiting for transfers between devices, local(): lax.all_to_all(outgoing, 'tile', split_axis=0, concat_axis=0, tiled=True)  19.7 us
    ppermute x2, starting transfers between devices, halo(): lax.ppermute(lax.slice_in_dim(block, 0, width, axis=dim), axis, backward)  12.5 us
    all_to_all x1, starting transfers between devices, local(): lax.all_to_all(outgoing, 'tile', split_axis=0, concat_axis=0, tiled=True)  8.2 us
    sub x1, other arithmetic, local(): return region - total  6.81 us
    pallas_call x1, Pallas kernels, assemble(): pl.pallas_call(assemble_kernel, grid=(fields,), in_specs=[pl.BlockSpec((1...  6.19 us
    ppermute x2, starting transfers between devices, halo(): lax.ppermute(lax.slice_in_dim(block, size - width, size, axis=dim), axis,...  5.92 us
    ppermute x1, starting transfers between devices, local(): lax.ppermute(coarse_fine, 'slab', [(i, (i + 1) % slabs) for i in range(sl...  4 us
    gather x2, local copies, waits for them, and re-layouts, local(): outgoing = old_fine[send_idx]  2.92 us
  transfers between devices with their start and end apart: 6, of which 3 were waited for; matrix products, arithmetic and copies ran while one was open for 12% of the time, Pallas kernels for 0%

profile of v1, /device:TPU:7, one launch (start us, length us, event | category | flops | bytes accessed | tf_op | source)
XLA Modules:
  0.0 83.6 jit_solution(3326491926450309412)
XLA Ops:
  0.0 1.1 %copy.18 = f32[64,5,64]{2,1,0:T(8,128)S(1)} copy(f32[64,5,64]{2,0,1:T(8,128)} %param.8) | data formatting | bytes 163840 | tf_op args[1]
  1.1 4.0 %collective-permute-start = (f32[64,5,64]{2,1,0:T(8,128)S(1)}, f32[64,5,64]{2,1,0:T(8,128)S(1)}, u32[]{:S(2)}, u32[]{:S(2)}) collective-permute-start(f32[64,5,64]{2,1,0:T(8,128)S(1)} %copy.18), channel_id=1, source_target_pairs={{0,16},{16,32},{32,48},{48,64},{64,80},{80,96},{96,112},{112,128},... | collective-permute-start | bytes 245768 | tf_op jit(solution)/shard_map/ppermute | solution.py:133
  5.1 0.9 %convert_reduce_fusion = s32[64]{0:T(128)S(1)} fusion(s32[64]{0:T(128)} %bitcast.33), kind=kLoop, calls=%fused_computation.45 | loop fusion | flops 20416 | bytes 512 | tf_op jit(solution)/shard_map/reduce_sum | solution.py:138
  6.0 0.7 bitcast_select_fusion
  6.7 0.1 select_reduce_fusion
  6.9 1.5 %gather_fusion = f32[64,5,512]{2,0,1:T(8,128)S(1)} fusion(f32[64,5,512]{2,0,1:T(8,128)S(1)} %copy-done, s32[1024]{0:T(1024)S(1)} %pad_clamp_fusion.1), kind=kCustom, calls=%fused_computation | custom fusion | bytes 1310976 | tf_op jit(solution)/shard_map/gather | solution.py:141
  8.4 1.4 %copy.16 = f32[64,5,512]{2,1,0:T(8,128)} copy(f32[64,5,512]{2,0,1:T(8,128)S(1)} %gather_fusion) | data formatting | bytes 1310720 | tf_op jit(solution)/shard_map/gather | solution.py:141
  9.8 8.2 %all-to-all-start = ((f32[64,5,512]{2,1,0:T(8,128)}), f32[64,5,512]{2,1,0:T(8,128)S(1)}, u32[]{:S(2)}, u32[]{:S(2)}) async-start(f32[64,5,512]{2,1,0:T(8,128)} %copy.16), calls=%async_computation | async-start | bytes 2097152 | tf_op jit(solution)/shard_map/all_to_all | solution.py:142
  18.0 0.1 broadcast_in_dim.13
  18.1 0.7 broadcast_in_dim_reshape.2.src_ref
  18.8 2.9 %collective-permute-done = f32[64,5,64]{2,1,0:T(8,128)S(1)} collective-permute-done((f32[64,5,64]{2,1,0:T(8,128)S(1)}, f32[64,5,64]{2,1,0:T(8,128)S(1)}, u32[]{:S(2)}, u32[]{:S(2)}) %collective-permute-start) | collective-permute-done | bytes 81952 | tf_op jit(solution)/shard_map/ppermute | solution.py:133
  21.7 0.6 gather_fusion.1
  22.3 0.1 copy.19
  22.5 0.1 fusion.24
  22.5 0.9 %minimum_multiply_fusion.2 = (f32[64,5,4,4,4]{0,4,3,2,1:T(4,128)S(1)}, f32[64,5,4,4,4]{0,4,3,2,1:T(4,128)S(1)}, f32[64,5,4,4,4]{0,4,3,2,1:T(4,128)S(1)}) fusion(f32[64,5,4,4,4]{0,4,3,2,1:T(4,128)S(1)} %bitcast.29, f32[64,5,1,4,4]{0,4,3,2,1:T(4,128)S(1)} %get-tuple-element.13, f32[64,5,1,4,4]{0,4,3,2,1:T(4,128)S(1)} %get-tuple-element.12, ...), kind=kLoop, calls=%fused_computation.42 | loop fusion | flops 737280 | bytes 450560 | tf_op jit(solution)/shard_map/mul | solution.py:15
  23.5 0.1 broadcast_multiply_fusion.1
  23.6 0.1 broadcast_multiply_fusion.2
  23.8 0.2 broadcast_multiply_fusion
  24.0 0.2 broadcast_add_fusion
  24.2 0.8 add_add_fusion
  25.0 1.3 %copy.20 = f32[64,5,512]{2,0,1:T(8,128)} copy(f32[64,5,512]{0,2,1:T(8,128)S(1)} %bitcast.25) | data formatting | bytes 1310720 | tf_op jit(solution)/shard_map/add | solution.py:43
  26.3 19.7 %all-to-all-done = f32[64,5,512]{2,1,0:T(8,128)S(1)} async-done(((f32[64,5,512]{2,1,0:T(8,128)}), f32[64,5,512]{2,1,0:T(8,128)S(1)}, u32[]{:S(2)}, u32[]{:S(2)}) %all-to-all-start) | async-done | bytes 655392 | tf_op jit(solution)/shard_map/all_to_all | solution.py:142
  46.0 1.2 %copy.22 = f32[64,5,512]{2,0,1:T(8,128)} copy(f32[64,5,512]{2,1,0:T(8,128)S(1)} %all-to-all-done) | data formatting | bytes 1310720 | tf_op jit(solution)/shard_map/all_to_all | solution.py:142
  47.2 6.2 %shard_map.73 = f32[5,8,32,128]{3,2,1,0:T(8,128)} custom-call(f32[5,64,512]{2,1,0:T(8,128)} %bitcast.31, f32[5,64,512]{2,1,0:T(8,128)} %bitcast.32, s32[1,512]{1,0:T(1,128)} %broadcast_in_dim_reshape.2.src_ref), custom_call_target="tpu_custom_call" | custom-call | tf_op jit(solution)/shard_map/pallas_call | solution.py:81
  53.4 1.0 %fusion.20 = (f32[5,2,32,128]{3,2,1,0:T(8,128)S(1)}, f32[5,2,32,128]{3,2,1,0:T(8,128)S(1)}) fusion(f32[5,8,32,128]{3,2,1,0:T(8,128)} %shard_map.73), kind=kLoop, calls=%fused_computation.65 | loop fusion | bytes 655360 | tf_op jit(solution)/shard_map/slice | solution.py:121
  54.4 1.0 %fusion.21 = (f32[5,8,2,128]{3,2,1,0:T(2,128)S(1)}, f32[5,8,2,128]{3,2,1,0:T(2,128)S(1)}) fusion(f32[5,8,32,128]{3,2,1,0:T(8,128)} %shard_map.73), kind=kLoop, calls=%fused_computation.66 | loop fusion | bytes 163840 | tf_op jit(solution)/shard_map/slice | solution.py:121
  55.4 4.0 %collective-permute-start.1 = (f32[5,2,32,128]{3,2,1,0:T(8,128)S(1)}, f32[5,2,32,128]{3,2,1,0:T(8,128)S(1)}, u32[]{:S(2)}, u32[]{:S(2)}) collective-permute-start(f32[5,2,32,128]{3,2,1,0:T(8,128)S(1)} %get-tuple-element.6), channel_id=1, source_target_pairs={{0,16},{16,32},{32,48},{48,64},{64,80},{80,96},{96,112},{112,128},... | collective-permute-start | bytes 491528 | tf_op jit(solution)/shard_map/ppermute | solution.py:120
  59.4 10.1 %collective-permute-start.2 = (f32[5,2,32,128]{3,2,1,0:T(8,128)S(1)}, f32[5,2,32,128]{3,2,1,0:T(8,128)S(1)}, u32[]{:S(2)}, u32[]{:S(2)}) collective-permute-start(f32[5,2,32,128]{3,2,1,0:T(8,128)S(1)} %get-tuple-element.5), channel_id=1, source_target_pairs={{16,0},{32,16},{48,32},{64,48},{80,64},{96,80},{112,96},{128,112},... | collective-permute-start | bytes 491528 | tf_op jit(solution)/shard_map/ppermute | solution.py:121
  69.6 1.9 %collective-permute-start.3 = (f32[5,8,2,128]{3,2,1,0:T(2,128)S(1)}, f32[5,8,2,128]{3,2,1,0:T(2,128)S(1)}, u32[]{:S(2)}, u32[]{:S(2)}) collective-permute-start(f32[5,8,2,128]{3,2,1,0:T(2,128)S(1)} %get-tuple-element.8), channel_id=1, source_target_pairs={{0,1},{1,2},{2,3},{3,4},{4,5},{5,6},{6,7},{7,8},{8,9},{9,10},{10,1... | collective-permute-start | bytes 122888 | tf_op jit(solution)/shard_map/ppermute | solution.py:120
  71.5 2.4 %collective-permute-start.4 = (f32[5,8,2,128]{3,2,1,0:T(2,128)S(1)}, f32[5,8,2,128]{3,2,1,0:T(2,128)S(1)}, u32[]{:S(2)}, u32[]{:S(2)}) collective-permute-start(f32[5,8,2,128]{3,2,1,0:T(2,128)S(1)} %get-tuple-element.7), channel_id=1, source_target_pairs={{1,0},{2,1},{3,2},{4,3},{5,4},{6,5},{7,6},{8,7},{9,8},{10,9},{11,1... | collective-permute-start | bytes 122888 | tf_op jit(solution)/shard_map/ppermute | solution.py:121
  74.0 2.9 %collective-permute-done.4 = f32[5,8,2,128]{3,2,1,0:T(2,128)S(1)} collective-permute-done((f32[5,8,2,128]{3,2,1,0:T(2,128)S(1)}, f32[5,8,2,128]{3,2,1,0:T(2,128)S(1)}, u32[]{:S(2)}, u32[]{:S(2)}) %collective-permute-start.4) | collective-permute-done | bytes 40992 | tf_op jit(solution)/shard_map/ppermute | solution.py:121
  76.8 6.8 %add_subtract_fusion = f32[5,8,32,128]{3,2,1,0:T(8,128)} fusion(f32[5,8,32,128]{3,2,1,0:T(8,128)} %shard_map.73, f32[5,8,2,128]{3,2,1,0:T(2,128)S(1)} %collective-permute-done.3, f32[5,8,2,128]{3,2,1,0:T(2,128)S(1)} %collective-permute-done.4, f32[5,2,32,128]{3,2,1,0:T(8,128)S(1)} %collective-permute-done.1, ...), kind=kLoop, calls=%fused_computation.23 | loop fusion | flops 12779520 | bytes 1720380 | tf_op jit(solution)/shard_map/sub | solution.py:160
  (18 shorter events, 0.1 us)
Async XLA Ops:
  0.0 6.8 %copy-start = (f32[64,5,512]{2,0,1:T(8,128)S(1)}, f32[64,5,512]{2,0,1:T(8,128)}, u32[]{:S(2)}) copy-start(f32[64,5,512]{2,0,1:T(8,128)} %param.7) | copy-start | bytes 1966084
  1.1 20.6 %collective-permute-start = (f32[64,5,64]{2,1,0:T(8,128)S(1)}, f32[64,5,64]{2,1,0:T(8,128)S(1)}, u32[]{:S(2)}, u32[]{:S(2)}) collective-permute-start(f32[64,5,64]{2,1,0:T(8,128)S(1)} %copy.18), channel_id=1, source_target_pairs={{0,16},{16,32},{32,48},{48,64},{64,80},{80,96},{96,112},{112,128},... | collective-permute-start | bytes 245768 | tf_op jit(solution)/shard_map/ppermute | solution.py:133
  9.8 8.2 %copy-start.3 = (s32[1,1,64]{2,1,0:T(1,128)S(1)}, s32[1,1,64]{2,1,0:T(1,128)}, u32[]{:S(2)}) copy-start(s32[1,1,64]{2,1,0:T(1,128)} %param.11) | copy-start | bytes 772
  9.8 36.2 %all-to-all-start = ((f32[64,5,512]{2,1,0:T(8,128)}), f32[64,5,512]{2,1,0:T(8,128)S(1)}, u32[]{:S(2)}, u32[]{:S(2)}) async-start(f32[64,5,512]{2,1,0:T(8,128)} %copy.16), calls=%async_computation | async-start | bytes 2097152 | tf_op jit(solution)/shard_map/all_to_all | solution.py:142
  18.0 5.5 %copy-start.1 = (f32[2]{0:T(128)S(1)}, f32[2]{0:T(128)}, u32[]{:S(2)}) copy-start(f32[2]{0:T(128)} %constant.36.clone) | copy-start | bytes 28
  47.2 26.7 %copy-start.2 = (f32[3,5]{1,0:T(4,128)S(1)}, f32[3,5]{1,0:T(4,128)}, u32[]{:S(2)}) copy-start(f32[3,5]{1,0:T(4,128)} %param.12) | copy-start | bytes 184
  55.4 21.4 %collective-permute-start.1 = (f32[5,2,32,128]{3,2,1,0:T(8,128)S(1)}, f32[5,2,32,128]{3,2,1,0:T(8,128)S(1)}, u32[]{:S(2)}, u32[]{:S(2)}) collective-permute-start(f32[5,2,32,128]{3,2,1,0:T(8,128)S(1)} %get-tuple-element.6), channel_id=1, source_target_pairs={{0,16},{16,32},{32,48},{48,64},{64,80},{80,96},{96,112},{112,128},... | collective-permute-start | bytes 491528 | tf_op jit(solution)/shard_map/ppermute | solution.py:120
  59.4 17.4 %collective-permute-start.2 = (f32[5,2,32,128]{3,2,1,0:T(8,128)S(1)}, f32[5,2,32,128]{3,2,1,0:T(8,128)S(1)}, u32[]{:S(2)}, u32[]{:S(2)}) collective-permute-start(f32[5,2,32,128]{3,2,1,0:T(8,128)S(1)} %get-tuple-element.5), channel_id=1, source_target_pairs={{16,0},{32,16},{48,32},{64,48},{80,64},{96,80},{112,96},{128,112},... | collective-permute-start | bytes 491528 | tf_op jit(solution)/shard_map/ppermute | solution.py:121
  69.6 4.4 %collective-permute-start.3 = (f32[5,8,2,128]{3,2,1,0:T(2,128)S(1)}, f32[5,8,2,128]{3,2,1,0:T(2,128)S(1)}, u32[]{:S(2)}, u32[]{:S(2)}) collective-permute-start(f32[5,8,2,128]{3,2,1,0:T(2,128)S(1)} %get-tuple-element.8), channel_id=1, source_target_pairs={{0,1},{1,2},{2,3},{3,4},{4,5},{5,6},{6,7},{7,8},{8,9},{9,10},{10,1... | collective-permute-start | bytes 122888 | tf_op jit(solution)/shard_map/ppermute | solution.py:120
  71.5 5.3 %collective-permute-start.4 = (f32[5,8,2,128]{3,2,1,0:T(2,128)S(1)}, f32[5,8,2,128]{3,2,1,0:T(2,128)S(1)}, u32[]{:S(2)}, u32[]{:S(2)}) collective-permute-start(f32[5,8,2,128]{3,2,1,0:T(2,128)S(1)} %get-tuple-element.7), channel_id=1, source_target_pairs={{1,0},{2,1},{3,2},{4,3},{5,4},{6,5},{7,6},{8,7},{9,8},{10,9},{11,1... | collective-permute-start | bytes 122888 | tf_op jit(solution)/shard_map/ppermute | solution.py:121

commit v2 on v1

--- a/solution.py
+++ b/solution.py
@@ -138,8 +138,9 @@
     rank = jnp.sum((same & (slot[None, :] < slot[:, None])).astype(jnp.int32), axis=1)
     position = owner * per_peer + rank
     send_idx = jnp.sum(jnp.where(position[None, :] == slot[:, None], slot[None, :], 0), axis=1)
-    outgoing = old_fine[send_idx]
+    outgoing = old_fine[send_idx].reshape(tiles, per_peer * fields * cells // 128, 128)
     arrived = lax.all_to_all(outgoing, "tile", split_axis=0, concat_axis=0, tiled=True)
+    arrived = arrived.reshape(blocks, fields, cells)
     source = (2 * myself - owner) % tiles
     inverse = source * per_peer + rank
 

time: 84.3 us -> 76 us (0.902)
  waiting for transfers between devices: 25.5 us -> 17.4 us
    all_to_all x1, waiting for transfers between devices: 19.7 us -> 11.5 us  [local(): lax.all_to_all(outgoing, 'tile', split_axis=0, concat_axis=0, tiled=True)]
    reshape x0 -> x3, local copies, waits for them, and re-layouts: none -> 2.28 us  [the longest x2 1.32 us: local(): arrived = arrived.reshape(blocks, fields, cells)]
    all_to_all x1 -> x0, local copies, waits for them, and re-layouts: 1.22 us -> none  [local(): lax.all_to_all(outgoing, 'tile', split_axis=0, concat_axis=0, tiled=True)]
    gather x2, local copies, waits for them, and re-layouts: 2.92 us -> 1.95 us  [local(): old_fine[send_idx].reshape(tiles, per_peer * fields * cells // 128, 128)]
  transfers between devices with their start and end apart: 6 -> 6, of which waited for: 3 -> 3; matrix products, arithmetic and copies ran while one was open for 12% -> 13% of each run, Pallas kernels for 0% -> 0%
where the time goes in v2:
time: 76 us; the launch traced here: 75.5 us
  starting transfers between devices  30.5 us (40%)
  waiting for transfers between devices  17.4 us (23%)
  other arithmetic  10.9 us (14%)
  local copies, waits for them, and re-layouts  10.2 us (13%)
  Pallas kernels  6.19 us (8%)
    ppermute x2, starting transfers between devices, halo(): lax.ppermute(lax.slice_in_dim(block, 0, width, axis=dim), axis, backward)  12.5 us
    all_to_all x1, waiting for transfers between devices, local(): lax.all_to_all(outgoing, 'tile', split_axis=0, concat_axis=0, tiled=True)  11.5 us
    all_to_all x1, starting transfers between devices, local(): lax.all_to_all(outgoing, 'tile', split_axis=0, concat_axis=0, tiled=True)  8.07 us
    sub x1, other arithmetic, local(): return region - total  6.75 us
    pallas_call x1, Pallas kernels, assemble(): pl.pallas_call(assemble_kernel, grid=(fields,), in_specs=[pl.BlockSpec((1...  6.19 us
    ppermute x2, starting transfers between devices, halo(): lax.ppermute(lax.slice_in_dim(block, size - width, size, axis=dim), axis,...  5.93 us
    ppermute x1, starting transfers between devices, local(): lax.ppermute(coarse_fine, 'slab', [(i, (i + 1) % slabs) for i in range(sl...  4 us
    ppermute x1, waiting for transfers between devices, local(): lax.ppermute(coarse_fine, 'slab', [(i, (i + 1) % slabs) for i in range(sl...  3.02 us
  transfers between devices with their start and end apart: 6, of which 3 were waited for; matrix products, arithmetic and copies ran while one was open for 13% of the time, Pallas kernels for 0%

profile of v2, /device:TPU:7, one launch (start us, length us, event | category | flops | bytes accessed | tf_op | source)
XLA Modules:
  0.0 75.5 jit_solution(4584801692434139426)
XLA Ops:
  0.0 1.1 %copy.15 = f32[64,5,64]{2,1,0:T(8,128)S(1)} copy(f32[64,5,64]{2,0,1:T(8,128)} %param.8) | data formatting | bytes 163840 | tf_op args[1]
  1.1 4.0 %collective-permute-start = (f32[64,5,64]{2,1,0:T(8,128)S(1)}, f32[64,5,64]{2,1,0:T(8,128)S(1)}, u32[]{:S(2)}, u32[]{:S(2)}) collective-permute-start(f32[64,5,64]{2,1,0:T(8,128)S(1)} %copy.15), channel_id=1, source_target_pairs={{0,16},{16,32},{32,48},{48,64},{64,80},{80,96},{96,112},{112,128},... | collective-permute-start | bytes 245768 | tf_op jit(solution)/shard_map/ppermute | solution.py:133
  5.1 0.9 %convert_reduce_fusion = s32[64]{0:T(128)S(1)} fusion(s32[64]{0:T(128)} %bitcast.33), kind=kLoop, calls=%fused_computation.45 | loop fusion | flops 20416 | bytes 512 | tf_op jit(solution)/shard_map/reduce_sum | solution.py:138
  6.0 0.7 bitcast_select_fusion
  6.7 0.1 select_reduce_fusion
  6.9 1.5 %gather_fusion = f32[64,5,512]{2,0,1:T(8,128)S(1)} fusion(f32[64,5,512]{2,0,1:T(8,128)S(1)} %copy-done, s32[1024]{0:T(1024)S(1)} %pad_clamp_fusion.1), kind=kCustom, calls=%fused_computation | custom fusion | bytes 1310976 | tf_op jit(solution)/shard_map/gather | solution.py:141
  8.4 0.4 copy.13
  8.8 1.0 %reshape.107 = f32[16,80,128]{2,1,0:T(8,128)} reshape(f32[64,5,512]{2,1,0:T(8,128)S(1)} %copy.13) | data formatting | bytes 1310720 | tf_op jit(solution)/shard_map/reshape | solution.py:141
  9.8 8.1 %all-to-all-start = ((f32[16,80,128]{2,1,0:T(8,128)}), f32[16,80,128]{2,1,0:T(8,128)S(1)}, u32[]{:S(2)}, u32[]{:S(2)}) async-start(f32[16,80,128]{2,1,0:T(8,128)} %reshape.107), calls=%async_computation | async-start | bytes 1310720 | tf_op jit(solution)/shard_map/all_to_all | solution.py:142
  18.0 0.7 broadcast_in_dim_reshape.2.src_ref
  18.6 3.0 %collective-permute-done = f32[64,5,64]{2,1,0:T(8,128)S(1)} collective-permute-done((f32[64,5,64]{2,1,0:T(8,128)S(1)}, f32[64,5,64]{2,1,0:T(8,128)S(1)}, u32[]{:S(2)}, u32[]{:S(2)}) %collective-permute-start) | collective-permute-done | bytes 81952 | tf_op jit(solution)/shard_map/ppermute | solution.py:133
  21.7 0.6 gather_fusion.1
  22.3 0.1 copy.16
  22.5 0.9 %minimum_multiply_fusion.2 = (f32[64,5,4,4,4]{0,4,3,2,1:T(4,128)S(1)}, f32[64,5,4,4,4]{0,4,3,2,1:T(4,128)S(1)}, f32[64,5,4,4,4]{0,4,3,2,1:T(4,128)S(1)}) fusion(f32[64,5,4,4,4]{0,4,3,2,1:T(4,128)S(1)} %bitcast.29, f32[64,5,1,4,4]{0,4,3,2,1:T(4,128)S(1)} %get-tuple-element.13, f32[64,5,1,4,4]{0,4,3,2,1:T(4,128)S(1)} %get-tuple-element.12, ...), kind=kLoop, calls=%fused_computation.42 | loop fusion | flops 737280 | bytes 450560 | tf_op jit(solution)/shard_map/mul | solution.py:15
  23.5 0.1 broadcast_multiply_fusion.1
  23.6 0.1 broadcast_multiply_fusion.2
  23.8 0.2 broadcast_multiply_fusion
  24.0 0.2 broadcast_add_fusion
  24.2 0.8 %add_add_fusion = f32[64,5,4,2,4,2,4,2]{0,7,6,5,4,3,2,1:T(2,128)S(1)} fusion(f32[64,5,4,4,4,2]{0,5,4,3,2,1:T(2,128)S(1)} %broadcast_multiply_fusion, f32[64,5,4,2,4,2,4]{0,6,5,4,3,2,1:T(4,128)S(1)} %broadcast_add_fusion, f32[64,5,4,4,4]{0,4,3,2,1:T(4,128)S(1)} %bitcast.30), kind=kLoop, calls=%fused_computation.5 | loop fusion | flops 327680 | bytes 1228800 | tf_op jit(solution)/shard_map/add | solution.py:43
  25.0 1.2 %copy.17 = f32[64,5,512]{2,0,1:T(8,128)} copy(f32[64,5,512]{0,2,1:T(8,128)S(1)} %bitcast.25) | data formatting | bytes 1310720 | tf_op jit(solution)/shard_map/add | solution.py:43
  26.3 11.5 %all-to-all-done = f32[16,80,128]{2,1,0:T(8,128)S(1)} async-done(((f32[16,80,128]{2,1,0:T(8,128)}), f32[16,80,128]{2,1,0:T(8,128)S(1)}, u32[]{:S(2)}, u32[]{:S(2)}) %all-to-all-start) | async-done | bytes 655392 | tf_op jit(solution)/shard_map/all_to_all | solution.py:142
  37.8 0.1 reshape.108
  37.9 1.2 %copy.19 = f32[64,5,512]{2,0,1:T(8,128)} copy(f32[64,5,512]{2,1,0:T(8,128)S(1)} %reshape.108) | data formatting | bytes 1310720 | tf_op jit(solution)/shard_map/reshape | solution.py:143
  39.1 6.2 %shard_map.73 = f32[5,8,32,128]{3,2,1,0:T(8,128)} custom-call(f32[5,64,512]{2,1,0:T(8,128)} %bitcast.31, f32[5,64,512]{2,1,0:T(8,128)} %bitcast.32, s32[1,512]{1,0:T(1,128)} %broadcast_in_dim_reshape.2.src_ref), custom_call_target="tpu_custom_call" | custom-call | tf_op jit(solution)/shard_map/pallas_call | solution.py:81
  45.3 1.0 %fusion.20 = (f32[5,2,32,128]{3,2,1,0:T(8,128)S(1)}, f32[5,2,32,128]{3,2,1,0:T(8,128)S(1)}) fusion(f32[5,8,32,128]{3,2,1,0:T(8,128)} %shard_map.73), kind=kLoop, calls=%fused_computation.65 | loop fusion | bytes 655360 | tf_op jit(solution)/shard_map/slice | solution.py:121
  46.3 1.0 %fusion.21 = (f32[5,8,2,128]{3,2,1,0:T(2,128)S(1)}, f32[5,8,2,128]{3,2,1,0:T(2,128)S(1)}) fusion(f32[5,8,32,128]{3,2,1,0:T(8,128)} %shard_map.73), kind=kLoop, calls=%fused_computation.66 | loop fusion | bytes 163840 | tf_op jit(solution)/shard_map/slice | solution.py:121
  47.4 4.0 %collective-permute-start.1 = (f32[5,2,32,128]{3,2,1,0:T(8,128)S(1)}, f32[5,2,32,128]{3,2,1,0:T(8,128)S(1)}, u32[]{:S(2)}, u32[]{:S(2)}) collective-permute-start(f32[5,2,32,128]{3,2,1,0:T(8,128)S(1)} %get-tuple-element.6), channel_id=1, source_target_pairs={{0,16},{16,32},{32,48},{48,64},{64,80},{80,96},{96,112},{112,128},... | collective-permute-start | bytes 491528 | tf_op jit(solution)/shard_map/ppermute | solution.py:120
  51.4 10.1 %collective-permute-start.2 = (f32[5,2,32,128]{3,2,1,0:T(8,128)S(1)}, f32[5,2,32,128]{3,2,1,0:T(8,128)S(1)}, u32[]{:S(2)}, u32[]{:S(2)}) collective-permute-start(f32[5,2,32,128]{3,2,1,0:T(8,128)S(1)} %get-tuple-element.5), channel_id=1, source_target_pairs={{16,0},{32,16},{48,32},{64,48},{80,64},{96,80},{112,96},{128,112},... | collective-permute-start | bytes 491528 | tf_op jit(solution)/shard_map/ppermute | solution.py:121
  61.5 1.9 %collective-permute-start.3 = (f32[5,8,2,128]{3,2,1,0:T(2,128)S(1)}, f32[5,8,2,128]{3,2,1,0:T(2,128)S(1)}, u32[]{:S(2)}, u32[]{:S(2)}) collective-permute-start(f32[5,8,2,128]{3,2,1,0:T(2,128)S(1)} %get-tuple-element.8), channel_id=1, source_target_pairs={{0,1},{1,2},{2,3},{3,4},{4,5},{5,6},{6,7},{7,8},{8,9},{9,10},{10,1... | collective-permute-start | bytes 122888 | tf_op jit(solution)/shard_map/ppermute | solution.py:120
  63.4 2.4 %collective-permute-start.4 = (f32[5,8,2,128]{3,2,1,0:T(2,128)S(1)}, f32[5,8,2,128]{3,2,1,0:T(2,128)S(1)}, u32[]{:S(2)}, u32[]{:S(2)}) collective-permute-start(f32[5,8,2,128]{3,2,1,0:T(2,128)S(1)} %get-tuple-element.7), channel_id=1, source_target_pairs={{1,0},{2,1},{3,2},{4,3},{5,4},{6,5},{7,6},{8,7},{9,8},{10,9},{11,1... | collective-permute-start | bytes 122888 | tf_op jit(solution)/shard_map/ppermute | solution.py:121
  65.9 2.9 %collective-permute-done.4 = f32[5,8,2,128]{3,2,1,0:T(2,128)S(1)} collective-permute-done((f32[5,8,2,128]{3,2,1,0:T(2,128)S(1)}, f32[5,8,2,128]{3,2,1,0:T(2,128)S(1)}, u32[]{:S(2)}, u32[]{:S(2)}) %collective-permute-start.4) | collective-permute-done | bytes 40992 | tf_op jit(solution)/shard_map/ppermute | solution.py:121
  68.8 6.8 %add_subtract_fusion = f32[5,8,32,128]{3,2,1,0:T(8,128)} fusion(f32[5,8,32,128]{3,2,1,0:T(8,128)} %shard_map.73, f32[5,8,2,128]{3,2,1,0:T(2,128)S(1)} %collective-permute-done.3, f32[5,8,2,128]{3,2,1,0:T(2,128)S(1)} %collective-permute-done.4, f32[5,2,32,128]{3,2,1,0:T(8,128)S(1)} %collective-permute-done.1, ...), kind=kLoop, calls=%fused_computation.23 | loop fusion | flops 12779520 | bytes 1720380 | tf_op jit(solution)/shard_map/sub | solution.py:161
  (20 shorter events, 0.2 us)
Async XLA Ops:
  0.0 6.8 %copy-start = (f32[64,5,512]{2,0,1:T(8,128)S(1)}, f32[64,5,512]{2,0,1:T(8,128)}, u32[]{:S(2)}) copy-start(f32[64,5,512]{2,0,1:T(8,128)} %param.7) | copy-start | bytes 1966084
  1.1 20.6 %collective-permute-start = (f32[64,5,64]{2,1,0:T(8,128)S(1)}, f32[64,5,64]{2,1,0:T(8,128)S(1)}, u32[]{:S(2)}, u32[]{:S(2)}) collective-permute-start(f32[64,5,64]{2,1,0:T(8,128)S(1)} %copy.15), channel_id=1, source_target_pairs={{0,16},{16,32},{32,48},{48,64},{64,80},{80,96},{96,112},{112,128},... | collective-permute-start | bytes 245768 | tf_op jit(solution)/shard_map/ppermute | solution.py:133
  8.8 9.0 %copy-start.3 = (s32[1,1,64]{2,1,0:T(1,128)S(1)}, s32[1,1,64]{2,1,0:T(1,128)}, u32[]{:S(2)}) copy-start(s32[1,1,64]{2,1,0:T(1,128)} %param.11) | copy-start | bytes 772
  9.8 28.0 %all-to-all-start = ((f32[16,80,128]{2,1,0:T(8,128)}), f32[16,80,128]{2,1,0:T(8,128)S(1)}, u32[]{:S(2)}, u32[]{:S(2)}) async-start(f32[16,80,128]{2,1,0:T(8,128)} %reshape.107), calls=%async_computation | async-start | bytes 1310720 | tf_op jit(solution)/shard_map/all_to_all | solution.py:142
  17.9 5.6 %copy-start.1 = (f32[2]{0:T(128)S(1)}, f32[2]{0:T(128)}, u32[]{:S(2)}) copy-start(f32[2]{0:T(128)} %constant.36.clone) | copy-start | bytes 28
  39.1 26.7 %copy-start.2 = (f32[3,5]{1,0:T(4,128)S(1)}, f32[3,5]{1,0:T(4,128)}, u32[]{:S(2)}) copy-start(f32[3,5]{1,0:T(4,128)} %param.12) | copy-start | bytes 184
  47.4 21.4 %collective-permute-start.1 = (f32[5,2,32,128]{3,2,1,0:T(8,128)S(1)}, f32[5,2,32,128]{3,2,1,0:T(8,128)S(1)}, u32[]{:S(2)}, u32[]{:S(2)}) collective-permute-start(f32[5,2,32,128]{3,2,1,0:T(8,128)S(1)} %get-tuple-element.6), channel_id=1, source_target_pairs={{0,16},{16,32},{32,48},{48,64},{64,80},{80,96},{96,112},{112,128},... | collective-permute-start | bytes 491528 | tf_op jit(solution)/shard_map/ppermute | solution.py:120
  51.4 17.4 %collective-permute-start.2 = (f32[5,2,32,128]{3,2,1,0:T(8,128)S(1)}, f32[5,2,32,128]{3,2,1,0:T(8,128)S(1)}, u32[]{:S(2)}, u32[]{:S(2)}) collective-permute-start(f32[5,2,32,128]{3,2,1,0:T(8,128)S(1)} %get-tuple-element.5), channel_id=1, source_target_pairs={{16,0},{32,16},{48,32},{64,48},{80,64},{96,80},{112,96},{128,112},... | collective-permute-start | bytes 491528 | tf_op jit(solution)/shard_map/ppermute | solution.py:121
  61.5 4.4 %collective-permute-start.3 = (f32[5,8,2,128]{3,2,1,0:T(2,128)S(1)}, f32[5,8,2,128]{3,2,1,0:T(2,128)S(1)}, u32[]{:S(2)}, u32[]{:S(2)}) collective-permute-start(f32[5,8,2,128]{3,2,1,0:T(2,128)S(1)} %get-tuple-element.8), channel_id=1, source_target_pairs={{0,1},{1,2},{2,3},{3,4},{4,5},{5,6},{6,7},{7,8},{8,9},{9,10},{10,1... | collective-permute-start | bytes 122888 | tf_op jit(solution)/shard_map/ppermute | solution.py:120
  63.4 5.3 %collective-permute-start.4 = (f32[5,8,2,128]{3,2,1,0:T(2,128)S(1)}, f32[5,8,2,128]{3,2,1,0:T(2,128)S(1)}, u32[]{:S(2)}, u32[]{:S(2)}) collective-permute-start(f32[5,8,2,128]{3,2,1,0:T(2,128)S(1)} %get-tuple-element.7), channel_id=1, source_target_pairs={{1,0},{2,1},{3,2},{4,3},{5,4},{6,5},{7,6},{8,7},{9,8},{10,9},{11,1... | collective-permute-start | bytes 122888 | tf_op jit(solution)/shard_map/ppermute | solution.py:121

commit v3 on v2

--- a/solution.py
+++ b/solution.py
@@ -45,7 +45,7 @@
     return fine.reshape(cells.shape[:-3] + (2 * half, 2 * half, 2 * half))
 
 
-def assemble_kernel(arr_ref, int_ref, src_ref, o_ref, at_ref, p_ref):
+def assemble_kernel(arr_ref, int_ref, src_ref, o_ref, zt_ref, zb_ref, yt_ref, yb_ref, at_ref, p_ref):
     rows = at_ref.shape[1]
     lanes = src_ref.shape[1]
 
@@ -71,8 +71,16 @@
     out = out + jnp.dot(mid, pm, preferred_element_type=jnp.float32)
     out = out + jnp.dot(lo, pm, preferred_element_type=jnp.float32)
     width = o_ref.shape[3]
-    for by in range(o_ref.shape[2] // E):
-        o_ref[0, :, by * E:(by + 1) * E, :] = out[:, by * width:(by + 1) * width].reshape(E, E, width)
+    count = o_ref.shape[2] // E
+    for by in range(count):
+        piece = out[:, by * width:(by + 1) * width].reshape(E, E, width)
+        o_ref[0, :, by * E:(by + 1) * E, :] = piece
+        zt_ref[0, :, by * E:(by + 1) * E, :] = piece[E - 2:]
+        zb_ref[0, :, by * E:(by + 1) * E, :] = piece[:2]
+        if by == 0:
+            yb_ref[0] = piece[:, :2, :]
+        if by == count - 1:
+            yt_ref[0] = piece[:, E - 2:, :]
 
 
 def assemble(arrived, interp, srcrow):
@@ -86,8 +94,20 @@
             pl.BlockSpec((1, blocks, cells), lambda f: (f, 0, 0)),
             pl.BlockSpec((1, lanes), lambda f: (0, 0)),
         ],
-        out_specs=pl.BlockSpec((1, E, BY * E, BX * E), lambda f: (f, 0, 0, 0)),
-        out_shape=jax.ShapeDtypeStruct((fields, E, BY * E, BX * E), jnp.float32),
+        out_specs=[
+            pl.BlockSpec((1, E, BY * E, BX * E), lambda f: (f, 0, 0, 0)),
+            pl.BlockSpec((1, 2, BY * E, BX * E), lambda f: (f, 0, 0, 0)),
+            pl.BlockSpec((1, 2, BY * E, BX * E), lambda f: (f, 0, 0, 0)),
+            pl.BlockSpec((1, E, 2, BX * E), lambda f: (f, 0, 0, 0)),
+            pl.BlockSpec((1, E, 2, BX * E), lambda f: (f, 0, 0, 0)),
+        ],
+        out_shape=[
+            jax.ShapeDtypeStruct((fields, E, BY * E, BX * E), jnp.float32),
+            jax.ShapeDtypeStruct((fields, 2, BY * E, BX * E), jnp.float32),
+            jax.ShapeDtypeStruct((fields, 2, BY * E, BX * E), jnp.float32),
+            jax.ShapeDtypeStruct((fields, E, 2, BX * E), jnp.float32),
+            jax.ShapeDtypeStruct((fields, E, 2, BX * E), jnp.float32),
+        ],
         scratch_shapes=[
             pltpu.VMEM((cells, 2 * blocks), jnp.float32),
             pltpu.VMEM((E * 2 * blocks, lanes), jnp.bfloat16),
@@ -95,6 +115,59 @@
         compiler_params=pltpu.CompilerParams(dimension_semantics=("arbitrary",)),
         interpret=INTERPRET,
     )(arrived, interp, srcrow)
+
+
+def kernel_minmod(left, right):
+    def sgn(v):
+        return jnp.where(v > 0, 1.0, 0.0) - jnp.where(v < 0, 1.0, 0.0)
+
+    return 0.5 * (sgn(left) + sgn(right)) * jnp.minimum(jnp.abs(left), jnp.abs(right))
+
+
+def kernel_term(center, lower1, lower2, upper1, coef):
+    face_hi = center + 0.5 * kernel_minmod(center - lower1, upper1 - center)
+    face_lo = lower1 + 0.5 * kernel_minmod(lower1 - lower2, center - lower1)
+    return coef * (face_hi - face_lo)
+
+
+def advance_kernel(c_ref, u_ref, zl_ref, zh_ref, yl_ref, yh_ref, o_ref, yp_ref):
+    f = pl.program_id(0)
+    u = u_ref[0]
+    zn, yn, xn = u.shape
+    zp = jnp.concatenate([zl_ref[0], u, zh_ref[0]], axis=0)
+    tz = kernel_term(u, zp[1:zn + 1], zp[0:zn], zp[3:zn + 3], c_ref[0, f])
+    yp_ref[:, E - 2:E, :] = yl_ref[0]
+    yp_ref[:, E:E + yn, :] = u
+    yp_ref[:, E + yn:E + yn + 2, :] = yh_ref[0]
+    ty = kernel_term(u, yp_ref[:, E - 1:E - 1 + yn, :], yp_ref[:, E - 2:E - 2 + yn, :],
+                     yp_ref[:, E + 1:E + 1 + yn, :], c_ref[1, f])
+    lane = lax.broadcasted_iota(jnp.int32, u.shape, 2)
+    lower1 = jnp.where(lane >= 1, pltpu.roll(u, 1, 2), 0.0)
+    lower2 = jnp.where(lane >= 2, pltpu.roll(u, 2, 2), 0.0)
+    upper1 = jnp.where(lane < xn - 1, pltpu.roll(u, xn - 1, 2), 0.0)
+    tx = kernel_term(u, lower1, lower2, upper1, c_ref[2, f])
+    o_ref[0] = u - ((tz + ty) + tx)
+
+
+def advance(courant, region, zlo, zhi, ylo, yhi):
+    fields, zn, yn, xn = region.shape
+    return pl.pallas_call(
+        advance_kernel,
+        grid=(fields,),
+        in_specs=[
+            pl.BlockSpec(memory_space=pltpu.SMEM),
+            pl.BlockSpec((1, zn, yn, xn), lambda f: (f, 0, 0, 0)),
+            pl.BlockSpec((1, 2, yn, xn), lambda f: (f, 0, 0, 0)),
+            pl.BlockSpec((1, 2, yn, xn), lambda f: (f, 0, 0, 0)),
+            pl.BlockSpec((1, zn, 2, xn), lambda f: (f, 0, 0, 0)),
+            pl.BlockSpec((1, zn, 2, xn), lambda f: (f, 0, 0, 0)),
+        ],
+        out_specs=pl.BlockSpec((1, zn, yn, xn), lambda f: (f, 0, 0, 0)),
+        out_shape=jax.ShapeDtypeStruct(region.shape, jnp.float32),
+        scratch_shapes=[pltpu.VMEM((zn, yn + 2 * E, xn), jnp.float32)],
+        compiler_params=pltpu.CompilerParams(dimension_semantics=("arbitrary",)),
+        interpret=INTERPRET,
+    )(courant, region, zlo, zhi, ylo, yhi)
 
 
 def axis_terms(padded, axis, coef):
@@ -120,6 +193,13 @@
     low = lax.ppermute(lax.slice_in_dim(block, size - width, size, axis=dim), axis, forward)
     high = lax.ppermute(lax.slice_in_dim(block, 0, width, axis=dim), axis, backward)
     return jnp.concatenate([low, block, high], axis=dim)
+
+
+def exchange(top, bottom, axis):
+    count = lax.axis_size(axis)
+    forward = [(i, i + 1) for i in range(count - 1)]
+    backward = [(target, source) for source, target in forward]
+    return lax.ppermute(top, axis, forward), lax.ppermute(bottom, axis, backward)
 
 
 def local(old_fine, coarse_fine, old_owner, new_refine, parent_map, courant):
@@ -150,15 +230,11 @@
     flags = new_refine.reshape(-1)
     src = jnp.where(flags == 1, blocks + slot, inverse)
     srcrow = jnp.repeat(src, E)[None, :]
-    region = assemble(arrived.transpose(1, 0, 2), interp.transpose(1, 0, 2), srcrow)
-
-    zpad = halo(region, "slab", 1, 2)
-    ypad = halo(region, "tile", 2, 2)
-    xpad = jnp.pad(region, ((0, 0), (0, 0), (0, 0), (2, 2)))
-    total = axis_terms(zpad, 1, courant[0])
-    total = total + axis_terms(ypad, 2, courant[1])
-    total = total + axis_terms(xpad, 3, courant[2])
-    return region - total
+    region, ztop, zbot, ytop, ybot = assemble(arrived.transpose(1, 0, 2), interp.transpose(1, 0, 2), srcrow)
+
+    zlo, zhi = exchange(ztop, zbot, "slab")
+    ylo, yhi = exchange(ytop, ybot, "tile")
+    return advance(courant, region, zlo, zhi, ylo, yhi)
 
 
 def solution(mesh):

time: 76 us -> 73.4 us (0.966)
  other arithmetic: 10.9 us -> 4.17 us
  Pallas kernels: 6.19 us -> 11.4 us
  local copies, waits for them, and re-layouts: 10.2 us -> 8.86 us
    sub x1 -> x0, other arithmetic: 6.75 us -> none  [local(): return region - total]
    pallas_call x0 -> x1, Pallas kernels: none -> 5.09 us  [advance(): pl.pallas_call(advance_kernel, grid=(fields,), in_specs=[pl.BlockSpec(mem...]
    slice x2 -> x0, local copies, waits for them, and re-layouts: 2.05 us -> none  [halo(): lax.slice_in_dim(block, 0, width, axis=dim)]
    unnamed x9 -> x15, local copies, waits for them, and re-layouts: 1.11 us -> 1.8 us
  transfers between devices with their start and end apart: 6 -> 6, of which waited for: 3 -> 3; matrix products, arithmetic and copies ran while one was open for 13% -> 14% of each run, Pallas kernels for 0% -> 0%
where the time goes in v3:
time: 73.4 us; the launch traced here: 72.9 us
  starting transfers between devices  30.5 us (42%)
  waiting for transfers between devices  17.6 us (24%)
  Pallas kernels  11.4 us (16%)
  local copies, waits for them, and re-layouts  8.86 us (12%)
  other arithmetic  4.17 us (6%)
    ppermute x2, starting transfers between devices, exchange(): lax.ppermute(bottom, axis, backward)  12.5 us
    all_to_all x1, waiting for transfers between devices, local(): lax.all_to_all(outgoing, 'tile', split_axis=0, concat_axis=0, tiled=True)  11.5 us
    all_to_all x1, starting transfers between devices, local(): lax.all_to_all(outgoing, 'tile', split_axis=0, concat_axis=0, tiled=True)  8.07 us
    pallas_call x1, Pallas kernels, assemble(): pl.pallas_call(assemble_kernel, grid=(fields,), in_specs=[pl.BlockSpec((1...  6.31 us
    ppermute x2, starting transfers between devices, exchange(): lax.ppermute(top, axis, forward)  5.92 us
    pallas_call x1, Pallas kernels, advance(): pl.pallas_call(advance_kernel, grid=(fields,), in_specs=[pl.BlockSpec(mem...  5.09 us
    ppermute x1, starting transfers between devices, local(): lax.ppermute(coarse_fine, 'slab', [(i, (i + 1) % slabs) for i in range(sl...  4 us
    ppermute x2, waiting for transfers between devices, exchange(): lax.ppermute(bottom, axis, backward)  3.1 us
  transfers between devices with their start and end apart: 6, of which 3 were waited for; matrix products, arithmetic and copies ran while one was open for 14% of the time, Pallas kernels for 0%

profile of v3, /device:TPU:7, one launch (start us, length us, event | category | flops | bytes accessed | tf_op | source)
XLA Modules:
  0.0 72.9 jit_solution(10228084115741691938)
XLA Ops:
  0.0 1.1 %copy.15 = f32[64,5,64]{2,1,0:T(8,128)S(1)} copy(f32[64,5,64]{2,0,1:T(8,128)} %param.8) | data formatting | bytes 163840 | tf_op args[1]
  1.1 4.0 %collective-permute-start = (f32[64,5,64]{2,1,0:T(8,128)S(1)}, f32[64,5,64]{2,1,0:T(8,128)S(1)}, u32[]{:S(2)}, u32[]{:S(2)}) collective-permute-start(f32[64,5,64]{2,1,0:T(8,128)S(1)} %copy.15), channel_id=1, source_target_pairs={{0,16},{16,32},{32,48},{48,64},{64,80},{80,96},{96,112},{112,128},... | collective-permute-start | bytes 245768 | tf_op jit(solution)/shard_map/ppermute | solution.py:213
  5.1 0.9 %convert_reduce_fusion = s32[64]{0:T(128)S(1)} fusion(s32[64]{0:T(128)} %bitcast.27), kind=kLoop, calls=%fused_computation.25 | loop fusion | flops 20416 | bytes 512 | tf_op jit(solution)/shard_map/reduce_sum | solution.py:218
  6.0 0.7 bitcast_select_fusion
  6.7 0.1 select_reduce_fusion
  6.9 1.5 %gather_fusion = f32[64,5,512]{2,0,1:T(8,128)S(1)} fusion(f32[64,5,512]{2,0,1:T(8,128)S(1)} %copy-done, s32[1024]{0:T(1024)S(1)} %pad_clamp_fusion.1), kind=kCustom, calls=%fused_computation | custom fusion | bytes 1310976 | tf_op jit(solution)/shard_map/gather | solution.py:221
  8.4 0.4 copy.13
  8.8 1.0 %reshape.104 = f32[16,80,128]{2,1,0:T(8,128)} reshape(f32[64,5,512]{2,1,0:T(8,128)S(1)} %copy.13) | data formatting | bytes 1310720 | tf_op jit(solution)/shard_map/reshape | solution.py:221
  9.8 8.1 %all-to-all-start = ((f32[16,80,128]{2,1,0:T(8,128)}), f32[16,80,128]{2,1,0:T(8,128)S(1)}, u32[]{:S(2)}, u32[]{:S(2)}) async-start(f32[16,80,128]{2,1,0:T(8,128)} %reshape.104), calls=%async_computation | async-start | bytes 1310720 | tf_op jit(solution)/shard_map/all_to_all | solution.py:222
  17.9 0.1 broadcast_in_dim.13
  18.0 0.7 broadcast_in_dim_reshape.2.src_ref
  18.6 3.0 %collective-permute-done = f32[64,5,64]{2,1,0:T(8,128)S(1)} collective-permute-done((f32[64,5,64]{2,1,0:T(8,128)S(1)}, f32[64,5,64]{2,1,0:T(8,128)S(1)}, u32[]{:S(2)}, u32[]{:S(2)}) %collective-permute-start) | collective-permute-done | bytes 81952 | tf_op jit(solution)/shard_map/ppermute | solution.py:213
  21.7 0.6 gather_fusion.1
  22.3 0.1 copy.16
  22.5 0.9 %minimum_multiply_fusion.2 = (f32[64,5,4,4,4]{0,4,3,2,1:T(4,128)S(1)}, f32[64,5,4,4,4]{0,4,3,2,1:T(4,128)S(1)}, f32[64,5,4,4,4]{0,4,3,2,1:T(4,128)S(1)}) fusion(f32[64,5,4,4,4]{0,4,3,2,1:T(4,128)S(1)} %bitcast.23, f32[64,5,1,4,4]{0,4,3,2,1:T(4,128)S(1)} %get-tuple-element.19, f32[64,5,1,4,4]{0,4,3,2,1:T(4,128)S(1)} %get-tuple-element.18, ...), kind=kLoop, calls=%fused_computation.22 | loop fusion | flops 737280 | bytes 450560 | tf_op jit(solution)/shard_map/mul | solution.py:15
  23.5 0.1 broadcast_multiply_fusion.1
  23.6 0.1 broadcast_multiply_fusion.2
  23.8 0.2 broadcast_multiply_fusion
  24.0 0.2 broadcast_add_fusion
  24.2 0.8 %add_add_fusion = f32[64,5,4,2,4,2,4,2]{0,7,6,5,4,3,2,1:T(2,128)S(1)} fusion(f32[64,5,4,4,4,2]{0,5,4,3,2,1:T(2,128)S(1)} %broadcast_multiply_fusion, f32[64,5,4,2,4,2,4]{0,6,5,4,3,2,1:T(4,128)S(1)} %broadcast_add_fusion, f32[64,5,4,4,4]{0,4,3,2,1:T(4,128)S(1)} %bitcast.24), kind=kLoop, calls=%fused_computation.2 | loop fusion | flops 327680 | bytes 1228800 | tf_op jit(solution)/shard_map/add | solution.py:43
  25.0 1.2 %copy.17 = f32[64,5,512]{2,0,1:T(8,128)} copy(f32[64,5,512]{0,2,1:T(8,128)S(1)} %bitcast.19) | data formatting | bytes 1310720 | tf_op jit(solution)/shard_map/add | solution.py:43
  26.3 11.5 %all-to-all-done = f32[16,80,128]{2,1,0:T(8,128)S(1)} async-done(((f32[16,80,128]{2,1,0:T(8,128)}), f32[16,80,128]{2,1,0:T(8,128)S(1)}, u32[]{:S(2)}, u32[]{:S(2)}) %all-to-all-start) | async-done | bytes 655392 | tf_op jit(solution)/shard_map/all_to_all | solution.py:222
  37.8 0.1 reshape.105
  37.9 1.2 %copy.19 = f32[64,5,512]{2,0,1:T(8,128)} copy(f32[64,5,512]{2,1,0:T(8,128)S(1)} %reshape.105) | data formatting | bytes 1310720 | tf_op jit(solution)/shard_map/reshape | solution.py:223
  39.1 6.3 %shard_map.73 = (f32[5,8,32,128]{3,2,1,0:T(8,128)}, f32[5,2,32,128]{3,2,1,0:T(8,128)}, f32[5,2,32,128]{3,2,1,0:T(8,128)}, f32[5,8,2,128]{3,2,1,0:T(2,128)}, f32[5,8,2,128]{3,2,1,0:T(2,128)}) custom-call(f32[5,64,512]{2,1,0:T(8,128)} %bitcast.25, f32[5,64,512]{2,1,0:T(8,128)} %bitcast.26, s32[1,512]{1,0:T(1,128)} %broadcast_in_dim_reshape.2.src_ref), custom_call_target="tpu_custom_call" | custom-call | tf_op jit(solution)/shard_map/pallas_call | solution.py:89
  45.4 4.0 %collective-permute-start.1 = (f32[5,2,32,128]{3,2,1,0:T(8,128)}, f32[5,2,32,128]{3,2,1,0:T(8,128)S(1)}, u32[]{:S(2)}, u32[]{:S(2)}) collective-permute-start(f32[5,2,32,128]{3,2,1,0:T(8,128)} %get-tuple-element.11), channel_id=1, source_target_pairs={{0,16},{16,32},{32,48},{48,64},{64,80},{80,96},{96,112},{112,128},... | collective-permute-start | bytes 491528 | tf_op jit(solution)/shard_map/ppermute | solution.py:202
  49.4 10.1 %collective-permute-start.2 = (f32[5,2,32,128]{3,2,1,0:T(8,128)}, f32[5,2,32,128]{3,2,1,0:T(8,128)S(1)}, u32[]{:S(2)}, u32[]{:S(2)}) collective-permute-start(f32[5,2,32,128]{3,2,1,0:T(8,128)} %get-tuple-element.12), channel_id=1, source_target_pairs={{16,0},{32,16},{48,32},{64,48},{80,64},{96,80},{112,96},{128,112},... | collective-permute-start | bytes 491528 | tf_op jit(solution)/shard_map/ppermute | solution.py:202
  59.6 1.9 %collective-permute-start.3 = (f32[5,8,2,128]{3,2,1,0:T(2,128)}, f32[5,8,2,128]{3,2,1,0:T(2,128)S(1)}, u32[]{:S(2)}, u32[]{:S(2)}) collective-permute-start(f32[5,8,2,128]{3,2,1,0:T(2,128)} %get-tuple-element.13), channel_id=1, source_target_pairs={{0,1},{1,2},{2,3},{3,4},{4,5},{5,6},{6,7},{7,8},{8,9},{9,10},{10,1... | collective-permute-start | bytes 122888 | tf_op jit(solution)/shard_map/ppermute | solution.py:202
  61.5 2.4 %collective-permute-start.4 = (f32[5,8,2,128]{3,2,1,0:T(2,128)}, f32[5,8,2,128]{3,2,1,0:T(2,128)S(1)}, u32[]{:S(2)}, u32[]{:S(2)}) collective-permute-start(f32[5,8,2,128]{3,2,1,0:T(2,128)} %get-tuple-element.14), channel_id=1, source_target_pairs={{1,0},{2,1},{3,2},{4,3},{5,4},{6,5},{7,6},{8,7},{9,8},{10,9},{11,1... | collective-permute-start | bytes 122888 | tf_op jit(solution)/shard_map/ppermute | solution.py:202
  63.9 3.1 %collective-permute-done.4.yh_ref = f32[5,8,2,128]{3,2,1,0:T(2,128)S(1)} collective-permute-done((f32[5,8,2,128]{3,2,1,0:T(2,128)}, f32[5,8,2,128]{3,2,1,0:T(2,128)S(1)}, u32[]{:S(2)}, u32[]{:S(2)}) %collective-permute-start.4) | collective-permute-done | bytes 40992 | tf_op jit(solution)/shard_map/ppermute | solution.py:202
  67.1 0.6 copy-done.4
  67.8 5.1 %shard_map.74 = f32[5,8,32,128]{3,2,1,0:T(8,128)} custom-call(f32[3,5]{1,0:T(4,128)} %c_ref.1, f32[5,8,32,128]{3,2,1,0:T(8,128)} %get-tuple-element.10.u_ref, f32[5,2,32,128]{3,2,1,0:T(8,128)} %copy-done.1, f32[5,2,32,128]{3,2,1,0:T(8,128)} %copy-done.2, f32[5,8,2,128]{3,2,1,0:T(2,128)} %copy-done.3, f32[5,8,2,128]{3,2,1,0:T(2,128)} %copy-done.4), custom_call_target="tpu_custom_call" | custom-call | tf_op jit(solution)/shard_map/pallas_call | solution.py:154
  (23 shorter events, 0.2 us)
Async XLA Ops:
  0.0 6.8 %copy-start = (f32[64,5,512]{2,0,1:T(8,128)S(1)}, f32[64,5,512]{2,0,1:T(8,128)}, u32[]{:S(2)}) copy-start(f32[64,5,512]{2,0,1:T(8,128)} %param.7) | copy-start | bytes 1966084
  1.1 20.6 %collective-permute-start = (f32[64,5,64]{2,1,0:T(8,128)S(1)}, f32[64,5,64]{2,1,0:T(8,128)S(1)}, u32[]{:S(2)}, u32[]{:S(2)}) collective-permute-start(f32[64,5,64]{2,1,0:T(8,128)S(1)} %copy.15), channel_id=1, source_target_pairs={{0,16},{16,32},{32,48},{48,64},{64,80},{80,96},{96,112},{112,128},... | collective-permute-start | bytes 245768 | tf_op jit(solution)/shard_map/ppermute | solution.py:213
  8.8 9.0 %copy-start.6 = (s32[1,1,64]{2,1,0:T(1,128)S(1)}, s32[1,1,64]{2,1,0:T(1,128)}, u32[]{:S(2)}) copy-start(s32[1,1,64]{2,1,0:T(1,128)} %param.11) | copy-start | bytes 772
  9.8 28.0 %all-to-all-start = ((f32[16,80,128]{2,1,0:T(8,128)}), f32[16,80,128]{2,1,0:T(8,128)S(1)}, u32[]{:S(2)}, u32[]{:S(2)}) async-start(f32[16,80,128]{2,1,0:T(8,128)} %reshape.104), calls=%async_computation | async-start | bytes 1310720 | tf_op jit(solution)/shard_map/all_to_all | solution.py:222
  17.9 5.6 %copy-start.5 = (f32[2]{0:T(128)S(1)}, f32[2]{0:T(128)}, u32[]{:S(2)}) copy-start(f32[2]{0:T(128)} %constant.33.clone) | copy-start | bytes 28
  45.4 21.6 %collective-permute-start.1 = (f32[5,2,32,128]{3,2,1,0:T(8,128)}, f32[5,2,32,128]{3,2,1,0:T(8,128)S(1)}, u32[]{:S(2)}, u32[]{:S(2)}) collective-permute-start(f32[5,2,32,128]{3,2,1,0:T(8,128)} %get-tuple-element.11), channel_id=1, source_target_pairs={{0,16},{16,32},{32,48},{48,64},{64,80},{80,96},{96,112},{112,128},... | collective-permute-start | bytes 491528 | tf_op jit(solution)/shard_map/ppermute | solution.py:202
  49.4 17.6 %collective-permute-start.2 = (f32[5,2,32,128]{3,2,1,0:T(8,128)}, f32[5,2,32,128]{3,2,1,0:T(8,128)S(1)}, u32[]{:S(2)}, u32[]{:S(2)}) collective-permute-start(f32[5,2,32,128]{3,2,1,0:T(8,128)} %get-tuple-element.12), channel_id=1, source_target_pairs={{16,0},{32,16},{48,32},{64,48},{80,64},{96,80},{112,96},{128,112},... | collective-permute-start | bytes 491528 | tf_op jit(solution)/shard_map/ppermute | solution.py:202
  59.6 4.3 %collective-permute-start.3 = (f32[5,8,2,128]{3,2,1,0:T(2,128)}, f32[5,8,2,128]{3,2,1,0:T(2,128)S(1)}, u32[]{:S(2)}, u32[]{:S(2)}) collective-permute-start(f32[5,8,2,128]{3,2,1,0:T(2,128)} %get-tuple-element.13), channel_id=1, source_target_pairs={{0,1},{1,2},{2,3},{3,4},{4,5},{5,6},{6,7},{7,8},{8,9},{9,10},{10,1... | collective-permute-start | bytes 122888 | tf_op jit(solution)/shard_map/ppermute | solution.py:202
  61.5 5.5 %collective-permute-start.4 = (f32[5,8,2,128]{3,2,1,0:T(2,128)}, f32[5,8,2,128]{3,2,1,0:T(2,128)S(1)}, u32[]{:S(2)}, u32[]{:S(2)}) collective-permute-start(f32[5,8,2,128]{3,2,1,0:T(2,128)} %get-tuple-element.14), channel_id=1, source_target_pairs={{1,0},{2,1},{3,2},{4,3},{5,4},{6,5},{7,6},{8,7},{9,8},{10,9},{11,1... | collective-permute-start | bytes 122888 | tf_op jit(solution)/shard_map/ppermute | solution.py:202
  63.9 3.1 %copy-start.3 = (f32[5,8,2,128]{3,2,1,0:T(2,128)}, f32[5,8,2,128]{3,2,1,0:T(2,128)S(1)}, u32[]{:S(2)}) copy-start(f32[5,8,2,128]{3,2,1,0:T(2,128)S(1)} %collective-permute-done.3.yl_ref) | copy-start | bytes 122884
  67.0 0.6 copy-start.4
  67.0 0.7 copy-start.1
  67.1 0.7 copy-start.2

commit v4 on v3

--- a/solution.py
+++ b/solution.py
@@ -45,62 +45,48 @@
     return fine.reshape(cells.shape[:-3] + (2 * half, 2 * half, 2 * half))
 
 
-def assemble_kernel(arr_ref, int_ref, src_ref, o_ref, zt_ref, zb_ref, yt_ref, yb_ref, at_ref, p_ref):
-    rows = at_ref.shape[1]
+def assemble_kernel(arr_ref, int_ref, src_ref, o_ref, zt_ref, zb_ref, yt_ref, yb_ref, at_ref):
+    fields, blocks, cells = arr_ref.shape
+    rows = 2 * blocks
     lanes = src_ref.shape[1]
-
-    @pl.when(pl.program_id(0) == 0)
-    def _():
-        row = lax.broadcasted_iota(jnp.int32, (rows, lanes), 0)
-        lane = lax.broadcasted_iota(jnp.int32, (rows, lanes), 1)
-        hit = row == src_ref[...]
-        for x in range(E):
-            sel = hit & (lane % E == x)
-            p_ref[x * rows:(x + 1) * rows, :] = jnp.where(sel, 1.0, 0.0).astype(jnp.bfloat16)
-
-    a = jnp.concatenate([arr_ref[0], int_ref[0]], axis=0)
-    at_ref[...] = a.T
-    zy = at_ref.shape[0] // E
-    w = jnp.concatenate([at_ref[pl.ds(x, zy, stride=E), :] for x in range(E)], axis=1)
+    zy = cells // E
+    row = lax.broadcasted_iota(jnp.int32, (rows, lanes), 0)
+    lane = lax.broadcasted_iota(jnp.int32, (rows, lanes), 1)
+    hit = row == src_ref[...]
+    pm = jnp.concatenate(
+        [jnp.where(hit & (lane % E == x), 1.0, 0.0).astype(jnp.bfloat16) for x in range(E)], axis=0)
+    parts = []
+    for f in range(fields):
+        a = jnp.concatenate([arr_ref[f], int_ref[f]], axis=0)
+        at_ref[f * cells:(f + 1) * cells, :] = a.T
+        parts.append(jnp.concatenate(
+            [at_ref[pl.ds(f * cells + x, zy, stride=E), :] for x in range(E)], axis=1))
+    w = jnp.concatenate(parts, axis=0)
     hi = w.astype(jnp.bfloat16)
     rest = w - hi.astype(jnp.float32)
     mid = rest.astype(jnp.bfloat16)
     lo = (rest - mid.astype(jnp.float32)).astype(jnp.bfloat16)
-    pm = p_ref[...]
-    out = jnp.dot(hi, pm, preferred_element_type=jnp.float32)
-    out = out + jnp.dot(mid, pm, preferred_element_type=jnp.float32)
-    out = out + jnp.dot(lo, pm, preferred_element_type=jnp.float32)
+    res = jnp.dot(jnp.concatenate([hi, mid, lo], axis=0), pm, preferred_element_type=jnp.float32)
+    n = fields * zy
+    out = (res[:n] + res[n:2 * n]) + res[2 * n:]
     width = o_ref.shape[3]
     count = o_ref.shape[2] // E
-    for by in range(count):
-        piece = out[:, by * width:(by + 1) * width].reshape(E, E, width)
-        o_ref[0, :, by * E:(by + 1) * E, :] = piece
-        zt_ref[0, :, by * E:(by + 1) * E, :] = piece[E - 2:]
-        zb_ref[0, :, by * E:(by + 1) * E, :] = piece[:2]
-        if by == 0:
-            yb_ref[0] = piece[:, :2, :]
-        if by == count - 1:
-            yt_ref[0] = piece[:, E - 2:, :]
+    for f in range(fields):
+        for by in range(count):
+            piece = out[f * zy:(f + 1) * zy, by * width:(by + 1) * width].reshape(E, E, width)
+            o_ref[f, :, by * E:(by + 1) * E, :] = piece
+            zt_ref[f, :, by * E:(by + 1) * E, :] = piece[E - 2:]
+            zb_ref[f, :, by * E:(by + 1) * E, :] = piece[:2]
+            if by == 0:
+                yb_ref[f] = piece[:, :2, :]
+            if by == count - 1:
+                yt_ref[f] = piece[:, E - 2:, :]
 
 
 def assemble(arrived, interp, srcrow):
     fields, blocks, cells = arrived.shape
-    lanes = srcrow.shape[1]
     return pl.pallas_call(
         assemble_kernel,
-        grid=(fields,),
-        in_specs=[
-            pl.BlockSpec((1, blocks, cells), lambda f: (f, 0, 0)),
-            pl.BlockSpec((1, blocks, cells), lambda f: (f, 0, 0)),
-            pl.BlockSpec((1, lanes), lambda f: (0, 0)),
-        ],
-        out_specs=[
-            pl.BlockSpec((1, E, BY * E, BX * E), lambda f: (f, 0, 0, 0)),
-            pl.BlockSpec((1, 2, BY * E, BX * E), lambda f: (f, 0, 0, 0)),
-            pl.BlockSpec((1, 2, BY * E, BX * E), lambda f: (f, 0, 0, 0)),
-            pl.BlockSpec((1, E, 2, BX * E), lambda f: (f, 0, 0, 0)),
-            pl.BlockSpec((1, E, 2, BX * E), lambda f: (f, 0, 0, 0)),
-        ],
         out_shape=[
             jax.ShapeDtypeStruct((fields, E, BY * E, BX * E), jnp.float32),
             jax.ShapeDtypeStruct((fields, 2, BY * E, BX * E), jnp.float32),
@@ -108,20 +94,15 @@
             jax.ShapeDtypeStruct((fields, E, 2, BX * E), jnp.float32),
             jax.ShapeDtypeStruct((fields, E, 2, BX * E), jnp.float32),
         ],
-        scratch_shapes=[
-            pltpu.VMEM((cells, 2 * blocks), jnp.float32),
-            pltpu.VMEM((E * 2 * blocks, lanes), jnp.bfloat16),
-        ],
-        compiler_params=pltpu.CompilerParams(dimension_semantics=("arbitrary",)),
+        scratch_shapes=[pltpu.VMEM((fields * cells, 2 * blocks), jnp.float32)],
         interpret=INTERPRET,
     )(arrived, interp, srcrow)
 
 
 def kernel_minmod(left, right):
-    def sgn(v):
-        return jnp.where(v > 0, 1.0, 0.0) - jnp.where(v < 0, 1.0, 0.0)
-
-    return 0.5 * (sgn(left) + sgn(right)) * jnp.minimum(jnp.abs(left), jnp.abs(right))
+    rising = (left > 0) & (right > 0)
+    falling = (left < 0) & (right < 0)
+    return jnp.where(rising, jnp.minimum(left, right), jnp.where(falling, jnp.maximum(left, right), 0.0))
 
 
 def kernel_term(center, lower1, lower2, upper1, coef):
@@ -170,31 +151,6 @@
     )(courant, region, zlo, zhi, ylo, yhi)
 
 
-def axis_terms(padded, axis, coef):
-    size = padded.shape[axis] - 4
-
-    def cut(d):
-        return lax.slice_in_dim(padded, 2 + d, 2 + d + size, axis=axis)
-
-    center = cut(0)
-    lower1 = cut(-1)
-    lower2 = cut(-2)
-    upper1 = cut(1)
-    face_hi = center + 0.5 * minmod(center - lower1, upper1 - center)
-    face_lo = lower1 + 0.5 * minmod(lower1 - lower2, center - lower1)
-    return coef[:, None, None, None] * (face_hi - face_lo)
-
-
-def halo(block, axis, dim, width):
-    count = lax.axis_size(axis)
-    forward = [(i, i + 1) for i in range(count - 1)]
-    backward = [(target, source) for source, target in forward]
-    size = block.shape[dim]
-    low = lax.ppermute(lax.slice_in_dim(block, size - width, size, axis=dim), axis, forward)
-    high = lax.ppermute(lax.slice_in_dim(block, 0, width, axis=dim), axis, backward)
-    return jnp.concatenate([low, block, high], axis=dim)
-
-
 def exchange(top, bottom, axis):
     count = lax.axis_size(axis)
     forward = [(i, i + 1) for i in range(count - 1)]

time: 73.4 us -> 70.7 us (0.963)
  Pallas kernels: 11.4 us -> 8.79 us
    pallas_call x1, Pallas kernels: 6.31 us -> 3.89 us  [assemble(): pl.pallas_call(assemble_kernel, out_shape=[jax.ShapeDtypeStruct((fields,...]
where the time goes in v4:
time: 70.7 us; the launch traced here: 70.2 us
  starting transfers between devices  30.5 us (43%)
  waiting for transfers between devices  17.6 us (25%)
  local copies, waits for them, and re-layouts  8.86 us (13%)
  Pallas kernels  8.79 us (12%)
  other arithmetic  4.17 us (6%)
    ppermute x2, starting transfers between devices, exchange(): lax.ppermute(bottom, axis, backward)  12.5 us
    all_to_all x1, waiting for transfers between devices, local(): lax.all_to_all(outgoing, 'tile', split_axis=0, concat_axis=0, tiled=True)  11.5 us
    all_to_all x1, starting transfers between devices, local(): lax.all_to_all(outgoing, 'tile', split_axis=0, concat_axis=0, tiled=True)  8.07 us
    ppermute x2, starting transfers between devices, exchange(): lax.ppermute(top, axis, forward)  5.91 us
    pallas_call x1, Pallas kernels, advance(): pl.pallas_call(advance_kernel, grid=(fields,), in_specs=[pl.BlockSpec(mem...  4.91 us
    ppermute x1, starting transfers between devices, local(): lax.ppermute(coarse_fine, 'slab', [(i, (i + 1) % slabs) for i in range(sl...  4 us
    pallas_call x1, Pallas kernels, assemble(): pl.pallas_call(assemble_kernel, out_shape=[jax.ShapeDtypeStruct((fields,...  3.89 us
    ppermute x2, waiting for transfers between devices, exchange(): lax.ppermute(bottom, axis, backward)  3.1 us
  transfers between devices with their start and end apart: 6, of which 3 were waited for; matrix products, arithmetic and copies ran while one was open for 14% of the time, Pallas kernels for 0%

profile of v4, /device:TPU:7, one launch (start us, length us, event | category | flops | bytes accessed | tf_op | source)
XLA Modules:
  0.0 70.2 jit_solution(1331424622153516801)
XLA Ops:
  0.0 1.1 %copy.15 = f32[64,5,64]{2,1,0:T(8,128)S(1)} copy(f32[64,5,64]{2,0,1:T(8,128)} %param.8) | data formatting | bytes 163840 | tf_op args[1]
  1.1 4.0 %collective-permute-start = (f32[64,5,64]{2,1,0:T(8,128)S(1)}, f32[64,5,64]{2,1,0:T(8,128)S(1)}, u32[]{:S(2)}, u32[]{:S(2)}) collective-permute-start(f32[64,5,64]{2,1,0:T(8,128)S(1)} %copy.15), channel_id=1, source_target_pairs={{0,16},{16,32},{32,48},{48,64},{64,80},{80,96},{96,112},{112,128},... | collective-permute-start | bytes 245768 | tf_op jit(solution)/shard_map/ppermute | solution.py:169
  5.1 0.9 %convert_reduce_fusion = s32[64]{0:T(128)S(1)} fusion(s32[64]{0:T(128)} %bitcast.27), kind=kLoop, calls=%fused_computation.25 | loop fusion | flops 20416 | bytes 512 | tf_op jit(solution)/shard_map/reduce_sum | solution.py:174
  6.0 0.7 bitcast_select_fusion
  6.7 0.1 select_reduce_fusion
  6.9 1.5 %gather_fusion = f32[64,5,512]{2,0,1:T(8,128)S(1)} fusion(f32[64,5,512]{2,0,1:T(8,128)S(1)} %copy-done, s32[1024]{0:T(1024)S(1)} %pad_clamp_fusion.1), kind=kCustom, calls=%fused_computation | custom fusion | bytes 1310976 | tf_op jit(solution)/shard_map/gather | solution.py:177
  8.4 0.4 copy.13
  8.8 1.0 %reshape.104 = f32[16,80,128]{2,1,0:T(8,128)} reshape(f32[64,5,512]{2,1,0:T(8,128)S(1)} %copy.13) | data formatting | bytes 1310720 | tf_op jit(solution)/shard_map/reshape | solution.py:177
  9.8 8.1 %all-to-all-start = ((f32[16,80,128]{2,1,0:T(8,128)}), f32[16,80,128]{2,1,0:T(8,128)S(1)}, u32[]{:S(2)}, u32[]{:S(2)}) async-start(f32[16,80,128]{2,1,0:T(8,128)} %reshape.104), calls=%async_computation | async-start | bytes 1310720 | tf_op jit(solution)/shard_map/all_to_all | solution.py:178
  17.9 0.1 broadcast_in_dim.13
  18.0 0.7 broadcast_in_dim_reshape.2.src_ref
  18.6 3.0 %collective-permute-done = f32[64,5,64]{2,1,0:T(8,128)S(1)} collective-permute-done((f32[64,5,64]{2,1,0:T(8,128)S(1)}, f32[64,5,64]{2,1,0:T(8,128)S(1)}, u32[]{:S(2)}, u32[]{:S(2)}) %collective-permute-start) | collective-permute-done | bytes 81952 | tf_op jit(solution)/shard_map/ppermute | solution.py:169
  21.7 0.6 gather_fusion.1
  22.3 0.1 copy.16
  22.5 0.9 %minimum_multiply_fusion.2 = (f32[64,5,4,4,4]{0,4,3,2,1:T(4,128)S(1)}, f32[64,5,4,4,4]{0,4,3,2,1:T(4,128)S(1)}, f32[64,5,4,4,4]{0,4,3,2,1:T(4,128)S(1)}) fusion(f32[64,5,4,4,4]{0,4,3,2,1:T(4,128)S(1)} %bitcast.23, f32[64,5,1,4,4]{0,4,3,2,1:T(4,128)S(1)} %get-tuple-element.19, f32[64,5,1,4,4]{0,4,3,2,1:T(4,128)S(1)} %get-tuple-element.18, ...), kind=kLoop, calls=%fused_computation.22 | loop fusion | flops 737280 | bytes 450560 | tf_op jit(solution)/shard_map/mul | solution.py:15
  23.5 0.1 broadcast_multiply_fusion.1
  23.6 0.1 broadcast_multiply_fusion.2
  23.8 0.2 broadcast_multiply_fusion
  24.0 0.2 broadcast_add_fusion
  24.2 0.8 %add_add_fusion = f32[64,5,4,2,4,2,4,2]{0,7,6,5,4,3,2,1:T(2,128)S(1)} fusion(f32[64,5,4,4,4,2]{0,5,4,3,2,1:T(2,128)S(1)} %broadcast_multiply_fusion, f32[64,5,4,2,4,2,4]{0,6,5,4,3,2,1:T(4,128)S(1)} %broadcast_add_fusion, f32[64,5,4,4,4]{0,4,3,2,1:T(4,128)S(1)} %bitcast.24), kind=kLoop, calls=%fused_computation.2 | loop fusion | flops 327680 | bytes 1228800 | tf_op jit(solution)/shard_map/add | solution.py:43
  25.0 1.2 %copy.17 = f32[64,5,512]{2,0,1:T(8,128)} copy(f32[64,5,512]{0,2,1:T(8,128)S(1)} %bitcast.19) | data formatting | bytes 1310720 | tf_op jit(solution)/shard_map/add | solution.py:43
  26.3 11.5 %all-to-all-done = f32[16,80,128]{2,1,0:T(8,128)S(1)} async-done(((f32[16,80,128]{2,1,0:T(8,128)}), f32[16,80,128]{2,1,0:T(8,128)S(1)}, u32[]{:S(2)}, u32[]{:S(2)}) %all-to-all-start) | async-done | bytes 655392 | tf_op jit(solution)/shard_map/all_to_all | solution.py:178
  37.8 0.1 reshape.105
  37.9 1.2 %copy.19 = f32[64,5,512]{2,0,1:T(8,128)} copy(f32[64,5,512]{2,1,0:T(8,128)S(1)} %reshape.105) | data formatting | bytes 1310720 | tf_op jit(solution)/shard_map/reshape | solution.py:179
  39.1 3.9 %shard_map.73 = (f32[5,8,32,128]{3,2,1,0:T(8,128)}, f32[5,2,32,128]{3,2,1,0:T(8,128)}, f32[5,2,32,128]{3,2,1,0:T(8,128)}, f32[5,8,2,128]{3,2,1,0:T(2,128)}, f32[5,8,2,128]{3,2,1,0:T(2,128)}) custom-call(f32[5,64,512]{2,1,0:T(8,128)} %bitcast.25, f32[5,64,512]{2,1,0:T(8,128)} %bitcast.26, s32[1,512]{1,0:T(1,128)} %broadcast_in_dim_reshape.2.src_ref), custom_call_target="tpu_custom_call" | custom-call | tf_op jit(solution)/shard_map/pallas_call | solution.py:88
  43.0 4.0 %collective-permute-start.1 = (f32[5,2,32,128]{3,2,1,0:T(8,128)}, f32[5,2,32,128]{3,2,1,0:T(8,128)S(1)}, u32[]{:S(2)}, u32[]{:S(2)}) collective-permute-start(f32[5,2,32,128]{3,2,1,0:T(8,128)} %get-tuple-element.11), channel_id=1, source_target_pairs={{0,16},{16,32},{32,48},{48,64},{64,80},{80,96},{96,112},{112,128},... | collective-permute-start | bytes 491528 | tf_op jit(solution)/shard_map/ppermute | solution.py:158
  47.0 10.1 %collective-permute-start.2 = (f32[5,2,32,128]{3,2,1,0:T(8,128)}, f32[5,2,32,128]{3,2,1,0:T(8,128)S(1)}, u32[]{:S(2)}, u32[]{:S(2)}) collective-permute-start(f32[5,2,32,128]{3,2,1,0:T(8,128)} %get-tuple-element.12), channel_id=1, source_target_pairs={{16,0},{32,16},{48,32},{64,48},{80,64},{96,80},{112,96},{128,112},... | collective-permute-start | bytes 491528 | tf_op jit(solution)/shard_map/ppermute | solution.py:158
  57.1 1.9 %collective-permute-start.3 = (f32[5,8,2,128]{3,2,1,0:T(2,128)}, f32[5,8,2,128]{3,2,1,0:T(2,128)S(1)}, u32[]{:S(2)}, u32[]{:S(2)}) collective-permute-start(f32[5,8,2,128]{3,2,1,0:T(2,128)} %get-tuple-element.13), channel_id=1, source_target_pairs={{0,1},{1,2},{2,3},{3,4},{4,5},{5,6},{6,7},{7,8},{8,9},{9,10},{10,1... | collective-permute-start | bytes 122888 | tf_op jit(solution)/shard_map/ppermute | solution.py:158
  59.1 2.4 %collective-permute-start.4 = (f32[5,8,2,128]{3,2,1,0:T(2,128)}, f32[5,8,2,128]{3,2,1,0:T(2,128)S(1)}, u32[]{:S(2)}, u32[]{:S(2)}) collective-permute-start(f32[5,8,2,128]{3,2,1,0:T(2,128)} %get-tuple-element.14), channel_id=1, source_target_pairs={{1,0},{2,1},{3,2},{4,3},{5,4},{6,5},{7,6},{8,7},{9,8},{10,9},{11,1... | collective-permute-start | bytes 122888 | tf_op jit(solution)/shard_map/ppermute | solution.py:158
  61.5 3.1 %collective-permute-done.4.yh_ref = f32[5,8,2,128]{3,2,1,0:T(2,128)S(1)} collective-permute-done((f32[5,8,2,128]{3,2,1,0:T(2,128)}, f32[5,8,2,128]{3,2,1,0:T(2,128)S(1)}, u32[]{:S(2)}, u32[]{:S(2)}) %collective-permute-start.4) | collective-permute-done | bytes 40992 | tf_op jit(solution)/shard_map/ppermute | solution.py:158
  64.6 0.6 copy-done.4
  65.3 4.9 %shard_map.74 = f32[5,8,32,128]{3,2,1,0:T(8,128)} custom-call(f32[3,5]{1,0:T(4,128)} %c_ref.1, f32[5,8,32,128]{3,2,1,0:T(8,128)} %get-tuple-element.10.u_ref, f32[5,2,32,128]{3,2,1,0:T(8,128)} %copy-done.1, f32[5,2,32,128]{3,2,1,0:T(8,128)} %copy-done.2, f32[5,8,2,128]{3,2,1,0:T(2,128)} %copy-done.3, f32[5,8,2,128]{3,2,1,0:T(2,128)} %copy-done.4), custom_call_target="tpu_custom_call" | custom-call | tf_op jit(solution)/shard_map/pallas_call | solution.py:135
  (23 shorter events, 0.2 us)
Async XLA Ops:
  0.0 6.8 %copy-start = (f32[64,5,512]{2,0,1:T(8,128)S(1)}, f32[64,5,512]{2,0,1:T(8,128)}, u32[]{:S(2)}) copy-start(f32[64,5,512]{2,0,1:T(8,128)} %param.7) | copy-start | bytes 1966084
  1.1 20.6 %collective-permute-start = (f32[64,5,64]{2,1,0:T(8,128)S(1)}, f32[64,5,64]{2,1,0:T(8,128)S(1)}, u32[]{:S(2)}, u32[]{:S(2)}) collective-permute-start(f32[64,5,64]{2,1,0:T(8,128)S(1)} %copy.15), channel_id=1, source_target_pairs={{0,16},{16,32},{32,48},{48,64},{64,80},{80,96},{96,112},{112,128},... | collective-permute-start | bytes 245768 | tf_op jit(solution)/shard_map/ppermute | solution.py:169
  8.8 9.0 %copy-start.6 = (s32[1,1,64]{2,1,0:T(1,128)S(1)}, s32[1,1,64]{2,1,0:T(1,128)}, u32[]{:S(2)}) copy-start(s32[1,1,64]{2,1,0:T(1,128)} %param.11) | copy-start | bytes 772
  9.8 28.0 %all-to-all-start = ((f32[16,80,128]{2,1,0:T(8,128)}), f32[16,80,128]{2,1,0:T(8,128)S(1)}, u32[]{:S(2)}, u32[]{:S(2)}) async-start(f32[16,80,128]{2,1,0:T(8,128)} %reshape.104), calls=%async_computation | async-start | bytes 1310720 | tf_op jit(solution)/shard_map/all_to_all | solution.py:178
  17.9 5.6 %copy-start.5 = (f32[2]{0:T(128)S(1)}, f32[2]{0:T(128)}, u32[]{:S(2)}) copy-start(f32[2]{0:T(128)} %constant.33.clone) | copy-start | bytes 28
  43.0 21.6 %collective-permute-start.1 = (f32[5,2,32,128]{3,2,1,0:T(8,128)}, f32[5,2,32,128]{3,2,1,0:T(8,128)S(1)}, u32[]{:S(2)}, u32[]{:S(2)}) collective-permute-start(f32[5,2,32,128]{3,2,1,0:T(8,128)} %get-tuple-element.11), channel_id=1, source_target_pairs={{0,16},{16,32},{32,48},{48,64},{64,80},{80,96},{96,112},{112,128},... | collective-permute-start | bytes 491528 | tf_op jit(solution)/shard_map/ppermute | solution.py:158
  47.0 17.6 %collective-permute-start.2 = (f32[5,2,32,128]{3,2,1,0:T(8,128)}, f32[5,2,32,128]{3,2,1,0:T(8,128)S(1)}, u32[]{:S(2)}, u32[]{:S(2)}) collective-permute-start(f32[5,2,32,128]{3,2,1,0:T(8,128)} %get-tuple-element.12), channel_id=1, source_target_pairs={{16,0},{32,16},{48,32},{64,48},{80,64},{96,80},{112,96},{128,112},... | collective-permute-start | bytes 491528 | tf_op jit(solution)/shard_map/ppermute | solution.py:158
  57.1 4.3 %collective-permute-start.3 = (f32[5,8,2,128]{3,2,1,0:T(2,128)}, f32[5,8,2,128]{3,2,1,0:T(2,128)S(1)}, u32[]{:S(2)}, u32[]{:S(2)}) collective-permute-start(f32[5,8,2,128]{3,2,1,0:T(2,128)} %get-tuple-element.13), channel_id=1, source_target_pairs={{0,1},{1,2},{2,3},{3,4},{4,5},{5,6},{6,7},{7,8},{8,9},{9,10},{10,1... | collective-permute-start | bytes 122888 | tf_op jit(solution)/shard_map/ppermute | solution.py:158
  59.1 5.5 %collective-permute-start.4 = (f32[5,8,2,128]{3,2,1,0:T(2,128)}, f32[5,8,2,128]{3,2,1,0:T(2,128)S(1)}, u32[]{:S(2)}, u32[]{:S(2)}) collective-permute-start(f32[5,8,2,128]{3,2,1,0:T(2,128)} %get-tuple-element.14), channel_id=1, source_target_pairs={{1,0},{2,1},{3,2},{4,3},{5,4},{6,5},{7,6},{8,7},{9,8},{10,9},{11,1... | collective-permute-start | bytes 122888 | tf_op jit(solution)/shard_map/ppermute | solution.py:158
  61.5 3.1 %copy-start.3 = (f32[5,8,2,128]{3,2,1,0:T(2,128)}, f32[5,8,2,128]{3,2,1,0:T(2,128)S(1)}, u32[]{:S(2)}) copy-start(f32[5,8,2,128]{3,2,1,0:T(2,128)S(1)} %collective-permute-done.3.yl_ref) | copy-start | bytes 122884
  64.6 0.6 copy-start.4
  64.6 0.7 copy-start.1
  64.6 0.7 %copy-start.2 = (f32[5,2,32,128]{3,2,1,0:T(8,128)}, f32[5,2,32,128]{3,2,1,0:T(8,128)S(1)}, u32[]{:S(2)}) copy-start(f32[5,2,32,128]{3,2,1,0:T(8,128)S(1)} %collective-permute-done.2.zh_ref) | copy-start | bytes 491524

commit v5 on v4

--- a/solution.py
+++ b/solution.py
@@ -45,19 +45,16 @@
     return fine.reshape(cells.shape[:-3] + (2 * half, 2 * half, 2 * half))
 
 
-def assemble_kernel(arr_ref, int_ref, src_ref, o_ref, zt_ref, zb_ref, yt_ref, yb_ref, at_ref):
-    fields, blocks, cells = arr_ref.shape
-    rows = 2 * blocks
-    lanes = src_ref.shape[1]
+def assemble_kernel(arr_ref, int_ref, p_ref, o_ref, zt_ref, zb_ref, yt_ref, yb_ref, at_ref):
+    fields, blocks, cells = int_ref.shape
+    stride = arr_ref.shape[0] // blocks
+    quarters = cells // arr_ref.shape[1]
     zy = cells // E
-    row = lax.broadcasted_iota(jnp.int32, (rows, lanes), 0)
-    lane = lax.broadcasted_iota(jnp.int32, (rows, lanes), 1)
-    hit = row == src_ref[...]
-    pm = jnp.concatenate(
-        [jnp.where(hit & (lane % E == x), 1.0, 0.0).astype(jnp.bfloat16) for x in range(E)], axis=0)
     parts = []
     for f in range(fields):
-        a = jnp.concatenate([arr_ref[f], int_ref[f]], axis=0)
+        moved = jnp.concatenate(
+            [arr_ref[pl.ds(f * quarters + q, blocks, stride=stride), :] for q in range(quarters)], axis=1)
+        a = jnp.concatenate([moved, int_ref[f]], axis=0)
         at_ref[f * cells:(f + 1) * cells, :] = a.T
         parts.append(jnp.concatenate(
             [at_ref[pl.ds(f * cells + x, zy, stride=E), :] for x in range(E)], axis=1))
@@ -66,7 +63,7 @@
     rest = w - hi.astype(jnp.float32)
     mid = rest.astype(jnp.bfloat16)
     lo = (rest - mid.astype(jnp.float32)).astype(jnp.bfloat16)
-    res = jnp.dot(jnp.concatenate([hi, mid, lo], axis=0), pm, preferred_element_type=jnp.float32)
+    res = jnp.dot(jnp.concatenate([hi, mid, lo], axis=0), p_ref[...], preferred_element_type=jnp.float32)
     n = fields * zy
     out = (res[:n] + res[n:2 * n]) + res[2 * n:]
     width = o_ref.shape[3]
@@ -83,8 +80,8 @@
                 yt_ref[f] = piece[:, E - 2:, :]
 
 
-def assemble(arrived, interp, srcrow):
-    fields, blocks, cells = arrived.shape
+def assemble(arrived, interp, onehot):
+    fields, blocks, cells = interp.shape
     return pl.pallas_call(
         assemble_kernel,
         out_shape=[
@@ -96,7 +93,7 @@
         ],
         scratch_shapes=[pltpu.VMEM((fields * cells, 2 * blocks), jnp.float32)],
         interpret=INTERPRET,
-    )(arrived, interp, srcrow)
+    )(arrived, interp, onehot)
 
 
 def kernel_minmod(left, right):
@@ -105,28 +102,30 @@
     return jnp.where(rising, jnp.minimum(left, right), jnp.where(falling, jnp.maximum(left, right), 0.0))
 
 
-def kernel_term(center, lower1, lower2, upper1, coef):
-    face_hi = center + 0.5 * kernel_minmod(center - lower1, upper1 - center)
-    face_lo = lower1 + 0.5 * kernel_minmod(lower1 - lower2, center - lower1)
-    return coef * (face_hi - face_lo)
-
-
-def advance_kernel(c_ref, u_ref, zl_ref, zh_ref, yl_ref, yh_ref, o_ref, yp_ref):
+def face(below, cell, above):
+    return cell + 0.5 * kernel_minmod(cell - below, above - cell)
+
+
+def advance_kernel(c_ref, u_ref, zl_ref, zh_ref, yl_ref, yh_ref, o_ref, yp_ref, g_ref):
     f = pl.program_id(0)
     u = u_ref[0]
     zn, yn, xn = u.shape
     zp = jnp.concatenate([zl_ref[0], u, zh_ref[0]], axis=0)
-    tz = kernel_term(u, zp[1:zn + 1], zp[0:zn], zp[3:zn + 3], c_ref[0, f])
+    gz = face(zp[0:zn + 1], zp[1:zn + 2], zp[2:zn + 3])
+    tz = c_ref[0, f] * (gz[1:] - gz[:-1])
     yp_ref[:, E - 2:E, :] = yl_ref[0]
     yp_ref[:, E:E + yn, :] = u
     yp_ref[:, E + yn:E + yn + 2, :] = yh_ref[0]
-    ty = kernel_term(u, yp_ref[:, E - 1:E - 1 + yn, :], yp_ref[:, E - 2:E - 2 + yn, :],
-                     yp_ref[:, E + 1:E + 1 + yn, :], c_ref[1, f])
+    span = g_ref.shape[1]
+    g_ref[...] = face(yp_ref[:, E - 2:E - 2 + span, :], yp_ref[:, E - 1:E - 1 + span, :],
+                      yp_ref[:, E:E + span, :])
+    ty = c_ref[1, f] * (g_ref[:, 1:yn + 1, :] - g_ref[:, 0:yn, :])
     lane = lax.broadcasted_iota(jnp.int32, u.shape, 2)
     lower1 = jnp.where(lane >= 1, pltpu.roll(u, 1, 2), 0.0)
-    lower2 = jnp.where(lane >= 2, pltpu.roll(u, 2, 2), 0.0)
     upper1 = jnp.where(lane < xn - 1, pltpu.roll(u, xn - 1, 2), 0.0)
-    tx = kernel_term(u, lower1, lower2, upper1, c_ref[2, f])
+    gx = face(lower1, u, upper1)
+    gx_lo = jnp.where(lane >= 1, pltpu.roll(gx, 1, 2), 0.0)
+    tx = c_ref[2, f] * (gx - gx_lo)
     o_ref[0] = u - ((tz + ty) + tx)
 
 
@@ -145,7 +144,10 @@
         ],
         out_specs=pl.BlockSpec((1, zn, yn, xn), lambda f: (f, 0, 0, 0)),
         out_shape=jax.ShapeDtypeStruct(region.shape, jnp.float32),
-        scratch_shapes=[pltpu.VMEM((zn, yn + 2 * E, xn), jnp.float32)],
+        scratch_shapes=[
+            pltpu.VMEM((zn, yn + 2 * E, xn), jnp.float32),
+            pltpu.VMEM((zn, yn + E, xn), jnp.float32),
+        ],
         compiler_params=pltpu.CompilerParams(dimension_semantics=("arbitrary",)),
         interpret=INTERPRET,
     )(courant, region, zlo, zhi, ylo, yhi)
@@ -176,7 +178,7 @@
     send_idx = jnp.sum(jnp.where(position[None, :] == slot[:, None], slot[None, :], 0), axis=1)
     outgoing = old_fine[send_idx].reshape(tiles, per_peer * fields * cells // 128, 128)
     arrived = lax.all_to_all(outgoing, "tile", split_axis=0, concat_axis=0, tiled=True)
-    arrived = arrived.reshape(blocks, fields, cells)
+    arrived = arrived.reshape(-1, 128)
     source = (2 * myself - owner) % tiles
     inverse = source * per_peer + rank
 
@@ -185,8 +187,12 @@
 
     flags = new_refine.reshape(-1)
     src = jnp.where(flags == 1, blocks + slot, inverse)
-    srcrow = jnp.repeat(src, E)[None, :]
-    region, ztop, zbot, ytop, ybot = assemble(arrived.transpose(1, 0, 2), interp.transpose(1, 0, 2), srcrow)
+    lane = jnp.arange(blocks * E, dtype=jnp.int32)
+    row = jnp.arange(2 * blocks, dtype=jnp.int32)
+    hit = (row[None, :, None] == src[lane // E][None, None, :]) & (
+        lane[None, None, :] % E == jnp.arange(E, dtype=jnp.int32)[:, None, None])
+    onehot = hit.astype(jnp.bfloat16).reshape(E * 2 * blocks, blocks * E)
+    region, ztop, zbot, ytop, ybot = assemble(arrived, interp.transpose(1, 0, 2), onehot)
 
     zlo, zhi = exchange(ztop, zbot, "slab")
     ylo, yhi = exchange(ytop, ybot, "tile")

time: 70.7 us -> 106 us (1.50)
  the two profiles are of different devices: /device:TPU:7 before, /device:TPU:31 now
where the time goes in v5:
time: 106 us; the launch traced here: 105 us
  other arithmetic  47.3 us (45%)
  starting transfers between devices  32.8 us (31%)
  local copies, waits for them, and re-layouts  10.5 us (10%)
  Pallas kernels  9.03 us (9%)
  waiting for transfers between devices  4.81 us (5%)
    gather x59, other arithmetic, local(): src[lane // E][None, None, :]  41.9 us
    ppermute x2, starting transfers between devices, exchange(): lax.ppermute(bottom, axis, backward)  12.1 us
    ppermute x2, starting transfers between devices, exchange(): lax.ppermute(top, axis, forward)  8.85 us
    all_to_all x1, starting transfers between devices, local(): lax.all_to_all(outgoing, 'tile', split_axis=0, concat_axis=0, tiled=True)  7.9 us
    ppermute x2, waiting for transfers between devices, exchange(): lax.ppermute(bottom, axis, backward)  4.8 us
    pallas_call x1, Pallas kernels, advance(): pl.pallas_call(advance_kernel, grid=(fields,), in_specs=[pl.BlockSpec(mem...  4.78 us
    pallas_call x1, Pallas kernels, assemble(): pl.pallas_call(assemble_kernel, out_shape=[jax.ShapeDtypeStruct((fields,...  4.25 us
    ppermute x1, starting transfers between devices, local(): lax.ppermute(coarse_fine, 'slab', [(i, (i + 1) % slabs) for i in range(sl...  4 us
  transfers between devices with their start and end apart: 6, of which 1 were waited for; matrix products, arithmetic and copies ran while one was open for 53% of the time, Pallas kernels for 0%

profile of v5, /device:TPU:31, one launch (start us, length us, event | category | flops | bytes accessed | tf_op | source)
XLA Modules:
  0.0 104.8 jit_solution(11420778713093972419)
XLA Ops:
  0.0 1.1 %copy.13 = f32[64,5,64]{2,1,0:T(8,128)S(1)} copy(f32[64,5,64]{2,0,1:T(8,128)} %param.8) | data formatting | bytes 163840 | tf_op args[1]
  1.1 4.0 %collective-permute-start = (f32[64,5,64]{2,1,0:T(8,128)S(1)}, f32[64,5,64]{2,1,0:T(8,128)S(1)}, u32[]{:S(2)}, u32[]{:S(2)}) collective-permute-start(f32[64,5,64]{2,1,0:T(8,128)S(1)} %copy.13), channel_id=1, source_target_pairs={{0,16},{16,32},{32,48},{48,64},{64,80},{80,96},{96,112},{112,128},... | collective-permute-start | bytes 245768 | tf_op jit(solution)/shard_map/ppermute | solution.py:171
  5.1 0.9 convert_reduce_fusion
  6.0 0.7 bitcast_select_fusion
  6.9 1.5 %gather_fusion = f32[64,5,512]{2,0,1:T(8,128)S(1)} fusion(f32[64,5,512]{2,0,1:T(8,128)S(1)} %copy-done, s32[1024]{0:T(1024)S(1)} %pad_clamp_fusion.1), kind=kCustom, calls=%fused_computation | custom fusion | bytes 1310976 | tf_op jit(solution)/shard_map/gather | solution.py:179
  8.4 0.4 copy.12
  8.8 1.0 reshape.215
  9.8 7.9 %all-to-all-start = ((f32[16,80,128]{2,1,0:T(8,128)}), f32[16,80,128]{2,1,0:T(8,128)S(1)}, u32[]{:S(2)}, u32[]{:S(2)}) async-start(f32[16,80,128]{2,1,0:T(8,128)} %reshape.215), calls=%async_computation | async-start | bytes 1310720 | tf_op jit(solution)/shard_map/all_to_all | solution.py:180
  19.7 0.7 fusion.21
  20.3 0.7 fusion.18
  21.1 0.7 fusion.19
  21.8 0.7 fusion.20
  22.6 4.4 %compare_select_fusion.1 = s32[512,1]{0,1:T(1,128)S(1)} fusion(s32[]{:T(128)} %bitcast.67, s32[]{:T(128)} %bitcast.68, s32[]{:T(128)} %bitcast.69, s32[]{:T(128)} %bitcast.70, s32[]{:T(128)} %bitcast.71, s32[]{:T(128)} %bitcast.73, s32[]{:T(128)} %bitcast.72), kind=kLoop, calls=%fused_computation.88 | loop fusion | flops 11776 | bytes 2076 | tf_op jit(solution)/shard_map/gather | solution.py:192
  27.0 35.5 %select_select_fusion = s32[512]{0:T(512)S(1)} fusion(pred[512]{0:T(512)(128)(4,1)S(1)} %compare_reduce_fusion, pred[512]{0:T(512)(128)(4,1)S(1)} %compare_reduce_fusion.1, pred[512]{0:T(512)(128)(4,1)S(1)} %compare_reduce_fusion.2, pred[512]{0:T(512)(128)(4,1)S(1)} %compare_reduce_fusion.3, pred[512]{0:T(512)(128)(4,1)S(1)} %compare_reduce_fusion.4, ...), kind=kLoop, calls=%fused_computation.105 | loop fusion | flops 29184 | bytes 33508 | tf_op jit(solution)/shard_map/gather | solution.py:192
  62.6 1.2 %and_convert_fusion = bf16[8,128,512]{2,1,0:T(8,128)(2,1)} fusion(pred[8,512]{1,0:T(8,128)(4,1)S(1)} %iota_compare_fusion.3, pred[128,512]{1,0:T(8,128)(4,1)S(1)} %iota_compare_fusion), kind=kLoop, calls=%fused_computation.2 | loop fusion | flops 1048576 | bytes 1118208 | tf_op jit(solution)/shard_map/convert_element_type | solution.py:194
  63.8 0.6 gather_fusion.1
  64.7 0.9 minimum_multiply_fusion.2
  65.6 0.1 broadcast_multiply_fusion.2
  65.7 0.1 broadcast_multiply_fusion.1
  65.9 0.2 broadcast_multiply_fusion
  66.1 0.2 broadcast_add_fusion
  66.3 0.8 add_add_fusion
  67.2 1.2 %copy.15 = f32[64,5,512]{2,0,1:T(8,128)} copy(f32[64,5,512]{0,2,1:T(8,128)S(1)} %bitcast.83) | data formatting | bytes 1310720 | tf_op jit(solution)/shard_map/add | solution.py:43
  68.4 0.8 copy-done.1
  69.2 4.3 %shard_map.73 = (f32[5,8,32,128]{3,2,1,0:T(8,128)}, f32[5,2,32,128]{3,2,1,0:T(8,128)}, f32[5,2,32,128]{3,2,1,0:T(8,128)}, f32[5,8,2,128]{3,2,1,0:T(2,128)}, f32[5,8,2,128]{3,2,1,0:T(2,128)}) custom-call(f32[1280,128]{1,0:T(8,128)} %bitcast.90, f32[5,64,512]{2,1,0:T(8,128)} %bitcast.91, bf16[1024,512]{1,0:T(8,128)(2,1)} %bitcast.84), custom_call_target="tpu_custom_call" | custom-call | tf_op jit(solution)/shard_map/pallas_call | solution.py:85
  73.5 4.0 %collective-permute-start.1 = (f32[5,2,32,128]{3,2,1,0:T(8,128)}, f32[5,2,32,128]{3,2,1,0:T(8,128)S(1)}, u32[]{:S(2)}, u32[]{:S(2)}) collective-permute-start(f32[5,2,32,128]{3,2,1,0:T(8,128)} %get-tuple-element.11), channel_id=1, source_target_pairs={{0,16},{16,32},{32,48},{48,64},{64,80},{80,96},{96,112},{112,128},... | collective-permute-start | bytes 491528 | tf_op jit(solution)/shard_map/ppermute | solution.py:160
  77.5 10.1 %collective-permute-start.2 = (f32[5,2,32,128]{3,2,1,0:T(8,128)}, f32[5,2,32,128]{3,2,1,0:T(8,128)S(1)}, u32[]{:S(2)}, u32[]{:S(2)}) collective-permute-start(f32[5,2,32,128]{3,2,1,0:T(8,128)} %get-tuple-element.12), channel_id=1, source_target_pairs={{16,0},{32,16},{48,32},{64,48},{80,64},{96,80},{112,96},{128,112},... | collective-permute-start | bytes 491528 | tf_op jit(solution)/shard_map/ppermute | solution.py:160
  87.6 4.9 %collective-permute-start.3 = (f32[5,8,2,128]{3,2,1,0:T(2,128)}, f32[5,8,2,128]{3,2,1,0:T(2,128)S(1)}, u32[]{:S(2)}, u32[]{:S(2)}) collective-permute-start(f32[5,8,2,128]{3,2,1,0:T(2,128)} %get-tuple-element.13), channel_id=1, source_target_pairs={{0,1},{1,2},{2,3},{3,4},{4,5},{5,6},{6,7},{7,8},{8,9},{9,10},{10,1... | collective-permute-start | bytes 122888 | tf_op jit(solution)/shard_map/ppermute | solution.py:160
  92.5 1.9 %collective-permute-start.4 = (f32[5,8,2,128]{3,2,1,0:T(2,128)}, f32[5,8,2,128]{3,2,1,0:T(2,128)S(1)}, u32[]{:S(2)}, u32[]{:S(2)}) collective-permute-start(f32[5,8,2,128]{3,2,1,0:T(2,128)} %get-tuple-element.14), channel_id=1, source_target_pairs={{1,0},{2,1},{3,2},{4,3},{5,4},{6,5},{7,6},{8,7},{9,8},{10,9},{11,1... | collective-permute-start | bytes 122888 | tf_op jit(solution)/shard_map/ppermute | solution.py:160
  94.4 4.8 %collective-permute-done.4.yh_ref = f32[5,8,2,128]{3,2,1,0:T(2,128)S(1)} collective-permute-done((f32[5,8,2,128]{3,2,1,0:T(2,128)}, f32[5,8,2,128]{3,2,1,0:T(2,128)S(1)}, u32[]{:S(2)}, u32[]{:S(2)}) %collective-permute-start.4) | collective-permute-done | bytes 40992 | tf_op jit(solution)/shard_map/ppermute | solution.py:160
  99.3 0.6 copy-done.5
  100.0 4.8 %shard_map.74 = f32[5,8,32,128]{3,2,1,0:T(8,128)} custom-call(f32[3,5]{1,0:T(4,128)} %c_ref.1, f32[5,8,32,128]{3,2,1,0:T(8,128)} %get-tuple-element.10.u_ref, f32[5,2,32,128]{3,2,1,0:T(8,128)} %copy-done.2, f32[5,2,32,128]{3,2,1,0:T(8,128)} %copy-done.3, f32[5,8,2,128]{3,2,1,0:T(2,128)} %copy-done.4, f32[5,8,2,128]{3,2,1,0:T(2,128)} %copy-done.5), custom_call_target="tpu_custom_call" | custom-call | tf_op jit(solution)/shard_map/pallas_call | solution.py:134
  (88 shorter events, 2.5 us)
Async XLA Ops:
  0.0 6.8 %copy-start = (f32[64,5,512]{2,0,1:T(8,128)S(1)}, f32[64,5,512]{2,0,1:T(8,128)}, u32[]{:S(2)}) copy-start(f32[64,5,512]{2,0,1:T(8,128)} %param.7) | copy-start | bytes 1966084
  1.1 62.7 %collective-permute-start = (f32[64,5,64]{2,1,0:T(8,128)S(1)}, f32[64,5,64]{2,1,0:T(8,128)S(1)}, u32[]{:S(2)}, u32[]{:S(2)}) collective-permute-start(f32[64,5,64]{2,1,0:T(8,128)S(1)} %copy.13), channel_id=1, source_target_pairs={{0,16},{16,32},{32,48},{48,64},{64,80},{80,96},{96,112},{112,128},... | collective-permute-start | bytes 245768 | tf_op jit(solution)/shard_map/ppermute | solution.py:171
  8.8 13.7 %copy-start.7 = (s32[1,1,64]{2,1,0:T(1,128)S(1)}, s32[1,1,64]{2,1,0:T(1,128)}, u32[]{:S(2)}) copy-start(s32[1,1,64]{2,1,0:T(1,128)} %param.11) | copy-start | bytes 772
  9.8 58.6 %all-to-all-start = ((f32[16,80,128]{2,1,0:T(8,128)}), f32[16,80,128]{2,1,0:T(8,128)S(1)}, u32[]{:S(2)}, u32[]{:S(2)}) async-start(f32[16,80,128]{2,1,0:T(8,128)} %reshape.215), calls=%async_computation | async-start | bytes 1310720 | tf_op jit(solution)/shard_map/all_to_all | solution.py:180
  63.8 1.8 %copy-start.6 = (f32[2]{0:T(128)S(1)}, f32[2]{0:T(128)}, u32[]{:S(2)}) copy-start(f32[2]{0:T(128)} %constant.64.clone) | copy-start | bytes 28
  68.4 0.8 copy-start.1
  73.5 25.8 %collective-permute-start.1 = (f32[5,2,32,128]{3,2,1,0:T(8,128)}, f32[5,2,32,128]{3,2,1,0:T(8,128)S(1)}, u32[]{:S(2)}, u32[]{:S(2)}) collective-permute-start(f32[5,2,32,128]{3,2,1,0:T(8,128)} %get-tuple-element.11), channel_id=1, source_target_pairs={{0,16},{16,32},{32,48},{48,64},{64,80},{80,96},{96,112},{112,128},... | collective-permute-start | bytes 491528 | tf_op jit(solution)/shard_map/ppermute | solution.py:160
  77.5 21.8 %collective-permute-start.2 = (f32[5,2,32,128]{3,2,1,0:T(8,128)}, f32[5,2,32,128]{3,2,1,0:T(8,128)S(1)}, u32[]{:S(2)}, u32[]{:S(2)}) collective-permute-start(f32[5,2,32,128]{3,2,1,0:T(8,128)} %get-tuple-element.12), channel_id=1, source_target_pairs={{16,0},{32,16},{48,32},{64,48},{80,64},{96,80},{112,96},{128,112},... | collective-permute-start | bytes 491528 | tf_op jit(solution)/shard_map/ppermute | solution.py:160
  87.6 6.8 %collective-permute-start.3 = (f32[5,8,2,128]{3,2,1,0:T(2,128)}, f32[5,8,2,128]{3,2,1,0:T(2,128)S(1)}, u32[]{:S(2)}, u32[]{:S(2)}) collective-permute-start(f32[5,8,2,128]{3,2,1,0:T(2,128)} %get-tuple-element.13), channel_id=1, source_target_pairs={{0,1},{1,2},{2,3},{3,4},{4,5},{5,6},{6,7},{7,8},{8,9},{9,10},{10,1... | collective-permute-start | bytes 122888 | tf_op jit(solution)/shard_map/ppermute | solution.py:160
  92.5 6.7 %collective-permute-start.4 = (f32[5,8,2,128]{3,2,1,0:T(2,128)}, f32[5,8,2,128]{3,2,1,0:T(2,128)S(1)}, u32[]{:S(2)}, u32[]{:S(2)}) collective-permute-start(f32[5,8,2,128]{3,2,1,0:T(2,128)} %get-tuple-element.14), channel_id=1, source_target_pairs={{1,0},{2,1},{3,2},{4,3},{5,4},{6,5},{7,6},{8,7},{9,8},{10,9},{11,1... | collective-permute-start | bytes 122888 | tf_op jit(solution)/shard_map/ppermute | solution.py:160
  94.4 4.8 %copy-start.4 = (f32[5,8,2,128]{3,2,1,0:T(2,128)}, f32[5,8,2,128]{3,2,1,0:T(2,128)S(1)}, u32[]{:S(2)}) copy-start(f32[5,8,2,128]{3,2,1,0:T(2,128)S(1)} %collective-permute-done.3.yl_ref) | copy-start | bytes 122884
  99.2 0.6 copy-start.5
  99.2 0.7 copy-start.2
  99.2 0.7 copy-start.3

commit v6 on v5

--- a/solution.py
+++ b/solution.py
@@ -80,6 +80,26 @@
                 yt_ref[f] = piece[:, E - 2:, :]
 
 
+def onehot_kernel(src_ref, p_ref):
+    rows = p_ref.shape[0] // E
+    lanes = src_ref.shape[1]
+    row = lax.broadcasted_iota(jnp.int32, (rows, lanes), 0)
+    lane = lax.broadcasted_iota(jnp.int32, (rows, lanes), 1)
+    hit = row == src_ref[...]
+    for x in range(E):
+        sel = hit & (lane % E == x)
+        p_ref[x * rows:(x + 1) * rows, :] = jnp.where(sel, 1.0, 0.0).astype(jnp.bfloat16)
+
+
+def build_onehot(srcrow, rows):
+    lanes = srcrow.shape[1]
+    return pl.pallas_call(
+        onehot_kernel,
+        out_shape=jax.ShapeDtypeStruct((E * rows, lanes), jnp.bfloat16),
+        interpret=INTERPRET,
+    )(srcrow)
+
+
 def assemble(arrived, interp, onehot):
     fields, blocks, cells = interp.shape
     return pl.pallas_call(
@@ -108,25 +128,38 @@
 
 def advance_kernel(c_ref, u_ref, zl_ref, zh_ref, yl_ref, yh_ref, o_ref, yp_ref, g_ref):
     f = pl.program_id(0)
-    u = u_ref[0]
-    zn, yn, xn = u.shape
-    zp = jnp.concatenate([zl_ref[0], u, zh_ref[0]], axis=0)
-    gz = face(zp[0:zn + 1], zp[1:zn + 2], zp[2:zn + 3])
-    tz = c_ref[0, f] * (gz[1:] - gz[:-1])
+    zn, yn, xn = u_ref.shape[1:]
+    cz = c_ref[0, f]
+    cy = c_ref[1, f]
+    cx = c_ref[2, f]
     yp_ref[:, E - 2:E, :] = yl_ref[0]
-    yp_ref[:, E:E + yn, :] = u
+    yp_ref[:, E:E + yn, :] = u_ref[0]
     yp_ref[:, E + yn:E + yn + 2, :] = yh_ref[0]
-    span = g_ref.shape[1]
-    g_ref[...] = face(yp_ref[:, E - 2:E - 2 + span, :], yp_ref[:, E - 1:E - 1 + span, :],
-                      yp_ref[:, E:E + span, :])
-    ty = c_ref[1, f] * (g_ref[:, 1:yn + 1, :] - g_ref[:, 0:yn, :])
-    lane = lax.broadcasted_iota(jnp.int32, u.shape, 2)
-    lower1 = jnp.where(lane >= 1, pltpu.roll(u, 1, 2), 0.0)
-    upper1 = jnp.where(lane < xn - 1, pltpu.roll(u, xn - 1, 2), 0.0)
-    gx = face(lower1, u, upper1)
-    gx_lo = jnp.where(lane >= 1, pltpu.roll(gx, 1, 2), 0.0)
-    tx = c_ref[2, f] * (gx - gx_lo)
-    o_ref[0] = u - ((tz + ty) + tx)
+    span = g_ref.shape[0]
+    lane = lax.broadcasted_iota(jnp.int32, (yn, xn), 1)
+
+    def plane(j):
+        if j < 2:
+            return zl_ref[0, j]
+        if j < zn + 2:
+            return u_ref[0, j - 2]
+        return zh_ref[0, j - zn - 2]
+
+    g_prev = face(plane(0), plane(1), plane(2))
+    for z in range(zn):
+        u = plane(z + 2)
+        g_next = face(plane(z + 1), u, plane(z + 3))
+        tz = cz * (g_next - g_prev)
+        g_prev = g_next
+        g_ref[...] = face(yp_ref[z, E - 2:E - 2 + span, :], yp_ref[z, E - 1:E - 1 + span, :],
+                          yp_ref[z, E:E + span, :])
+        ty = cy * (g_ref[1:yn + 1, :] - g_ref[0:yn, :])
+        lower1 = jnp.where(lane >= 1, pltpu.roll(u, 1, 1), 0.0)
+        upper1 = jnp.where(lane < xn - 1, pltpu.roll(u, xn - 1, 1), 0.0)
+        gx = face(lower1, u, upper1)
+        gx_lo = jnp.where(lane >= 1, pltpu.roll(gx, 1, 1), 0.0)
+        tx = cx * (gx - gx_lo)
+        o_ref[0, z] = u - ((tz + ty) + tx)
 
 
 def advance(courant, region, zlo, zhi, ylo, yhi):
@@ -146,7 +179,7 @@
         out_shape=jax.ShapeDtypeStruct(region.shape, jnp.float32),
         scratch_shapes=[
             pltpu.VMEM((zn, yn + 2 * E, xn), jnp.float32),
-            pltpu.VMEM((zn, yn + E, xn), jnp.float32),
+            pltpu.VMEM((yn + E, xn), jnp.float32),
         ],
         compiler_params=pltpu.CompilerParams(dimension_semantics=("arbitrary",)),
         interpret=INTERPRET,
@@ -187,11 +220,7 @@
 
     flags = new_refine.reshape(-1)
     src = jnp.where(flags == 1, blocks + slot, inverse)
-    lane = jnp.arange(blocks * E, dtype=jnp.int32)
-    row = jnp.arange(2 * blocks, dtype=jnp.int32)
-    hit = (row[None, :, None] == src[lane // E][None, None, :]) & (
-        lane[None, None, :] % E == jnp.arange(E, dtype=jnp.int32)[:, None, None])
-    onehot = hit.astype(jnp.bfloat16).reshape(E * 2 * blocks, blocks * E)
+    onehot = build_onehot(jnp.repeat(src, E)[None, :], 2 * blocks)
     region, ztop, zbot, ytop, ybot = assemble(arrived, interp.transpose(1, 0, 2), onehot)
 
     zlo, zhi = exchange(ztop, zbot, "slab")

time: 106 us -> 70.4 us (0.66)
  the two profiles are of different devices: /device:TPU:31 before, /device:TPU:7 now
where the time goes in v6:
time: 70.4 us; the launch traced here: 69.9 us
  starting transfers between devices  30.5 us (43%)
  waiting for transfers between devices  15.8 us (22%)
  Pallas kernels  10.8 us (15%)
  local copies, waits for them, and re-layouts  8.38 us (12%)
  other arithmetic  4.17 us (6%)
    ppermute x2, starting transfers between devices, exchange(): lax.ppermute(bottom, axis, backward)  12.5 us
    all_to_all x1, waiting for transfers between devices, local(): lax.all_to_all(outgoing, 'tile', split_axis=0, concat_axis=0, tiled=True)  11.5 us
    all_to_all x1, starting transfers between devices, local(): lax.all_to_all(outgoing, 'tile', split_axis=0, concat_axis=0, tiled=True)  8.07 us
    ppermute x2, starting transfers between devices, exchange(): lax.ppermute(top, axis, forward)  5.91 us
    pallas_call x1, Pallas kernels, advance(): pl.pallas_call(advance_kernel, grid=(fields,), in_specs=[pl.BlockSpec(mem...  4.7 us
    pallas_call x1, Pallas kernels, assemble(): pl.pallas_call(assemble_kernel, out_shape=[jax.ShapeDtypeStruct((fields,...  4.26 us
    ppermute x1, starting transfers between devices, local(): lax.ppermute(coarse_fine, 'slab', [(i, (i + 1) % slabs) for i in range(sl...  4 us
    ppermute x2, waiting for transfers between devices, exchange(): lax.ppermute(bottom, axis, backward)  3.1 us
  transfers between devices with their start and end apart: 6, of which 3 were waited for; matrix products, arithmetic and copies ran while one was open for 14% of the time, Pallas kernels for 3%

profile of v6, /device:TPU:7, one launch (start us, length us, event | category | flops | bytes accessed | tf_op | source)
XLA Modules:
  0.0 69.9 jit_solution(3264766168176322449)
XLA Ops:
  0.0 1.1 %copy.13 = f32[64,5,64]{2,1,0:T(8,128)S(1)} copy(f32[64,5,64]{2,0,1:T(8,128)} %param.8) | data formatting | bytes 163840 | tf_op args[1]
  1.1 4.0 %collective-permute-start = (f32[64,5,64]{2,1,0:T(8,128)S(1)}, f32[64,5,64]{2,1,0:T(8,128)S(1)}, u32[]{:S(2)}, u32[]{:S(2)}) collective-permute-start(f32[64,5,64]{2,1,0:T(8,128)S(1)} %copy.13), channel_id=1, source_target_pairs={{0,16},{16,32},{32,48},{48,64},{64,80},{80,96},{96,112},{112,128},... | collective-permute-start | bytes 245768 | tf_op jit(solution)/shard_map/ppermute | solution.py:204
  5.1 0.9 %convert_reduce_fusion = s32[64]{0:T(128)S(1)} fusion(s32[64]{0:T(128)} %bitcast.25), kind=kLoop, calls=%fused_computation.24 | loop fusion | flops 20416 | bytes 512 | tf_op jit(solution)/shard_map/reduce_sum | solution.py:209
  6.0 0.7 bitcast_select_fusion
  6.7 0.1 select_reduce_fusion
  6.9 1.5 %gather_fusion = f32[64,5,512]{2,0,1:T(8,128)S(1)} fusion(f32[64,5,512]{2,0,1:T(8,128)S(1)} %copy-done, s32[1024]{0:T(1024)S(1)} %pad_clamp_fusion.1), kind=kCustom, calls=%fused_computation | custom fusion | bytes 1310976 | tf_op jit(solution)/shard_map/gather | solution.py:212
  8.4 0.4 copy.12
  8.8 1.0 %reshape.104 = f32[16,80,128]{2,1,0:T(8,128)} reshape(f32[64,5,512]{2,1,0:T(8,128)S(1)} %copy.12) | data formatting | bytes 1310720 | tf_op jit(solution)/shard_map/reshape | solution.py:212
  9.8 8.1 %all-to-all-start = ((f32[16,80,128]{2,1,0:T(8,128)}), f32[16,80,128]{2,1,0:T(8,128)S(1)}, u32[]{:S(2)}, u32[]{:S(2)}) async-start(f32[16,80,128]{2,1,0:T(8,128)} %reshape.104), calls=%async_computation | async-start | bytes 1310720 | tf_op jit(solution)/shard_map/all_to_all | solution.py:213
  17.9 0.1 broadcast_in_dim.13
  17.9 0.7 broadcast_in_dim_reshape.2.src_ref
  18.6 1.8 %shard_map.73.p_ref = bf16[1024,512]{1,0:T(8,128)(2,1)} custom-call(s32[1,512]{1,0:T(1,128)} %broadcast_in_dim_reshape.2.src_ref), custom_call_target="tpu_custom_call" | custom-call | tf_op jit(solution)/shard_map/pallas_call | solution.py:96
  20.5 1.2 %collective-permute-done = f32[64,5,64]{2,1,0:T(8,128)S(1)} collective-permute-done((f32[64,5,64]{2,1,0:T(8,128)S(1)}, f32[64,5,64]{2,1,0:T(8,128)S(1)}, u32[]{:S(2)}, u32[]{:S(2)}) %collective-permute-start) | collective-permute-done | bytes 81952 | tf_op jit(solution)/shard_map/ppermute | solution.py:204
  21.7 0.6 gather_fusion.1
  22.3 0.1 copy.14
  22.5 0.9 %minimum_multiply_fusion.2 = (f32[64,5,4,4,4]{0,4,3,2,1:T(4,128)S(1)}, f32[64,5,4,4,4]{0,4,3,2,1:T(4,128)S(1)}, f32[64,5,4,4,4]{0,4,3,2,1:T(4,128)S(1)}) fusion(f32[64,5,4,4,4]{0,4,3,2,1:T(4,128)S(1)} %bitcast.21, f32[64,5,1,4,4]{0,4,3,2,1:T(4,128)S(1)} %get-tuple-element.19, f32[64,5,1,4,4]{0,4,3,2,1:T(4,128)S(1)} %get-tuple-element.18, ...), kind=kLoop, calls=%fused_computation.21 | loop fusion | flops 737280 | bytes 450560 | tf_op jit(solution)/shard_map/mul | solution.py:15
  23.5 0.1 broadcast_multiply_fusion.2
  23.6 0.1 broadcast_multiply_fusion.1
  23.8 0.2 broadcast_multiply_fusion
  24.0 0.2 broadcast_add_fusion
  24.2 0.8 %add_add_fusion = f32[64,5,4,2,4,2,4,2]{0,7,6,5,4,3,2,1:T(2,128)S(1)} fusion(f32[64,5,4,4,4,2]{0,5,4,3,2,1:T(2,128)S(1)} %broadcast_multiply_fusion, f32[64,5,4,2,4,2,4]{0,6,5,4,3,2,1:T(4,128)S(1)} %broadcast_add_fusion, f32[64,5,4,4,4]{0,4,3,2,1:T(4,128)S(1)} %bitcast.22), kind=kLoop, calls=%fused_computation.2 | loop fusion | flops 327680 | bytes 1228800 | tf_op jit(solution)/shard_map/add | solution.py:43
  25.0 1.2 %copy.15 = f32[64,5,512]{2,0,1:T(8,128)} copy(f32[64,5,512]{0,2,1:T(8,128)S(1)} %bitcast.17) | data formatting | bytes 1310720 | tf_op jit(solution)/shard_map/add | solution.py:43
  26.3 11.5 %all-to-all-done = f32[16,80,128]{2,1,0:T(8,128)S(1)} async-done(((f32[16,80,128]{2,1,0:T(8,128)}), f32[16,80,128]{2,1,0:T(8,128)S(1)}, u32[]{:S(2)}, u32[]{:S(2)}) %all-to-all-start) | async-done | bytes 655392 | tf_op jit(solution)/shard_map/all_to_all | solution.py:213
  37.8 0.8 %copy-done.1 = f32[16,80,128]{2,1,0:T(8,128)} copy-done((f32[16,80,128]{2,1,0:T(8,128)}, f32[16,80,128]{2,1,0:T(8,128)S(1)}, u32[]{:S(2)}) %copy-start.1) | copy-done | bytes 655384
  38.6 4.3 %shard_map.74 = (f32[5,8,32,128]{3,2,1,0:T(8,128)}, f32[5,2,32,128]{3,2,1,0:T(8,128)}, f32[5,2,32,128]{3,2,1,0:T(8,128)}, f32[5,8,2,128]{3,2,1,0:T(2,128)}, f32[5,8,2,128]{3,2,1,0:T(2,128)}) custom-call(f32[1280,128]{1,0:T(8,128)} %bitcast.23, f32[5,64,512]{2,1,0:T(8,128)} %bitcast.24, bf16[1024,512]{1,0:T(8,128)(2,1)} %shard_map.73.p_ref), custom_call_target="tpu_custom_call" | custom-call | tf_op jit(solution)/shard_map/pallas_call | solution.py:105
  42.9 4.0 %collective-permute-start.1 = (f32[5,2,32,128]{3,2,1,0:T(8,128)}, f32[5,2,32,128]{3,2,1,0:T(8,128)S(1)}, u32[]{:S(2)}, u32[]{:S(2)}) collective-permute-start(f32[5,2,32,128]{3,2,1,0:T(8,128)} %get-tuple-element.11), channel_id=1, source_target_pairs={{0,16},{16,32},{32,48},{48,64},{64,80},{80,96},{96,112},{112,128},... | collective-permute-start | bytes 491528 | tf_op jit(solution)/shard_map/ppermute | solution.py:193
  46.9 10.1 %collective-permute-start.2 = (f32[5,2,32,128]{3,2,1,0:T(8,128)}, f32[5,2,32,128]{3,2,1,0:T(8,128)S(1)}, u32[]{:S(2)}, u32[]{:S(2)}) collective-permute-start(f32[5,2,32,128]{3,2,1,0:T(8,128)} %get-tuple-element.12), channel_id=1, source_target_pairs={{16,0},{32,16},{48,32},{64,48},{80,64},{96,80},{112,96},{128,112},... | collective-permute-start | bytes 491528 | tf_op jit(solution)/shard_map/ppermute | solution.py:193
  57.0 1.9 %collective-permute-start.3 = (f32[5,8,2,128]{3,2,1,0:T(2,128)}, f32[5,8,2,128]{3,2,1,0:T(2,128)S(1)}, u32[]{:S(2)}, u32[]{:S(2)}) collective-permute-start(f32[5,8,2,128]{3,2,1,0:T(2,128)} %get-tuple-element.13), channel_id=1, source_target_pairs={{0,1},{1,2},{2,3},{3,4},{4,5},{5,6},{6,7},{7,8},{8,9},{9,10},{10,1... | collective-permute-start | bytes 122888 | tf_op jit(solution)/shard_map/ppermute | solution.py:193
  59.0 2.4 %collective-permute-start.4 = (f32[5,8,2,128]{3,2,1,0:T(2,128)}, f32[5,8,2,128]{3,2,1,0:T(2,128)S(1)}, u32[]{:S(2)}, u32[]{:S(2)}) collective-permute-start(f32[5,8,2,128]{3,2,1,0:T(2,128)} %get-tuple-element.14), channel_id=1, source_target_pairs={{1,0},{2,1},{3,2},{4,3},{5,4},{6,5},{7,6},{8,7},{9,8},{10,9},{11,1... | collective-permute-start | bytes 122888 | tf_op jit(solution)/shard_map/ppermute | solution.py:193
  61.4 3.1 %collective-permute-done.4.yh_ref = f32[5,8,2,128]{3,2,1,0:T(2,128)S(1)} collective-permute-done((f32[5,8,2,128]{3,2,1,0:T(2,128)}, f32[5,8,2,128]{3,2,1,0:T(2,128)S(1)}, u32[]{:S(2)}, u32[]{:S(2)}) %collective-permute-start.4) | collective-permute-done | bytes 40992 | tf_op jit(solution)/shard_map/ppermute | solution.py:193
  64.5 0.6 copy-done.5
  65.2 4.7 %shard_map.75 = f32[5,8,32,128]{3,2,1,0:T(8,128)} custom-call(f32[3,5]{1,0:T(4,128)} %c_ref.1, f32[5,8,32,128]{3,2,1,0:T(8,128)} %get-tuple-element.10.u_ref, f32[5,2,32,128]{3,2,1,0:T(8,128)} %copy-done.2, f32[5,2,32,128]{3,2,1,0:T(8,128)} %copy-done.3, f32[5,8,2,128]{3,2,1,0:T(2,128)} %copy-done.4, f32[5,8,2,128]{3,2,1,0:T(2,128)} %copy-done.5), custom_call_target="tpu_custom_call" | custom-call | tf_op jit(solution)/shard_map/pallas_call | solution.py:167
  (24 shorter events, 0.3 us)
Async XLA Ops:
  0.0 6.8 %copy-start = (f32[64,5,512]{2,0,1:T(8,128)S(1)}, f32[64,5,512]{2,0,1:T(8,128)}, u32[]{:S(2)}) copy-start(f32[64,5,512]{2,0,1:T(8,128)} %param.7) | copy-start | bytes 1966084
  1.1 20.6 %collective-permute-start = (f32[64,5,64]{2,1,0:T(8,128)S(1)}, f32[64,5,64]{2,1,0:T(8,128)S(1)}, u32[]{:S(2)}, u32[]{:S(2)}) collective-permute-start(f32[64,5,64]{2,1,0:T(8,128)S(1)} %copy.13), channel_id=1, source_target_pairs={{0,16},{16,32},{32,48},{48,64},{64,80},{80,96},{96,112},{112,128},... | collective-permute-start | bytes 245768 | tf_op jit(solution)/shard_map/ppermute | solution.py:204
  8.8 9.0 %copy-start.7 = (s32[1,1,64]{2,1,0:T(1,128)S(1)}, s32[1,1,64]{2,1,0:T(1,128)}, u32[]{:S(2)}) copy-start(s32[1,1,64]{2,1,0:T(1,128)} %param.11) | copy-start | bytes 772
  9.8 28.0 %all-to-all-start = ((f32[16,80,128]{2,1,0:T(8,128)}), f32[16,80,128]{2,1,0:T(8,128)S(1)}, u32[]{:S(2)}, u32[]{:S(2)}) async-start(f32[16,80,128]{2,1,0:T(8,128)} %reshape.104), calls=%async_computation | async-start | bytes 1310720 | tf_op jit(solution)/shard_map/all_to_all | solution.py:213
  20.5 3.0 %copy-start.6 = (f32[2]{0:T(128)S(1)}, f32[2]{0:T(128)}, u32[]{:S(2)}) copy-start(f32[2]{0:T(128)} %constant.33.clone) | copy-start | bytes 28
  37.8 0.8 %copy-start.1 = (f32[16,80,128]{2,1,0:T(8,128)}, f32[16,80,128]{2,1,0:T(8,128)S(1)}, u32[]{:S(2)}) copy-start(f32[16,80,128]{2,1,0:T(8,128)S(1)} %all-to-all-done) | copy-start | bytes 1966084
  42.9 21.6 %collective-permute-start.1 = (f32[5,2,32,128]{3,2,1,0:T(8,128)}, f32[5,2,32,128]{3,2,1,0:T(8,128)S(1)}, u32[]{:S(2)}, u32[]{:S(2)}) collective-permute-start(f32[5,2,32,128]{3,2,1,0:T(8,128)} %get-tuple-element.11), channel_id=1, source_target_pairs={{0,16},{16,32},{32,48},{48,64},{64,80},{80,96},{96,112},{112,128},... | collective-permute-start | bytes 491528 | tf_op jit(solution)/shard_map/ppermute | solution.py:193
  46.9 17.6 %collective-permute-start.2 = (f32[5,2,32,128]{3,2,1,0:T(8,128)}, f32[5,2,32,128]{3,2,1,0:T(8,128)S(1)}, u32[]{:S(2)}, u32[]{:S(2)}) collective-permute-start(f32[5,2,32,128]{3,2,1,0:T(8,128)} %get-tuple-element.12), channel_id=1, source_target_pairs={{16,0},{32,16},{48,32},{64,48},{80,64},{96,80},{112,96},{128,112},... | collective-permute-start | bytes 491528 | tf_op jit(solution)/shard_map/ppermute | solution.py:193
  57.0 4.3 %collective-permute-start.3 = (f32[5,8,2,128]{3,2,1,0:T(2,128)}, f32[5,8,2,128]{3,2,1,0:T(2,128)S(1)}, u32[]{:S(2)}, u32[]{:S(2)}) collective-permute-start(f32[5,8,2,128]{3,2,1,0:T(2,128)} %get-tuple-element.13), channel_id=1, source_target_pairs={{0,1},{1,2},{2,3},{3,4},{4,5},{5,6},{6,7},{7,8},{8,9},{9,10},{10,1... | collective-permute-start | bytes 122888 | tf_op jit(solution)/shard_map/ppermute | solution.py:193
  59.0 5.5 %collective-permute-start.4 = (f32[5,8,2,128]{3,2,1,0:T(2,128)}, f32[5,8,2,128]{3,2,1,0:T(2,128)S(1)}, u32[]{:S(2)}, u32[]{:S(2)}) collective-permute-start(f32[5,8,2,128]{3,2,1,0:T(2,128)} %get-tuple-element.14), channel_id=1, source_target_pairs={{1,0},{2,1},{3,2},{4,3},{5,4},{6,5},{7,6},{8,7},{9,8},{10,9},{11,1... | collective-permute-start | bytes 122888 | tf_op jit(solution)/shard_map/ppermute | solution.py:193
  61.4 3.1 %copy-start.4 = (f32[5,8,2,128]{3,2,1,0:T(2,128)}, f32[5,8,2,128]{3,2,1,0:T(2,128)S(1)}, u32[]{:S(2)}) copy-start(f32[5,8,2,128]{3,2,1,0:T(2,128)S(1)} %collective-permute-done.3.yl_ref) | copy-start | bytes 122884
  64.5 0.6 copy-start.5
  64.5 0.7 copy-start.2
  64.5 0.7 %copy-start.3 = (f32[5,2,32,128]{3,2,1,0:T(8,128)}, f32[5,2,32,128]{3,2,1,0:T(8,128)S(1)}, u32[]{:S(2)}) copy-start(f32[5,2,32,128]{3,2,1,0:T(8,128)S(1)} %collective-permute-done.2.zh_ref) | copy-start | bytes 491524

commit v7 on v6

--- a/solution.py
+++ b/solution.py
@@ -15,7 +15,7 @@
     return 0.5 * (jnp.sign(left) + jnp.sign(right)) * jnp.minimum(jnp.abs(left), jnp.abs(right))
 
 
-def slopes(cells, axis):
+def slopes_kt(cells, axis):
     width = [(0, 0)] * cells.ndim
     width[axis] = (1, 1)
     padded = jnp.pad(cells, width, mode="edge")
@@ -25,28 +25,28 @@
     return minmod(cells - below, above - cells)
 
 
-def refine_block(cells):
+def refine_block_kt(cells):
     nd = cells.ndim
-    slope_z = slopes(cells, nd - 3)
-    slope_y = slopes(cells, nd - 2)
-    slope_x = slopes(cells, nd - 1)
+    slope_z = slopes_kt(cells, nd - 4)
+    slope_y = slopes_kt(cells, nd - 3)
+    slope_x = slopes_kt(cells, nd - 2)
     sigma = jnp.array([-0.25, 0.25], jnp.float32)
 
     def spread(value):
-        return value[..., :, None, :, None, :, None]
+        return value[..., :, None, :, None, :, None, :]
 
     offset = (
-        spread(slope_z) * sigma[:, None, None, None, None]
-        + spread(slope_y) * sigma[:, None, None]
-        + spread(slope_x) * sigma
+        spread(slope_z) * sigma[:, None, None, None, None, None]
+        + spread(slope_y) * sigma[:, None, None, None]
+        + spread(slope_x) * sigma[:, None]
     )
     fine = spread(cells) + offset
-    half = cells.shape[-1]
-    return fine.reshape(cells.shape[:-3] + (2 * half, 2 * half, 2 * half))
+    half = cells.shape[-2]
+    return fine.reshape(cells.shape[:-4] + ((2 * half) ** 3, cells.shape[-1]))
 
 
 def assemble_kernel(arr_ref, int_ref, p_ref, o_ref, zt_ref, zb_ref, yt_ref, yb_ref, at_ref):
-    fields, blocks, cells = int_ref.shape
+    fields, cells, blocks = int_ref.shape
     stride = arr_ref.shape[0] // blocks
     quarters = cells // arr_ref.shape[1]
     zy = cells // E
@@ -54,8 +54,9 @@
     for f in range(fields):
         moved = jnp.concatenate(
             [arr_ref[pl.ds(f * quarters + q, blocks, stride=stride), :] for q in range(quarters)], axis=1)
-        a = jnp.concatenate([moved, int_ref[f]], axis=0)
+        a = jnp.concatenate([moved, jnp.zeros_like(moved)], axis=0)
         at_ref[f * cells:(f + 1) * cells, :] = a.T
+        at_ref[f * cells:(f + 1) * cells, blocks:] = int_ref[f]
         parts.append(jnp.concatenate(
             [at_ref[pl.ds(f * cells + x, zy, stride=E), :] for x in range(E)], axis=1))
     w = jnp.concatenate(parts, axis=0)
@@ -101,7 +102,7 @@
 
 
 def assemble(arrived, interp, onehot):
-    fields, blocks, cells = interp.shape
+    fields, cells, blocks = interp.shape
     return pl.pallas_call(
         assemble_kernel,
         out_shape=[
@@ -216,12 +217,13 @@
     inverse = source * per_peer + rank
 
     parents = coarse_prev[parent_map.reshape(-1)]
-    interp = refine_block(parents.reshape(blocks, fields, half, half, half)).reshape(blocks, fields, cells)
+    parents = parents.transpose(1, 2, 0).reshape(fields, half, half, half, blocks)
+    interp = refine_block_kt(parents)
 
     flags = new_refine.reshape(-1)
     src = jnp.where(flags == 1, blocks + slot, inverse)
     onehot = build_onehot(jnp.repeat(src, E)[None, :], 2 * blocks)
-    region, ztop, zbot, ytop, ybot = assemble(arrived, interp.transpose(1, 0, 2), onehot)
+    region, ztop, zbot, ytop, ybot = assemble(arrived, interp, onehot)
 
     zlo, zhi = exchange(ztop, zbot, "slab")
     ylo, yhi = exchange(ytop, ybot, "tile")

time: 70.4 us -> 70.9 us (level)
  local copies, waits for them, and re-layouts: 8.38 us -> 7.14 us
  other arithmetic: 4.17 us -> 5.27 us
    add x1 -> x0, local copies, waits for them, and re-layouts: 1.23 us -> none  [refine_block(): fine = spread(cells) + offset]
    add x2, other arithmetic: 1.01 us -> 2.11 us  [the longest x1 1.92 us: refine_block_kt(): fine = spread(cells) + offset]
where the time goes in v7:
time: 70.9 us; the launch traced here: 70.5 us
  starting transfers between devices  30.5 us (43%)
  waiting for transfers between devices  16 us (23%)
  Pallas kernels  11.3 us (16%)
  local copies, waits for them, and re-layouts  7.14 us (10%)
  other arithmetic  5.27 us (7%)
    ppermute x2, starting transfers between devices, exchange(): lax.ppermute(bottom, axis, backward)  12.5 us
    all_to_all x1, waiting for transfers between devices, local(): lax.all_to_all(outgoing, 'tile', split_axis=0, concat_axis=0, tiled=True)  11.7 us
    all_to_all x1, starting transfers between devices, local(): lax.all_to_all(outgoing, 'tile', split_axis=0, concat_axis=0, tiled=True)  8.07 us
    ppermute x2, starting transfers between devices, exchange(): lax.ppermute(top, axis, forward)  5.91 us
    pallas_call x1, Pallas kernels, assemble(): pl.pallas_call(assemble_kernel, out_shape=[jax.ShapeDtypeStruct((fields,...  4.8 us
    pallas_call x1, Pallas kernels, advance(): pl.pallas_call(advance_kernel, grid=(fields,), in_specs=[pl.BlockSpec(mem...  4.7 us
    ppermute x1, starting transfers between devices, local(): lax.ppermute(coarse_fine, 'slab', [(i, (i + 1) % slabs) for i in range(sl...  4 us
    ppermute x2, waiting for transfers between devices, exchange(): lax.ppermute(bottom, axis, backward)  3.1 us
  transfers between devices with their start and end apart: 6, of which 3 were waited for; matrix products, arithmetic and copies ran while one was open for 14% of the time, Pallas kernels for 3%

profile of v7, /device:TPU:7, one launch (start us, length us, event | category | flops | bytes accessed | tf_op | source)
XLA Modules:
  0.0 70.5 jit_solution(8867449062730033426)
XLA Ops:
  0.0 1.1 %copy.16 = f32[64,5,64]{2,1,0:T(8,128)S(1)} copy(f32[64,5,64]{2,0,1:T(8,128)} %param.8) | data formatting | bytes 163840 | tf_op args[1]
  1.1 4.0 %collective-permute-start = (f32[64,5,64]{2,1,0:T(8,128)S(1)}, f32[64,5,64]{2,1,0:T(8,128)S(1)}, u32[]{:S(2)}, u32[]{:S(2)}) collective-permute-start(f32[64,5,64]{2,1,0:T(8,128)S(1)} %copy.16), channel_id=1, source_target_pairs={{0,16},{16,32},{32,48},{48,64},{64,80},{80,96},{96,112},{112,128},... | collective-permute-start | bytes 245768 | tf_op jit(solution)/shard_map/ppermute | solution.py:205
  5.1 0.9 %convert_reduce_fusion = s32[64]{0:T(128)S(1)} fusion(s32[64]{0:T(128)} %bitcast.25), kind=kLoop, calls=%fused_computation.24 | loop fusion | flops 20416 | bytes 512 | tf_op jit(solution)/shard_map/reduce_sum | solution.py:210
  6.0 0.7 bitcast_select_fusion
  6.7 0.1 select_reduce_fusion
  6.9 1.5 %gather_fusion = f32[64,5,512]{2,0,1:T(8,128)S(1)} fusion(f32[64,5,512]{2,0,1:T(8,128)S(1)} %copy-done, s32[1024]{0:T(1024)S(1)} %pad_clamp_fusion.1), kind=kCustom, calls=%fused_computation | custom fusion | bytes 1310976 | tf_op jit(solution)/shard_map/gather | solution.py:213
  8.4 0.4 copy.15
  8.8 1.0 %reshape.105 = f32[16,80,128]{2,1,0:T(8,128)} reshape(f32[64,5,512]{2,1,0:T(8,128)S(1)} %copy.15) | data formatting | bytes 1310720 | tf_op jit(solution)/shard_map/reshape | solution.py:213
  9.8 8.1 %all-to-all-start = ((f32[16,80,128]{2,1,0:T(8,128)}), f32[16,80,128]{2,1,0:T(8,128)S(1)}, u32[]{:S(2)}, u32[]{:S(2)}) async-start(f32[16,80,128]{2,1,0:T(8,128)} %reshape.105), calls=%async_computation | async-start | bytes 1310720 | tf_op jit(solution)/shard_map/all_to_all | solution.py:214
  17.9 0.1 broadcast_in_dim.13
  17.9 0.7 broadcast_in_dim_reshape.2.src_ref
  18.6 1.8 %shard_map.73.p_ref = bf16[1024,512]{1,0:T(8,128)(2,1)} custom-call(s32[1,512]{1,0:T(1,128)} %broadcast_in_dim_reshape.2.src_ref), custom_call_target="tpu_custom_call" | custom-call | tf_op jit(solution)/shard_map/pallas_call | solution.py:97
  20.4 1.2 %collective-permute-done = f32[64,5,64]{2,1,0:T(8,128)S(1)} collective-permute-done((f32[64,5,64]{2,1,0:T(8,128)S(1)}, f32[64,5,64]{2,1,0:T(8,128)S(1)}, u32[]{:S(2)}, u32[]{:S(2)}) %collective-permute-start) | collective-permute-done | bytes 81952 | tf_op jit(solution)/shard_map/ppermute | solution.py:205
  21.7 0.6 gather_fusion.1
  22.3 0.1 copy.17
  22.5 0.9 %minimum_multiply_fusion.2 = (f32[5,4,4,4,64]{4,3,2,1,0:T(4,128)S(1)}, f32[5,4,4,4,64]{4,3,2,1,0:T(4,128)S(1)}, f32[5,4,4,4,64]{4,3,2,1,0:T(4,128)S(1)}) fusion(f32[5,4,4,4,64]{4,3,2,1,0:T(4,128)S(1)} %bitcast.21, f32[5,1,4,4,64]{4,3,2,1,0:T(4,128)S(1)} %get-tuple-element.19, f32[5,1,4,4,64]{4,3,2,1,0:T(4,128)S(1)} %get-tuple-element.18, ...), kind=kLoop, calls=%fused_computation.21 | loop fusion | flops 737280 | bytes 450560 | tf_op jit(solution)/shard_map/mul | solution.py:15
  23.5 0.1 broadcast_multiply_fusion.2
  23.6 0.1 broadcast_multiply_fusion.1
  23.8 0.2 broadcast_multiply_fusion
  24.0 0.2 broadcast_add_fusion
  24.2 1.9 %add_add_fusion = f32[5,4,2,4,2,4,2,64]{7,6,5,4,3,2,1,0:T(2,128)} fusion(f32[5,4,4,4,2,64]{5,4,3,2,1,0:T(2,128)S(1)} %broadcast_multiply_fusion, f32[5,4,2,4,2,4,64]{6,5,4,3,2,1,0:T(4,128)S(1)} %broadcast_add_fusion, f32[5,4,4,4,64]{4,3,2,1,0:T(4,128)S(1)} %bitcast.22), kind=kLoop, calls=%fused_computation.2 | loop fusion | flops 327680 | bytes 1228800 | tf_op jit(solution)/shard_map/add | solution.py:43
  26.1 11.7 %all-to-all-done = f32[16,80,128]{2,1,0:T(8,128)S(1)} async-done(((f32[16,80,128]{2,1,0:T(8,128)}), f32[16,80,128]{2,1,0:T(8,128)S(1)}, u32[]{:S(2)}, u32[]{:S(2)}) %all-to-all-start) | async-done | bytes 655392 | tf_op jit(solution)/shard_map/all_to_all | solution.py:214
  37.8 0.8 %copy-done.1 = f32[16,80,128]{2,1,0:T(8,128)} copy-done((f32[16,80,128]{2,1,0:T(8,128)}, f32[16,80,128]{2,1,0:T(8,128)S(1)}, u32[]{:S(2)}) %copy-start.1) | copy-done | bytes 655384
  38.6 4.8 %shard_map.74 = (f32[5,8,32,128]{3,2,1,0:T(8,128)}, f32[5,2,32,128]{3,2,1,0:T(8,128)}, f32[5,2,32,128]{3,2,1,0:T(8,128)}, f32[5,8,2,128]{3,2,1,0:T(2,128)}, f32[5,8,2,128]{3,2,1,0:T(2,128)}) custom-call(f32[1280,128]{1,0:T(8,128)} %bitcast.23, f32[5,512,64]{2,1,0:T(8,128)} %bitcast.17, bf16[1024,512]{1,0:T(8,128)(2,1)} %shard_map.73.p_ref), custom_call_target="tpu_custom_call" | custom-call | tf_op jit(solution)/shard_map/pallas_call | solution.py:106
  43.4 4.0 %collective-permute-start.1 = (f32[5,2,32,128]{3,2,1,0:T(8,128)}, f32[5,2,32,128]{3,2,1,0:T(8,128)S(1)}, u32[]{:S(2)}, u32[]{:S(2)}) collective-permute-start(f32[5,2,32,128]{3,2,1,0:T(8,128)} %get-tuple-element.11), channel_id=1, source_target_pairs={{0,16},{16,32},{32,48},{48,64},{64,80},{80,96},{96,112},{112,128},... | collective-permute-start | bytes 491528 | tf_op jit(solution)/shard_map/ppermute | solution.py:194
  47.4 10.1 %collective-permute-start.2 = (f32[5,2,32,128]{3,2,1,0:T(8,128)}, f32[5,2,32,128]{3,2,1,0:T(8,128)S(1)}, u32[]{:S(2)}, u32[]{:S(2)}) collective-permute-start(f32[5,2,32,128]{3,2,1,0:T(8,128)} %get-tuple-element.12), channel_id=1, source_target_pairs={{16,0},{32,16},{48,32},{64,48},{80,64},{96,80},{112,96},{128,112},... | collective-permute-start | bytes 491528 | tf_op jit(solution)/shard_map/ppermute | solution.py:194
  57.6 1.9 %collective-permute-start.3 = (f32[5,8,2,128]{3,2,1,0:T(2,128)}, f32[5,8,2,128]{3,2,1,0:T(2,128)S(1)}, u32[]{:S(2)}, u32[]{:S(2)}) collective-permute-start(f32[5,8,2,128]{3,2,1,0:T(2,128)} %get-tuple-element.13), channel_id=1, source_target_pairs={{0,1},{1,2},{2,3},{3,4},{4,5},{5,6},{6,7},{7,8},{8,9},{9,10},{10,1... | collective-permute-start | bytes 122888 | tf_op jit(solution)/shard_map/ppermute | solution.py:194
  59.5 2.4 %collective-permute-start.4 = (f32[5,8,2,128]{3,2,1,0:T(2,128)}, f32[5,8,2,128]{3,2,1,0:T(2,128)S(1)}, u32[]{:S(2)}, u32[]{:S(2)}) collective-permute-start(f32[5,8,2,128]{3,2,1,0:T(2,128)} %get-tuple-element.14), channel_id=1, source_target_pairs={{1,0},{2,1},{3,2},{4,3},{5,4},{6,5},{7,6},{8,7},{9,8},{10,9},{11,1... | collective-permute-start | bytes 122888 | tf_op jit(solution)/shard_map/ppermute | solution.py:194
  61.9 3.1 %collective-permute-done.4.yh_ref = f32[5,8,2,128]{3,2,1,0:T(2,128)S(1)} collective-permute-done((f32[5,8,2,128]{3,2,1,0:T(2,128)}, f32[5,8,2,128]{3,2,1,0:T(2,128)S(1)}, u32[]{:S(2)}, u32[]{:S(2)}) %collective-permute-start.4) | collective-permute-done | bytes 40992 | tf_op jit(solution)/shard_map/ppermute | solution.py:194
  65.1 0.6 copy-done.5
  65.6 0.1 copy-done.2
  65.8 4.7 %shard_map.75 = f32[5,8,32,128]{3,2,1,0:T(8,128)} custom-call(f32[3,5]{1,0:T(4,128)} %c_ref.1, f32[5,8,32,128]{3,2,1,0:T(8,128)} %get-tuple-element.10.u_ref, f32[5,2,32,128]{3,2,1,0:T(8,128)} %copy-done.2, f32[5,2,32,128]{3,2,1,0:T(8,128)} %copy-done.3, f32[5,8,2,128]{3,2,1,0:T(2,128)} %copy-done.4, f32[5,8,2,128]{3,2,1,0:T(2,128)} %copy-done.5), custom_call_target="tpu_custom_call" | custom-call | tf_op jit(solution)/shard_map/pallas_call | solution.py:168
  (23 shorter events, 0.2 us)
Async XLA Ops:
  0.0 6.8 %copy-start = (f32[64,5,512]{2,0,1:T(8,128)S(1)}, f32[64,5,512]{2,0,1:T(8,128)}, u32[]{:S(2)}) copy-start(f32[64,5,512]{2,0,1:T(8,128)} %param.7) | copy-start | bytes 1966084
  1.1 20.6 %collective-permute-start = (f32[64,5,64]{2,1,0:T(8,128)S(1)}, f32[64,5,64]{2,1,0:T(8,128)S(1)}, u32[]{:S(2)}, u32[]{:S(2)}) collective-permute-start(f32[64,5,64]{2,1,0:T(8,128)S(1)} %copy.16), channel_id=1, source_target_pairs={{0,16},{16,32},{32,48},{48,64},{64,80},{80,96},{96,112},{112,128},... | collective-permute-start | bytes 245768 | tf_op jit(solution)/shard_map/ppermute | solution.py:205
  8.8 9.0 %copy-start.7 = (s32[1,1,64]{2,1,0:T(1,128)S(1)}, s32[1,1,64]{2,1,0:T(1,128)}, u32[]{:S(2)}) copy-start(s32[1,1,64]{2,1,0:T(1,128)} %param.11) | copy-start | bytes 772
  9.8 28.0 %all-to-all-start = ((f32[16,80,128]{2,1,0:T(8,128)}), f32[16,80,128]{2,1,0:T(8,128)S(1)}, u32[]{:S(2)}, u32[]{:S(2)}) async-start(f32[16,80,128]{2,1,0:T(8,128)} %reshape.105), calls=%async_computation | async-start | bytes 1310720 | tf_op jit(solution)/shard_map/all_to_all | solution.py:214
  20.4 3.1 %copy-start.6 = (f32[2]{0:T(128)S(1)}, f32[2]{0:T(128)}, u32[]{:S(2)}) copy-start(f32[2]{0:T(128)} %constant.33.clone) | copy-start | bytes 28
  37.8 0.8 %copy-start.1 = (f32[16,80,128]{2,1,0:T(8,128)}, f32[16,80,128]{2,1,0:T(8,128)S(1)}, u32[]{:S(2)}) copy-start(f32[16,80,128]{2,1,0:T(8,128)S(1)} %all-to-all-done) | copy-start | bytes 1966084
  43.4 21.6 %collective-permute-start.1 = (f32[5,2,32,128]{3,2,1,0:T(8,128)}, f32[5,2,32,128]{3,2,1,0:T(8,128)S(1)}, u32[]{:S(2)}, u32[]{:S(2)}) collective-permute-start(f32[5,2,32,128]{3,2,1,0:T(8,128)} %get-tuple-element.11), channel_id=1, source_target_pairs={{0,16},{16,32},{32,48},{48,64},{64,80},{80,96},{96,112},{112,128},... | collective-permute-start | bytes 491528 | tf_op jit(solution)/shard_map/ppermute | solution.py:194
  47.4 17.6 %collective-permute-start.2 = (f32[5,2,32,128]{3,2,1,0:T(8,128)}, f32[5,2,32,128]{3,2,1,0:T(8,128)S(1)}, u32[]{:S(2)}, u32[]{:S(2)}) collective-permute-start(f32[5,2,32,128]{3,2,1,0:T(8,128)} %get-tuple-element.12), channel_id=1, source_target_pairs={{16,0},{32,16},{48,32},{64,48},{80,64},{96,80},{112,96},{128,112},... | collective-permute-start | bytes 491528 | tf_op jit(solution)/shard_map/ppermute | solution.py:194
  57.6 4.3 %collective-permute-start.3 = (f32[5,8,2,128]{3,2,1,0:T(2,128)}, f32[5,8,2,128]{3,2,1,0:T(2,128)S(1)}, u32[]{:S(2)}, u32[]{:S(2)}) collective-permute-start(f32[5,8,2,128]{3,2,1,0:T(2,128)} %get-tuple-element.13), channel_id=1, source_target_pairs={{0,1},{1,2},{2,3},{3,4},{4,5},{5,6},{6,7},{7,8},{8,9},{9,10},{10,1... | collective-permute-start | bytes 122888 | tf_op jit(solution)/shard_map/ppermute | solution.py:194
  59.5 5.5 %collective-permute-start.4 = (f32[5,8,2,128]{3,2,1,0:T(2,128)}, f32[5,8,2,128]{3,2,1,0:T(2,128)S(1)}, u32[]{:S(2)}, u32[]{:S(2)}) collective-permute-start(f32[5,8,2,128]{3,2,1,0:T(2,128)} %get-tuple-element.14), channel_id=1, source_target_pairs={{1,0},{2,1},{3,2},{4,3},{5,4},{6,5},{7,6},{8,7},{9,8},{10,9},{11,1... | collective-permute-start | bytes 122888 | tf_op jit(solution)/shard_map/ppermute | solution.py:194
  61.9 3.1 %copy-start.4 = (f32[5,8,2,128]{3,2,1,0:T(2,128)}, f32[5,8,2,128]{3,2,1,0:T(2,128)S(1)}, u32[]{:S(2)}) copy-start(f32[5,8,2,128]{3,2,1,0:T(2,128)S(1)} %collective-permute-done.3.yl_ref) | copy-start | bytes 122884
  65.0 0.6 copy-start.5
  65.0 0.7 copy-start.2
  65.0 0.7 %copy-start.3 = (f32[5,2,32,128]{3,2,1,0:T(8,128)}, f32[5,2,32,128]{3,2,1,0:T(8,128)S(1)}, u32[]{:S(2)}) copy-start(f32[5,2,32,128]{3,2,1,0:T(8,128)S(1)} %collective-permute-done.2.zh_ref) | copy-start | bytes 491524

commit v8 on v7

--- a/solution.py
+++ b/solution.py
@@ -9,10 +9,6 @@
 BX = 16
 BY = 4
 INTERPRET = False
-
-
-def minmod(left, right):
-    return 0.5 * (jnp.sign(left) + jnp.sign(right)) * jnp.minimum(jnp.abs(left), jnp.abs(right))
 
 
 def slopes_kt(cells, axis):
@@ -22,7 +18,7 @@
     size = cells.shape[axis]
     below = lax.slice_in_dim(padded, 0, size, axis=axis)
     above = lax.slice_in_dim(padded, 2, size + 2, axis=axis)
-    return minmod(cells - below, above - cells)
+    return kernel_minmod(cells - below, above - cells)
 
 
 def refine_block_kt(cells):
@@ -118,9 +114,7 @@
 
 
 def kernel_minmod(left, right):
-    rising = (left > 0) & (right > 0)
-    falling = (left < 0) & (right < 0)
-    return jnp.where(rising, jnp.minimum(left, right), jnp.where(falling, jnp.maximum(left, right), 0.0))
+    return jnp.maximum(jnp.minimum(left, right), jnp.minimum(0.0, jnp.maximum(left, right)))
 
 
 def face(below, cell, above):

time: 70.9 us -> 70.7 us (level)
    mul x1 -> x0, other arithmetic: 0.94 us -> none  [minmod(): 0.5 * (jnp.sign(left) + jnp.sign(right))]
  transfers between devices with their start and end apart: 6 -> 6, of which waited for: 3 -> 3; matrix products, arithmetic and copies ran while one was open for 14% -> 13% of each run, Pallas kernels for 3% -> 3%
where the time goes in v8:
time: 70.7 us; the launch traced here: 70.2 us
  starting transfers between devices  30.5 us (43%)
  waiting for transfers between devices  16.5 us (23%)
  Pallas kernels  11.1 us (16%)
  local copies, waits for them, and re-layouts  7.14 us (10%)
  other arithmetic  4.76 us (7%)
    ppermute x2, starting transfers between devices, exchange(): lax.ppermute(bottom, axis, backward)  12.5 us
    all_to_all x1, waiting for transfers between devices, local(): lax.all_to_all(outgoing, 'tile', split_axis=0, concat_axis=0, tiled=True)  12.2 us
    all_to_all x1, starting transfers between devices, local(): lax.all_to_all(outgoing, 'tile', split_axis=0, concat_axis=0, tiled=True)  8.07 us
    ppermute x2, starting transfers between devices, exchange(): lax.ppermute(top, axis, forward)  5.91 us
    pallas_call x1, Pallas kernels, assemble(): pl.pallas_call(assemble_kernel, out_shape=[jax.ShapeDtypeStruct((fields,...  4.8 us
    pallas_call x1, Pallas kernels, advance(): pl.pallas_call(advance_kernel, grid=(fields,), in_specs=[pl.BlockSpec(mem...  4.46 us
    ppermute x1, starting transfers between devices, local(): lax.ppermute(coarse_fine, 'slab', [(i, (i + 1) % slabs) for i in range(sl...  4 us
    ppermute x2, waiting for transfers between devices, exchange(): lax.ppermute(bottom, axis, backward)  3.1 us
  transfers between devices with their start and end apart: 6, of which 3 were waited for; matrix products, arithmetic and copies ran while one was open for 13% of the time, Pallas kernels for 3%

profile of v8, /device:TPU:7, one launch (start us, length us, event | category | flops | bytes accessed | tf_op | source)
XLA Modules:
  0.0 70.2 jit_solution(7237745798473921752)
XLA Ops:
  0.0 1.1 %copy.16 = f32[64,5,64]{2,1,0:T(8,128)S(1)} copy(f32[64,5,64]{2,0,1:T(8,128)} %param.8) | data formatting | bytes 163840 | tf_op args[1]
  1.1 4.0 %collective-permute-start = (f32[64,5,64]{2,1,0:T(8,128)S(1)}, f32[64,5,64]{2,1,0:T(8,128)S(1)}, u32[]{:S(2)}, u32[]{:S(2)}) collective-permute-start(f32[64,5,64]{2,1,0:T(8,128)S(1)} %copy.16), channel_id=1, source_target_pairs={{0,16},{16,32},{32,48},{48,64},{64,80},{80,96},{96,112},{112,128},... | collective-permute-start | bytes 245768 | tf_op jit(solution)/shard_map/ppermute | solution.py:199
  5.1 0.9 %convert_reduce_fusion = s32[64]{0:T(128)S(1)} fusion(s32[64]{0:T(128)} %bitcast.25), kind=kLoop, calls=%fused_computation.24 | loop fusion | flops 20416 | bytes 512 | tf_op jit(solution)/shard_map/reduce_sum | solution.py:204
  6.0 0.7 bitcast_select_fusion
  6.7 0.1 select_reduce_fusion
  6.9 1.5 %gather_fusion = f32[64,5,512]{2,0,1:T(8,128)S(1)} fusion(f32[64,5,512]{2,0,1:T(8,128)S(1)} %copy-done, s32[1024]{0:T(1024)S(1)} %pad_clamp_fusion.1), kind=kCustom, calls=%fused_computation | custom fusion | bytes 1310976 | tf_op jit(solution)/shard_map/gather | solution.py:207
  8.4 0.4 copy.15
  8.8 1.0 %reshape.105 = f32[16,80,128]{2,1,0:T(8,128)} reshape(f32[64,5,512]{2,1,0:T(8,128)S(1)} %copy.15) | data formatting | bytes 1310720 | tf_op jit(solution)/shard_map/reshape | solution.py:207
  9.8 8.1 %all-to-all-start = ((f32[16,80,128]{2,1,0:T(8,128)}), f32[16,80,128]{2,1,0:T(8,128)S(1)}, u32[]{:S(2)}, u32[]{:S(2)}) async-start(f32[16,80,128]{2,1,0:T(8,128)} %reshape.105), calls=%async_computation | async-start | bytes 1310720 | tf_op jit(solution)/shard_map/all_to_all | solution.py:208
  17.9 0.1 broadcast_in_dim.13
  17.9 0.7 broadcast_in_dim_reshape.2.src_ref
  18.6 1.8 %shard_map.73.p_ref = bf16[1024,512]{1,0:T(8,128)(2,1)} custom-call(s32[1,512]{1,0:T(1,128)} %broadcast_in_dim_reshape.2.src_ref), custom_call_target="tpu_custom_call" | custom-call | tf_op jit(solution)/shard_map/pallas_call | solution.py:93
  20.4 1.2 %collective-permute-done = f32[64,5,64]{2,1,0:T(8,128)S(1)} collective-permute-done((f32[64,5,64]{2,1,0:T(8,128)S(1)}, f32[64,5,64]{2,1,0:T(8,128)S(1)}, u32[]{:S(2)}, u32[]{:S(2)}) %collective-permute-start) | collective-permute-done | bytes 81952 | tf_op jit(solution)/shard_map/ppermute | solution.py:199
  21.7 0.6 gather_fusion.1
  22.3 0.1 copy.17
  22.5 0.4 minimum_maximum_fusion.2
  23.0 0.1 broadcast_multiply_fusion.2
  23.1 0.1 broadcast_multiply_fusion.1
  23.3 0.2 broadcast_multiply_fusion
  23.5 0.2 broadcast_add_fusion
  23.7 1.9 %add_add_fusion = f32[5,4,2,4,2,4,2,64]{7,6,5,4,3,2,1,0:T(2,128)} fusion(f32[5,4,4,4,2,64]{5,4,3,2,1,0:T(2,128)S(1)} %broadcast_multiply_fusion, f32[5,4,2,4,2,4,64]{6,5,4,3,2,1,0:T(4,128)S(1)} %broadcast_add_fusion, f32[5,4,4,4,64]{4,3,2,1,0:T(4,128)S(1)} %bitcast.22), kind=kLoop, calls=%fused_computation.2 | loop fusion | flops 327680 | bytes 1228800 | tf_op jit(solution)/shard_map/add | solution.py:39
  25.6 12.2 %all-to-all-done = f32[16,80,128]{2,1,0:T(8,128)S(1)} async-done(((f32[16,80,128]{2,1,0:T(8,128)}), f32[16,80,128]{2,1,0:T(8,128)S(1)}, u32[]{:S(2)}, u32[]{:S(2)}) %all-to-all-start) | async-done | bytes 655392 | tf_op jit(solution)/shard_map/all_to_all | solution.py:208
  37.8 0.8 %copy-done.1 = f32[16,80,128]{2,1,0:T(8,128)} copy-done((f32[16,80,128]{2,1,0:T(8,128)}, f32[16,80,128]{2,1,0:T(8,128)S(1)}, u32[]{:S(2)}) %copy-start.1) | copy-done | bytes 655384
  38.6 4.8 %shard_map.74 = (f32[5,8,32,128]{3,2,1,0:T(8,128)}, f32[5,2,32,128]{3,2,1,0:T(8,128)}, f32[5,2,32,128]{3,2,1,0:T(8,128)}, f32[5,8,2,128]{3,2,1,0:T(2,128)}, f32[5,8,2,128]{3,2,1,0:T(2,128)}) custom-call(f32[1280,128]{1,0:T(8,128)} %bitcast.23, f32[5,512,64]{2,1,0:T(8,128)} %bitcast.17, bf16[1024,512]{1,0:T(8,128)(2,1)} %shard_map.73.p_ref), custom_call_target="tpu_custom_call" | custom-call | tf_op jit(solution)/shard_map/pallas_call | solution.py:102
  43.4 4.0 %collective-permute-start.1 = (f32[5,2,32,128]{3,2,1,0:T(8,128)}, f32[5,2,32,128]{3,2,1,0:T(8,128)S(1)}, u32[]{:S(2)}, u32[]{:S(2)}) collective-permute-start(f32[5,2,32,128]{3,2,1,0:T(8,128)} %get-tuple-element.11), channel_id=1, source_target_pairs={{0,16},{16,32},{32,48},{48,64},{64,80},{80,96},{96,112},{112,128},... | collective-permute-start | bytes 491528 | tf_op jit(solution)/shard_map/ppermute | solution.py:188
  47.4 10.1 %collective-permute-start.2 = (f32[5,2,32,128]{3,2,1,0:T(8,128)}, f32[5,2,32,128]{3,2,1,0:T(8,128)S(1)}, u32[]{:S(2)}, u32[]{:S(2)}) collective-permute-start(f32[5,2,32,128]{3,2,1,0:T(8,128)} %get-tuple-element.12), channel_id=1, source_target_pairs={{16,0},{32,16},{48,32},{64,48},{80,64},{96,80},{112,96},{128,112},... | collective-permute-start | bytes 491528 | tf_op jit(solution)/shard_map/ppermute | solution.py:188
  57.6 1.9 %collective-permute-start.3 = (f32[5,8,2,128]{3,2,1,0:T(2,128)}, f32[5,8,2,128]{3,2,1,0:T(2,128)S(1)}, u32[]{:S(2)}, u32[]{:S(2)}) collective-permute-start(f32[5,8,2,128]{3,2,1,0:T(2,128)} %get-tuple-element.13), channel_id=1, source_target_pairs={{0,1},{1,2},{2,3},{3,4},{4,5},{5,6},{6,7},{7,8},{8,9},{9,10},{10,1... | collective-permute-start | bytes 122888 | tf_op jit(solution)/shard_map/ppermute | solution.py:188
  59.5 2.4 %collective-permute-start.4 = (f32[5,8,2,128]{3,2,1,0:T(2,128)}, f32[5,8,2,128]{3,2,1,0:T(2,128)S(1)}, u32[]{:S(2)}, u32[]{:S(2)}) collective-permute-start(f32[5,8,2,128]{3,2,1,0:T(2,128)} %get-tuple-element.14), channel_id=1, source_target_pairs={{1,0},{2,1},{3,2},{4,3},{5,4},{6,5},{7,6},{8,7},{9,8},{10,9},{11,1... | collective-permute-start | bytes 122888 | tf_op jit(solution)/shard_map/ppermute | solution.py:188
  61.9 3.1 %collective-permute-done.4.yh_ref = f32[5,8,2,128]{3,2,1,0:T(2,128)S(1)} collective-permute-done((f32[5,8,2,128]{3,2,1,0:T(2,128)}, f32[5,8,2,128]{3,2,1,0:T(2,128)S(1)}, u32[]{:S(2)}, u32[]{:S(2)}) %collective-permute-start.4) | collective-permute-done | bytes 40992 | tf_op jit(solution)/shard_map/ppermute | solution.py:188
  65.1 0.6 copy-done.5
  65.6 0.1 copy-done.2
  65.8 4.5 %shard_map.75 = f32[5,8,32,128]{3,2,1,0:T(8,128)} custom-call(f32[3,5]{1,0:T(4,128)} %c_ref.1, f32[5,8,32,128]{3,2,1,0:T(8,128)} %get-tuple-element.10.u_ref, f32[5,2,32,128]{3,2,1,0:T(8,128)} %copy-done.2, f32[5,2,32,128]{3,2,1,0:T(8,128)} %copy-done.3, f32[5,8,2,128]{3,2,1,0:T(2,128)} %copy-done.4, f32[5,8,2,128]{3,2,1,0:T(2,128)} %copy-done.5), custom_call_target="tpu_custom_call" | custom-call | tf_op jit(solution)/shard_map/pallas_call | solution.py:162
  (23 shorter events, 0.2 us)
Async XLA Ops:
  0.0 6.8 %copy-start = (f32[64,5,512]{2,0,1:T(8,128)S(1)}, f32[64,5,512]{2,0,1:T(8,128)}, u32[]{:S(2)}) copy-start(f32[64,5,512]{2,0,1:T(8,128)} %param.7) | copy-start | bytes 1966084
  1.1 20.6 %collective-permute-start = (f32[64,5,64]{2,1,0:T(8,128)S(1)}, f32[64,5,64]{2,1,0:T(8,128)S(1)}, u32[]{:S(2)}, u32[]{:S(2)}) collective-permute-start(f32[64,5,64]{2,1,0:T(8,128)S(1)} %copy.16), channel_id=1, source_target_pairs={{0,16},{16,32},{32,48},{48,64},{64,80},{80,96},{96,112},{112,128},... | collective-permute-start | bytes 245768 | tf_op jit(solution)/shard_map/ppermute | solution.py:199
  8.8 9.0 %copy-start.7 = (s32[1,1,64]{2,1,0:T(1,128)S(1)}, s32[1,1,64]{2,1,0:T(1,128)}, u32[]{:S(2)}) copy-start(s32[1,1,64]{2,1,0:T(1,128)} %param.11) | copy-start | bytes 772
  9.8 28.0 %all-to-all-start = ((f32[16,80,128]{2,1,0:T(8,128)}), f32[16,80,128]{2,1,0:T(8,128)S(1)}, u32[]{:S(2)}, u32[]{:S(2)}) async-start(f32[16,80,128]{2,1,0:T(8,128)} %reshape.105), calls=%async_computation | async-start | bytes 1310720 | tf_op jit(solution)/shard_map/all_to_all | solution.py:208
  20.4 2.6 %copy-start.6 = (f32[2]{0:T(128)S(1)}, f32[2]{0:T(128)}, u32[]{:S(2)}) copy-start(f32[2]{0:T(128)} %constant.33.clone) | copy-start | bytes 28
  37.8 0.8 %copy-start.1 = (f32[16,80,128]{2,1,0:T(8,128)}, f32[16,80,128]{2,1,0:T(8,128)S(1)}, u32[]{:S(2)}) copy-start(f32[16,80,128]{2,1,0:T(8,128)S(1)} %all-to-all-done) | copy-start | bytes 1966084
  43.4 21.6 %collective-permute-start.1 = (f32[5,2,32,128]{3,2,1,0:T(8,128)}, f32[5,2,32,128]{3,2,1,0:T(8,128)S(1)}, u32[]{:S(2)}, u32[]{:S(2)}) collective-permute-start(f32[5,2,32,128]{3,2,1,0:T(8,128)} %get-tuple-element.11), channel_id=1, source_target_pairs={{0,16},{16,32},{32,48},{48,64},{64,80},{80,96},{96,112},{112,128},... | collective-permute-start | bytes 491528 | tf_op jit(solution)/shard_map/ppermute | solution.py:188
  47.4 17.6 %collective-permute-start.2 = (f32[5,2,32,128]{3,2,1,0:T(8,128)}, f32[5,2,32,128]{3,2,1,0:T(8,128)S(1)}, u32[]{:S(2)}, u32[]{:S(2)}) collective-permute-start(f32[5,2,32,128]{3,2,1,0:T(8,128)} %get-tuple-element.12), channel_id=1, source_target_pairs={{16,0},{32,16},{48,32},{64,48},{80,64},{96,80},{112,96},{128,112},... | collective-permute-start | bytes 491528 | tf_op jit(solution)/shard_map/ppermute | solution.py:188
  57.6 4.3 %collective-permute-start.3 = (f32[5,8,2,128]{3,2,1,0:T(2,128)}, f32[5,8,2,128]{3,2,1,0:T(2,128)S(1)}, u32[]{:S(2)}, u32[]{:S(2)}) collective-permute-start(f32[5,8,2,128]{3,2,1,0:T(2,128)} %get-tuple-element.13), channel_id=1, source_target_pairs={{0,1},{1,2},{2,3},{3,4},{4,5},{5,6},{6,7},{7,8},{8,9},{9,10},{10,1... | collective-permute-start | bytes 122888 | tf_op jit(solution)/shard_map/ppermute | solution.py:188
  59.5 5.5 %collective-permute-start.4 = (f32[5,8,2,128]{3,2,1,0:T(2,128)}, f32[5,8,2,128]{3,2,1,0:T(2,128)S(1)}, u32[]{:S(2)}, u32[]{:S(2)}) collective-permute-start(f32[5,8,2,128]{3,2,1,0:T(2,128)} %get-tuple-element.14), channel_id=1, source_target_pairs={{1,0},{2,1},{3,2},{4,3},{5,4},{6,5},{7,6},{8,7},{9,8},{10,9},{11,1... | collective-permute-start | bytes 122888 | tf_op jit(solution)/shard_map/ppermute | solution.py:188
  61.9 3.1 %copy-start.4 = (f32[5,8,2,128]{3,2,1,0:T(2,128)}, f32[5,8,2,128]{3,2,1,0:T(2,128)S(1)}, u32[]{:S(2)}) copy-start(f32[5,8,2,128]{3,2,1,0:T(2,128)S(1)} %collective-permute-done.3.yl_ref) | copy-start | bytes 122884
  65.0 0.6 copy-start.5
  65.0 0.7 copy-start.2
  65.0 0.7 %copy-start.3 = (f32[5,2,32,128]{3,2,1,0:T(8,128)}, f32[5,2,32,128]{3,2,1,0:T(8,128)S(1)}, u32[]{:S(2)}) copy-start(f32[5,2,32,128]{3,2,1,0:T(8,128)S(1)} %collective-permute-done.2.zh_ref) | copy-start | bytes 491524

commit v9 on v8

--- a/solution.py
+++ b/solution.py
@@ -122,61 +122,53 @@
 
 
 def advance_kernel(c_ref, u_ref, zl_ref, zh_ref, yl_ref, yh_ref, o_ref, yp_ref, g_ref):
-    f = pl.program_id(0)
-    zn, yn, xn = u_ref.shape[1:]
-    cz = c_ref[0, f]
-    cy = c_ref[1, f]
-    cx = c_ref[2, f]
-    yp_ref[:, E - 2:E, :] = yl_ref[0]
-    yp_ref[:, E:E + yn, :] = u_ref[0]
-    yp_ref[:, E + yn:E + yn + 2, :] = yh_ref[0]
+    fields, zn, yn, xn = u_ref.shape
     span = g_ref.shape[0]
     lane = lax.broadcasted_iota(jnp.int32, (yn, xn), 1)
-
-    def plane(j):
-        if j < 2:
-            return zl_ref[0, j]
-        if j < zn + 2:
-            return u_ref[0, j - 2]
-        return zh_ref[0, j - zn - 2]
-
-    g_prev = face(plane(0), plane(1), plane(2))
-    for z in range(zn):
-        u = plane(z + 2)
-        g_next = face(plane(z + 1), u, plane(z + 3))
-        tz = cz * (g_next - g_prev)
-        g_prev = g_next
-        g_ref[...] = face(yp_ref[z, E - 2:E - 2 + span, :], yp_ref[z, E - 1:E - 1 + span, :],
-                          yp_ref[z, E:E + span, :])
-        ty = cy * (g_ref[1:yn + 1, :] - g_ref[0:yn, :])
-        lower1 = jnp.where(lane >= 1, pltpu.roll(u, 1, 1), 0.0)
-        upper1 = jnp.where(lane < xn - 1, pltpu.roll(u, xn - 1, 1), 0.0)
-        gx = face(lower1, u, upper1)
-        gx_lo = jnp.where(lane >= 1, pltpu.roll(gx, 1, 1), 0.0)
-        tx = cx * (gx - gx_lo)
-        o_ref[0, z] = u - ((tz + ty) + tx)
+    for f in range(fields):
+        cz = c_ref[0, f]
+        cy = c_ref[1, f]
+        cx = c_ref[2, f]
+        yp_ref[:, E - 2:E, :] = yl_ref[f]
+        yp_ref[:, E:E + yn, :] = u_ref[f]
+        yp_ref[:, E + yn:E + yn + 2, :] = yh_ref[f]
+
+        def plane(j):
+            if j < 2:
+                return zl_ref[f, j]
+            if j < zn + 2:
+                return u_ref[f, j - 2]
+            return zh_ref[f, j - zn - 2]
+
+        g_prev = face(plane(0), plane(1), plane(2))
+        for z in range(zn):
+            u = plane(z + 2)
+            g_next = face(plane(z + 1), u, plane(z + 3))
+            tz = cz * (g_next - g_prev)
+            g_prev = g_next
+            g_ref[...] = face(yp_ref[z, E - 2:E - 2 + span, :], yp_ref[z, E - 1:E - 1 + span, :],
+                              yp_ref[z, E:E + span, :])
+            ty = cy * (g_ref[1:yn + 1, :] - g_ref[0:yn, :])
+            lower1 = jnp.where(lane >= 1, pltpu.roll(u, 1, 1), 0.0)
+            upper1 = jnp.where(lane < xn - 1, pltpu.roll(u, xn - 1, 1), 0.0)
+            gx = face(lower1, u, upper1)
+            gx_lo = jnp.where(lane >= 1, pltpu.roll(gx, 1, 1), 0.0)
+            tx = cx * (gx - gx_lo)
+            o_ref[f, z] = u - ((tz + ty) + tx)
 
 
 def advance(courant, region, zlo, zhi, ylo, yhi):
-    fields, zn, yn, xn = region.shape
+    _, zn, yn, xn = region.shape
+    vmem = pl.BlockSpec(memory_space=pltpu.VMEM)
     return pl.pallas_call(
         advance_kernel,
-        grid=(fields,),
-        in_specs=[
-            pl.BlockSpec(memory_space=pltpu.SMEM),
-            pl.BlockSpec((1, zn, yn, xn), lambda f: (f, 0, 0, 0)),
-            pl.BlockSpec((1, 2, yn, xn), lambda f: (f, 0, 0, 0)),
-            pl.BlockSpec((1, 2, yn, xn), lambda f: (f, 0, 0, 0)),
-            pl.BlockSpec((1, zn, 2, xn), lambda f: (f, 0, 0, 0)),
-            pl.BlockSpec((1, zn, 2, xn), lambda f: (f, 0, 0, 0)),
-        ],
-        out_specs=pl.BlockSpec((1, zn, yn, xn), lambda f: (f, 0, 0, 0)),
+        in_specs=[pl.BlockSpec(memory_space=pltpu.SMEM), vmem, vmem, vmem, vmem, vmem],
+        out_specs=vmem,
         out_shape=jax.ShapeDtypeStruct(region.shape, jnp.float32),
         scratch_shapes=[
             pltpu.VMEM((zn, yn + 2 * E, xn), jnp.float32),
             pltpu.VMEM((yn + E, xn), jnp.float32),
         ],
-        compiler_params=pltpu.CompilerParams(dimension_semantics=("arbitrary",)),
         interpret=INTERPRET,
     )(courant, region, zlo, zhi, ylo, yhi)
 

time: 70.7 us -> 70.9 us (level)
  no operation moved by 1% of the time
where the time goes in v9:
time: 70.9 us; the launch traced here: 70.5 us
  starting transfers between devices  30.5 us (43%)
  waiting for transfers between devices  16.5 us (23%)
  Pallas kernels  11.4 us (16%)
  local copies, waits for them, and re-layouts  7.14 us (10%)
  other arithmetic  4.76 us (7%)
    ppermute x2, starting transfers between devices, exchange(): lax.ppermute(bottom, axis, backward)  12.5 us
    all_to_all x1, waiting for transfers between devices, local(): lax.all_to_all(outgoing, 'tile', split_axis=0, concat_axis=0, tiled=True)  12.2 us
    all_to_all x1, starting transfers between devices, local(): lax.all_to_all(outgoing, 'tile', split_axis=0, concat_axis=0, tiled=True)  8.07 us
    ppermute x2, starting transfers between devices, exchange(): lax.ppermute(top, axis, forward)  5.91 us
    pallas_call x1, Pallas kernels, assemble(): pl.pallas_call(assemble_kernel, out_shape=[jax.ShapeDtypeStruct((fields,...  4.8 us
    pallas_call x1, Pallas kernels, advance(): pl.pallas_call(advance_kernel, in_specs=[pl.BlockSpec(memory_space=pltpu....  4.75 us
    ppermute x1, starting transfers between devices, local(): lax.ppermute(coarse_fine, 'slab', [(i, (i + 1) % slabs) for i in range(sl...  4 us
    ppermute x2, waiting for transfers between devices, exchange(): lax.ppermute(bottom, axis, backward)  3.1 us
  transfers between devices with their start and end apart: 6, of which 3 were waited for; matrix products, arithmetic and copies ran while one was open for 13% of the time, Pallas kernels for 3%

profile of v9, /device:TPU:7, one launch (start us, length us, event | category | flops | bytes accessed | tf_op | source)
XLA Modules:
  0.0 70.5 jit_solution(7507396254888478552)
XLA Ops:
  0.0 1.1 %copy.16 = f32[64,5,64]{2,1,0:T(8,128)S(1)} copy(f32[64,5,64]{2,0,1:T(8,128)} %param.8) | data formatting | bytes 163840 | tf_op args[1]
  1.1 4.0 %collective-permute-start = (f32[64,5,64]{2,1,0:T(8,128)S(1)}, f32[64,5,64]{2,1,0:T(8,128)S(1)}, u32[]{:S(2)}, u32[]{:S(2)}) collective-permute-start(f32[64,5,64]{2,1,0:T(8,128)S(1)} %copy.16), channel_id=1, source_target_pairs={{0,16},{16,32},{32,48},{48,64},{64,80},{80,96},{96,112},{112,128},... | collective-permute-start | bytes 245768 | tf_op jit(solution)/shard_map/ppermute | solution.py:191
  5.1 0.9 %convert_reduce_fusion = s32[64]{0:T(128)S(1)} fusion(s32[64]{0:T(128)} %bitcast.25), kind=kLoop, calls=%fused_computation.24 | loop fusion | flops 20416 | bytes 512 | tf_op jit(solution)/shard_map/reduce_sum | solution.py:196
  6.0 0.7 bitcast_select_fusion
  6.7 0.1 select_reduce_fusion
  6.9 1.5 %gather_fusion = f32[64,5,512]{2,0,1:T(8,128)S(1)} fusion(f32[64,5,512]{2,0,1:T(8,128)S(1)} %copy-done, s32[1024]{0:T(1024)S(1)} %pad_clamp_fusion.1), kind=kCustom, calls=%fused_computation | custom fusion | bytes 1310976 | tf_op jit(solution)/shard_map/gather | solution.py:199
  8.4 0.4 copy.15
  8.8 1.0 %reshape.105 = f32[16,80,128]{2,1,0:T(8,128)} reshape(f32[64,5,512]{2,1,0:T(8,128)S(1)} %copy.15) | data formatting | bytes 1310720 | tf_op jit(solution)/shard_map/reshape | solution.py:199
  9.8 8.1 %all-to-all-start = ((f32[16,80,128]{2,1,0:T(8,128)}), f32[16,80,128]{2,1,0:T(8,128)S(1)}, u32[]{:S(2)}, u32[]{:S(2)}) async-start(f32[16,80,128]{2,1,0:T(8,128)} %reshape.105), calls=%async_computation | async-start | bytes 1310720 | tf_op jit(solution)/shard_map/all_to_all | solution.py:200
  17.9 0.1 broadcast_in_dim.13
  17.9 0.7 broadcast_in_dim_reshape.2.src_ref
  18.6 1.8 %shard_map.73.p_ref = bf16[1024,512]{1,0:T(8,128)(2,1)} custom-call(s32[1,512]{1,0:T(1,128)} %broadcast_in_dim_reshape.2.src_ref), custom_call_target="tpu_custom_call" | custom-call | tf_op jit(solution)/shard_map/pallas_call | solution.py:93
  20.4 1.2 %collective-permute-done = f32[64,5,64]{2,1,0:T(8,128)S(1)} collective-permute-done((f32[64,5,64]{2,1,0:T(8,128)S(1)}, f32[64,5,64]{2,1,0:T(8,128)S(1)}, u32[]{:S(2)}, u32[]{:S(2)}) %collective-permute-start) | collective-permute-done | bytes 81952 | tf_op jit(solution)/shard_map/ppermute | solution.py:191
  21.7 0.6 gather_fusion.1
  22.3 0.1 copy.17
  22.5 0.4 minimum_maximum_fusion.2
  23.0 0.1 broadcast_multiply_fusion.2
  23.1 0.1 broadcast_multiply_fusion.1
  23.3 0.2 broadcast_multiply_fusion
  23.5 0.2 broadcast_add_fusion
  23.7 1.9 %add_add_fusion = f32[5,4,2,4,2,4,2,64]{7,6,5,4,3,2,1,0:T(2,128)} fusion(f32[5,4,4,4,2,64]{5,4,3,2,1,0:T(2,128)S(1)} %broadcast_multiply_fusion, f32[5,4,2,4,2,4,64]{6,5,4,3,2,1,0:T(4,128)S(1)} %broadcast_add_fusion, f32[5,4,4,4,64]{4,3,2,1,0:T(4,128)S(1)} %bitcast.22), kind=kLoop, calls=%fused_computation.2 | loop fusion | flops 327680 | bytes 1228800 | tf_op jit(solution)/shard_map/add | solution.py:39
  25.6 12.2 %all-to-all-done = f32[16,80,128]{2,1,0:T(8,128)S(1)} async-done(((f32[16,80,128]{2,1,0:T(8,128)}), f32[16,80,128]{2,1,0:T(8,128)S(1)}, u32[]{:S(2)}, u32[]{:S(2)}) %all-to-all-start) | async-done | bytes 655392 | tf_op jit(solution)/shard_map/all_to_all | solution.py:200
  37.8 0.8 %copy-done.1 = f32[16,80,128]{2,1,0:T(8,128)} copy-done((f32[16,80,128]{2,1,0:T(8,128)}, f32[16,80,128]{2,1,0:T(8,128)S(1)}, u32[]{:S(2)}) %copy-start.1) | copy-done | bytes 655384
  38.6 4.8 %shard_map.74 = (f32[5,8,32,128]{3,2,1,0:T(8,128)}, f32[5,2,32,128]{3,2,1,0:T(8,128)}, f32[5,2,32,128]{3,2,1,0:T(8,128)}, f32[5,8,2,128]{3,2,1,0:T(2,128)}, f32[5,8,2,128]{3,2,1,0:T(2,128)}) custom-call(f32[1280,128]{1,0:T(8,128)} %bitcast.23, f32[5,512,64]{2,1,0:T(8,128)} %bitcast.17, bf16[1024,512]{1,0:T(8,128)(2,1)} %shard_map.73.p_ref), custom_call_target="tpu_custom_call" | custom-call | tf_op jit(solution)/shard_map/pallas_call | solution.py:102
  43.4 4.0 %collective-permute-start.1 = (f32[5,2,32,128]{3,2,1,0:T(8,128)}, f32[5,2,32,128]{3,2,1,0:T(8,128)S(1)}, u32[]{:S(2)}, u32[]{:S(2)}) collective-permute-start(f32[5,2,32,128]{3,2,1,0:T(8,128)} %get-tuple-element.11), channel_id=1, source_target_pairs={{0,16},{16,32},{32,48},{48,64},{64,80},{80,96},{96,112},{112,128},... | collective-permute-start | bytes 491528 | tf_op jit(solution)/shard_map/ppermute | solution.py:180
  47.4 10.1 %collective-permute-start.2 = (f32[5,2,32,128]{3,2,1,0:T(8,128)}, f32[5,2,32,128]{3,2,1,0:T(8,128)S(1)}, u32[]{:S(2)}, u32[]{:S(2)}) collective-permute-start(f32[5,2,32,128]{3,2,1,0:T(8,128)} %get-tuple-element.12), channel_id=1, source_target_pairs={{16,0},{32,16},{48,32},{64,48},{80,64},{96,80},{112,96},{128,112},... | collective-permute-start | bytes 491528 | tf_op jit(solution)/shard_map/ppermute | solution.py:180
  57.6 1.9 %collective-permute-start.3 = (f32[5,8,2,128]{3,2,1,0:T(2,128)}, f32[5,8,2,128]{3,2,1,0:T(2,128)S(1)}, u32[]{:S(2)}, u32[]{:S(2)}) collective-permute-start(f32[5,8,2,128]{3,2,1,0:T(2,128)} %get-tuple-element.13), channel_id=1, source_target_pairs={{0,1},{1,2},{2,3},{3,4},{4,5},{5,6},{6,7},{7,8},{8,9},{9,10},{10,1... | collective-permute-start | bytes 122888 | tf_op jit(solution)/shard_map/ppermute | solution.py:180
  59.5 2.4 %collective-permute-start.4 = (f32[5,8,2,128]{3,2,1,0:T(2,128)}, f32[5,8,2,128]{3,2,1,0:T(2,128)S(1)}, u32[]{:S(2)}, u32[]{:S(2)}) collective-permute-start(f32[5,8,2,128]{3,2,1,0:T(2,128)} %get-tuple-element.14), channel_id=1, source_target_pairs={{1,0},{2,1},{3,2},{4,3},{5,4},{6,5},{7,6},{8,7},{9,8},{10,9},{11,1... | collective-permute-start | bytes 122888 | tf_op jit(solution)/shard_map/ppermute | solution.py:180
  61.9 3.1 %collective-permute-done.4.yh_ref = f32[5,8,2,128]{3,2,1,0:T(2,128)S(1)} collective-permute-done((f32[5,8,2,128]{3,2,1,0:T(2,128)}, f32[5,8,2,128]{3,2,1,0:T(2,128)S(1)}, u32[]{:S(2)}, u32[]{:S(2)}) %collective-permute-start.4) | collective-permute-done | bytes 40992 | tf_op jit(solution)/shard_map/ppermute | solution.py:180
  65.1 0.6 copy-done.5
  65.6 0.1 copy-done.2
  65.8 4.8 %shard_map.75 = f32[5,8,32,128]{3,2,1,0:T(8,128)} custom-call(f32[3,5]{1,0:T(4,128)} %c_ref.1, f32[5,8,32,128]{3,2,1,0:T(8,128)} %get-tuple-element.10.u_ref, f32[5,2,32,128]{3,2,1,0:T(8,128)} %copy-done.2, f32[5,2,32,128]{3,2,1,0:T(8,128)} %copy-done.3, f32[5,8,2,128]{3,2,1,0:T(2,128)} %copy-done.4, f32[5,8,2,128]{3,2,1,0:T(2,128)} %copy-done.5), custom_call_target="tpu_custom_call" | custom-call | tf_op jit(solution)/shard_map/pallas_call | solution.py:163
  (23 shorter events, 0.2 us)
Async XLA Ops:
  0.0 6.8 %copy-start = (f32[64,5,512]{2,0,1:T(8,128)S(1)}, f32[64,5,512]{2,0,1:T(8,128)}, u32[]{:S(2)}) copy-start(f32[64,5,512]{2,0,1:T(8,128)} %param.7) | copy-start | bytes 1966084
  1.1 20.6 %collective-permute-start = (f32[64,5,64]{2,1,0:T(8,128)S(1)}, f32[64,5,64]{2,1,0:T(8,128)S(1)}, u32[]{:S(2)}, u32[]{:S(2)}) collective-permute-start(f32[64,5,64]{2,1,0:T(8,128)S(1)} %copy.16), channel_id=1, source_target_pairs={{0,16},{16,32},{32,48},{48,64},{64,80},{80,96},{96,112},{112,128},... | collective-permute-start | bytes 245768 | tf_op jit(solution)/shard_map/ppermute | solution.py:191
  8.8 9.0 %copy-start.7 = (s32[1,1,64]{2,1,0:T(1,128)S(1)}, s32[1,1,64]{2,1,0:T(1,128)}, u32[]{:S(2)}) copy-start(s32[1,1,64]{2,1,0:T(1,128)} %param.11) | copy-start | bytes 772
  9.8 28.0 %all-to-all-start = ((f32[16,80,128]{2,1,0:T(8,128)}), f32[16,80,128]{2,1,0:T(8,128)S(1)}, u32[]{:S(2)}, u32[]{:S(2)}) async-start(f32[16,80,128]{2,1,0:T(8,128)} %reshape.105), calls=%async_computation | async-start | bytes 1310720 | tf_op jit(solution)/shard_map/all_to_all | solution.py:200
  20.4 2.6 %copy-start.6 = (f32[2]{0:T(128)S(1)}, f32[2]{0:T(128)}, u32[]{:S(2)}) copy-start(f32[2]{0:T(128)} %constant.33.clone) | copy-start | bytes 28
  37.8 0.8 %copy-start.1 = (f32[16,80,128]{2,1,0:T(8,128)}, f32[16,80,128]{2,1,0:T(8,128)S(1)}, u32[]{:S(2)}) copy-start(f32[16,80,128]{2,1,0:T(8,128)S(1)} %all-to-all-done) | copy-start | bytes 1966084
  43.4 21.6 %collective-permute-start.1 = (f32[5,2,32,128]{3,2,1,0:T(8,128)}, f32[5,2,32,128]{3,2,1,0:T(8,128)S(1)}, u32[]{:S(2)}, u32[]{:S(2)}) collective-permute-start(f32[5,2,32,128]{3,2,1,0:T(8,128)} %get-tuple-element.11), channel_id=1, source_target_pairs={{0,16},{16,32},{32,48},{48,64},{64,80},{80,96},{96,112},{112,128},... | collective-permute-start | bytes 491528 | tf_op jit(solution)/shard_map/ppermute | solution.py:180
  47.4 17.6 %collective-permute-start.2 = (f32[5,2,32,128]{3,2,1,0:T(8,128)}, f32[5,2,32,128]{3,2,1,0:T(8,128)S(1)}, u32[]{:S(2)}, u32[]{:S(2)}) collective-permute-start(f32[5,2,32,128]{3,2,1,0:T(8,128)} %get-tuple-element.12), channel_id=1, source_target_pairs={{16,0},{32,16},{48,32},{64,48},{80,64},{96,80},{112,96},{128,112},... | collective-permute-start | bytes 491528 | tf_op jit(solution)/shard_map/ppermute | solution.py:180
  57.6 4.3 %collective-permute-start.3 = (f32[5,8,2,128]{3,2,1,0:T(2,128)}, f32[5,8,2,128]{3,2,1,0:T(2,128)S(1)}, u32[]{:S(2)}, u32[]{:S(2)}) collective-permute-start(f32[5,8,2,128]{3,2,1,0:T(2,128)} %get-tuple-element.13), channel_id=1, source_target_pairs={{0,1},{1,2},{2,3},{3,4},{4,5},{5,6},{6,7},{7,8},{8,9},{9,10},{10,1... | collective-permute-start | bytes 122888 | tf_op jit(solution)/shard_map/ppermute | solution.py:180
  59.5 5.5 %collective-permute-start.4 = (f32[5,8,2,128]{3,2,1,0:T(2,128)}, f32[5,8,2,128]{3,2,1,0:T(2,128)S(1)}, u32[]{:S(2)}, u32[]{:S(2)}) collective-permute-start(f32[5,8,2,128]{3,2,1,0:T(2,128)} %get-tuple-element.14), channel_id=1, source_target_pairs={{1,0},{2,1},{3,2},{4,3},{5,4},{6,5},{7,6},{8,7},{9,8},{10,9},{11,1... | collective-permute-start | bytes 122888 | tf_op jit(solution)/shard_map/ppermute | solution.py:180
  61.9 3.1 %copy-start.4 = (f32[5,8,2,128]{3,2,1,0:T(2,128)}, f32[5,8,2,128]{3,2,1,0:T(2,128)S(1)}, u32[]{:S(2)}) copy-start(f32[5,8,2,128]{3,2,1,0:T(2,128)S(1)} %collective-permute-done.3.yl_ref) | copy-start | bytes 122884
  65.0 0.6 copy-start.5
  65.0 0.7 copy-start.2
  65.0 0.7 %copy-start.3 = (f32[5,2,32,128]{3,2,1,0:T(8,128)}, f32[5,2,32,128]{3,2,1,0:T(8,128)S(1)}, u32[]{:S(2)}) copy-start(f32[5,2,32,128]{3,2,1,0:T(8,128)S(1)} %collective-permute-done.2.zh_ref) | copy-start | bytes 491524

commit v10 on v9

--- a/solution.py
+++ b/solution.py
@@ -121,17 +121,14 @@
     return cell + 0.5 * kernel_minmod(cell - below, above - cell)
 
 
-def advance_kernel(c_ref, u_ref, zl_ref, zh_ref, yl_ref, yh_ref, o_ref, yp_ref, g_ref):
+def advance_kernel(c_ref, u_ref, zl_ref, zh_ref, yl_ref, yh_ref, o_ref):
     fields, zn, yn, xn = u_ref.shape
-    span = g_ref.shape[0]
     lane = lax.broadcasted_iota(jnp.int32, (yn, xn), 1)
+    row = lax.broadcasted_iota(jnp.int32, (yn, xn), 0)
     for f in range(fields):
         cz = c_ref[0, f]
         cy = c_ref[1, f]
         cx = c_ref[2, f]
-        yp_ref[:, E - 2:E, :] = yl_ref[f]
-        yp_ref[:, E:E + yn, :] = u_ref[f]
-        yp_ref[:, E + yn:E + yn + 2, :] = yh_ref[f]
 
         def plane(j):
             if j < 2:
@@ -146,9 +143,14 @@
             g_next = face(plane(z + 1), u, plane(z + 3))
             tz = cz * (g_next - g_prev)
             g_prev = g_next
-            g_ref[...] = face(yp_ref[z, E - 2:E - 2 + span, :], yp_ref[z, E - 1:E - 1 + span, :],
-                              yp_ref[z, E:E + span, :])
-            ty = cy * (g_ref[1:yn + 1, :] - g_ref[0:yn, :])
+            ylo = yl_ref[f, z]
+            yhi = yh_ref[f, z]
+            below = jnp.where(row == 0, ylo[1:2], pltpu.roll(u, 1, 0))
+            above = jnp.where(row == yn - 1, yhi[0:1], pltpu.roll(u, yn - 1, 0))
+            gy = face(below, u, above)
+            gy_first = face(ylo[0:1], ylo[1:2], u[0:1])
+            gy_lo = jnp.where(row == 0, gy_first, pltpu.roll(gy, 1, 0))
+            ty = cy * (gy - gy_lo)
             lower1 = jnp.where(lane >= 1, pltpu.roll(u, 1, 1), 0.0)
             upper1 = jnp.where(lane < xn - 1, pltpu.roll(u, xn - 1, 1), 0.0)
             gx = face(lower1, u, upper1)
@@ -158,17 +160,12 @@
 
 
 def advance(courant, region, zlo, zhi, ylo, yhi):
-    _, zn, yn, xn = region.shape
     vmem = pl.BlockSpec(memory_space=pltpu.VMEM)
     return pl.pallas_call(
         advance_kernel,
         in_specs=[pl.BlockSpec(memory_space=pltpu.SMEM), vmem, vmem, vmem, vmem, vmem],
         out_specs=vmem,
         out_shape=jax.ShapeDtypeStruct(region.shape, jnp.float32),
-        scratch_shapes=[
-            pltpu.VMEM((zn, yn + 2 * E, xn), jnp.float32),
-            pltpu.VMEM((yn + E, xn), jnp.float32),
-        ],
         interpret=INTERPRET,
     )(courant, region, zlo, zhi, ylo, yhi)
 

time: 70.9 us -> 70.9 us (level)
  no operation moved by 1% of the time
where the time goes in v10:
time: 70.9 us; the launch traced here: 70.4 us
  starting transfers between devices  30.5 us (43%)
  waiting for transfers between devices  16.5 us (23%)
  Pallas kernels  11.3 us (16%)
  local copies, waits for them, and re-layouts  7.14 us (10%)
  other arithmetic  4.76 us (7%)
    ppermute x2, starting transfers between devices, exchange(): lax.ppermute(bottom, axis, backward)  12.5 us
    all_to_all x1, waiting for transfers between devices, local(): lax.all_to_all(outgoing, 'tile', split_axis=0, concat_axis=0, tiled=True)  12.2 us
    all_to_all x1, starting transfers between devices, local(): lax.all_to_all(outgoing, 'tile', split_axis=0, concat_axis=0, tiled=True)  8.07 us
    ppermute x2, starting transfers between devices, exchange(): lax.ppermute(top, axis, forward)  5.91 us
    pallas_call x1, Pallas kernels, assemble(): pl.pallas_call(assemble_kernel, out_shape=[jax.ShapeDtypeStruct((fields,...  4.8 us
    pallas_call x1, Pallas kernels, advance(): pl.pallas_call(advance_kernel, in_specs=[pl.BlockSpec(memory_space=pltpu....  4.69 us
    ppermute x1, starting transfers between devices, local(): lax.ppermute(coarse_fine, 'slab', [(i, (i + 1) % slabs) for i in range(sl...  4 us
    ppermute x2, waiting for transfers between devices, exchange(): lax.ppermute(bottom, axis, backward)  3.1 us
  transfers between devices with their start and end apart: 6, of which 3 were waited for; matrix products, arithmetic and copies ran while one was open for 13% of the time, Pallas kernels for 3%

profile of v10, /device:TPU:7, one launch (start us, length us, event | category | flops | bytes accessed | tf_op | source)
XLA Modules:
  0.0 70.4 jit_solution(2912672914348085702)
XLA Ops:
  0.0 1.1 %copy.16 = f32[64,5,64]{2,1,0:T(8,128)S(1)} copy(f32[64,5,64]{2,0,1:T(8,128)} %param.8) | data formatting | bytes 163840 | tf_op args[1]
  1.1 4.0 %collective-permute-start = (f32[64,5,64]{2,1,0:T(8,128)S(1)}, f32[64,5,64]{2,1,0:T(8,128)S(1)}, u32[]{:S(2)}, u32[]{:S(2)}) collective-permute-start(f32[64,5,64]{2,1,0:T(8,128)S(1)} %copy.16), channel_id=1, source_target_pairs={{0,16},{16,32},{32,48},{48,64},{64,80},{80,96},{96,112},{112,128},... | collective-permute-start | bytes 245768 | tf_op jit(solution)/shard_map/ppermute | solution.py:188
  5.1 0.9 %convert_reduce_fusion = s32[64]{0:T(128)S(1)} fusion(s32[64]{0:T(128)} %bitcast.25), kind=kLoop, calls=%fused_computation.24 | loop fusion | flops 20416 | bytes 512 | tf_op jit(solution)/shard_map/reduce_sum | solution.py:193
  6.0 0.7 bitcast_select_fusion
  6.7 0.1 select_reduce_fusion
  6.9 1.5 %gather_fusion = f32[64,5,512]{2,0,1:T(8,128)S(1)} fusion(f32[64,5,512]{2,0,1:T(8,128)S(1)} %copy-done, s32[1024]{0:T(1024)S(1)} %pad_clamp_fusion.1), kind=kCustom, calls=%fused_computation | custom fusion | bytes 1310976 | tf_op jit(solution)/shard_map/gather | solution.py:196
  8.4 0.4 copy.15
  8.8 1.0 %reshape.105 = f32[16,80,128]{2,1,0:T(8,128)} reshape(f32[64,5,512]{2,1,0:T(8,128)S(1)} %copy.15) | data formatting | bytes 1310720 | tf_op jit(solution)/shard_map/reshape | solution.py:196
  9.8 8.1 %all-to-all-start = ((f32[16,80,128]{2,1,0:T(8,128)}), f32[16,80,128]{2,1,0:T(8,128)S(1)}, u32[]{:S(2)}, u32[]{:S(2)}) async-start(f32[16,80,128]{2,1,0:T(8,128)} %reshape.105), calls=%async_computation | async-start | bytes 1310720 | tf_op jit(solution)/shard_map/all_to_all | solution.py:197
  17.9 0.1 broadcast_in_dim.13
  17.9 0.7 broadcast_in_dim_reshape.2.src_ref
  18.6 1.8 %shard_map.73.p_ref = bf16[1024,512]{1,0:T(8,128)(2,1)} custom-call(s32[1,512]{1,0:T(1,128)} %broadcast_in_dim_reshape.2.src_ref), custom_call_target="tpu_custom_call" | custom-call | tf_op jit(solution)/shard_map/pallas_call | solution.py:93
  20.4 1.2 %collective-permute-done = f32[64,5,64]{2,1,0:T(8,128)S(1)} collective-permute-done((f32[64,5,64]{2,1,0:T(8,128)S(1)}, f32[64,5,64]{2,1,0:T(8,128)S(1)}, u32[]{:S(2)}, u32[]{:S(2)}) %collective-permute-start) | collective-permute-done | bytes 81952 | tf_op jit(solution)/shard_map/ppermute | solution.py:188
  21.7 0.6 gather_fusion.1
  22.3 0.1 copy.17
  22.5 0.4 minimum_maximum_fusion.2
  23.0 0.1 broadcast_multiply_fusion.2
  23.1 0.1 broadcast_multiply_fusion.1
  23.3 0.2 broadcast_multiply_fusion
  23.5 0.2 broadcast_add_fusion
  23.7 1.9 %add_add_fusion = f32[5,4,2,4,2,4,2,64]{7,6,5,4,3,2,1,0:T(2,128)} fusion(f32[5,4,4,4,2,64]{5,4,3,2,1,0:T(2,128)S(1)} %broadcast_multiply_fusion, f32[5,4,2,4,2,4,64]{6,5,4,3,2,1,0:T(4,128)S(1)} %broadcast_add_fusion, f32[5,4,4,4,64]{4,3,2,1,0:T(4,128)S(1)} %bitcast.22), kind=kLoop, calls=%fused_computation.2 | loop fusion | flops 327680 | bytes 1228800 | tf_op jit(solution)/shard_map/add | solution.py:39
  25.6 12.2 %all-to-all-done = f32[16,80,128]{2,1,0:T(8,128)S(1)} async-done(((f32[16,80,128]{2,1,0:T(8,128)}), f32[16,80,128]{2,1,0:T(8,128)S(1)}, u32[]{:S(2)}, u32[]{:S(2)}) %all-to-all-start) | async-done | bytes 655392 | tf_op jit(solution)/shard_map/all_to_all | solution.py:197
  37.8 0.8 %copy-done.1 = f32[16,80,128]{2,1,0:T(8,128)} copy-done((f32[16,80,128]{2,1,0:T(8,128)}, f32[16,80,128]{2,1,0:T(8,128)S(1)}, u32[]{:S(2)}) %copy-start.1) | copy-done | bytes 655384
  38.6 4.8 %shard_map.74 = (f32[5,8,32,128]{3,2,1,0:T(8,128)}, f32[5,2,32,128]{3,2,1,0:T(8,128)}, f32[5,2,32,128]{3,2,1,0:T(8,128)}, f32[5,8,2,128]{3,2,1,0:T(2,128)}, f32[5,8,2,128]{3,2,1,0:T(2,128)}) custom-call(f32[1280,128]{1,0:T(8,128)} %bitcast.23, f32[5,512,64]{2,1,0:T(8,128)} %bitcast.17, bf16[1024,512]{1,0:T(8,128)(2,1)} %shard_map.73.p_ref), custom_call_target="tpu_custom_call" | custom-call | tf_op jit(solution)/shard_map/pallas_call | solution.py:102
  43.4 4.0 %collective-permute-start.1 = (f32[5,2,32,128]{3,2,1,0:T(8,128)}, f32[5,2,32,128]{3,2,1,0:T(8,128)S(1)}, u32[]{:S(2)}, u32[]{:S(2)}) collective-permute-start(f32[5,2,32,128]{3,2,1,0:T(8,128)} %get-tuple-element.11), channel_id=1, source_target_pairs={{0,16},{16,32},{32,48},{48,64},{64,80},{80,96},{96,112},{112,128},... | collective-permute-start | bytes 491528 | tf_op jit(solution)/shard_map/ppermute | solution.py:177
  47.4 10.1 %collective-permute-start.2 = (f32[5,2,32,128]{3,2,1,0:T(8,128)}, f32[5,2,32,128]{3,2,1,0:T(8,128)S(1)}, u32[]{:S(2)}, u32[]{:S(2)}) collective-permute-start(f32[5,2,32,128]{3,2,1,0:T(8,128)} %get-tuple-element.12), channel_id=1, source_target_pairs={{16,0},{32,16},{48,32},{64,48},{80,64},{96,80},{112,96},{128,112},... | collective-permute-start | bytes 491528 | tf_op jit(solution)/shard_map/ppermute | solution.py:177
  57.6 1.9 %collective-permute-start.3 = (f32[5,8,2,128]{3,2,1,0:T(2,128)}, f32[5,8,2,128]{3,2,1,0:T(2,128)S(1)}, u32[]{:S(2)}, u32[]{:S(2)}) collective-permute-start(f32[5,8,2,128]{3,2,1,0:T(2,128)} %get-tuple-element.13), channel_id=1, source_target_pairs={{0,1},{1,2},{2,3},{3,4},{4,5},{5,6},{6,7},{7,8},{8,9},{9,10},{10,1... | collective-permute-start | bytes 122888 | tf_op jit(solution)/shard_map/ppermute | solution.py:177
  59.5 2.4 %collective-permute-start.4 = (f32[5,8,2,128]{3,2,1,0:T(2,128)}, f32[5,8,2,128]{3,2,1,0:T(2,128)S(1)}, u32[]{:S(2)}, u32[]{:S(2)}) collective-permute-start(f32[5,8,2,128]{3,2,1,0:T(2,128)} %get-tuple-element.14), channel_id=1, source_target_pairs={{1,0},{2,1},{3,2},{4,3},{5,4},{6,5},{7,6},{8,7},{9,8},{10,9},{11,1... | collective-permute-start | bytes 122888 | tf_op jit(solution)/shard_map/ppermute | solution.py:177
  61.9 3.1 %collective-permute-done.4.yh_ref = f32[5,8,2,128]{3,2,1,0:T(2,128)S(1)} collective-permute-done((f32[5,8,2,128]{3,2,1,0:T(2,128)}, f32[5,8,2,128]{3,2,1,0:T(2,128)S(1)}, u32[]{:S(2)}, u32[]{:S(2)}) %collective-permute-start.4) | collective-permute-done | bytes 40992 | tf_op jit(solution)/shard_map/ppermute | solution.py:177
  65.1 0.6 copy-done.5
  65.6 0.1 copy-done.2
  65.8 4.7 %shard_map.75 = f32[5,8,32,128]{3,2,1,0:T(8,128)} custom-call(f32[3,5]{1,0:T(4,128)} %c_ref.1, f32[5,8,32,128]{3,2,1,0:T(8,128)} %get-tuple-element.10.u_ref, f32[5,2,32,128]{3,2,1,0:T(8,128)} %copy-done.2, f32[5,2,32,128]{3,2,1,0:T(8,128)} %copy-done.3, f32[5,8,2,128]{3,2,1,0:T(2,128)} %copy-done.4, f32[5,8,2,128]{3,2,1,0:T(2,128)} %copy-done.5), custom_call_target="tpu_custom_call" | custom-call | tf_op jit(solution)/shard_map/pallas_call | solution.py:164
  (23 shorter events, 0.2 us)
Async XLA Ops:
  0.0 6.8 %copy-start = (f32[64,5,512]{2,0,1:T(8,128)S(1)}, f32[64,5,512]{2,0,1:T(8,128)}, u32[]{:S(2)}) copy-start(f32[64,5,512]{2,0,1:T(8,128)} %param.7) | copy-start | bytes 1966084
  1.1 20.6 %collective-permute-start = (f32[64,5,64]{2,1,0:T(8,128)S(1)}, f32[64,5,64]{2,1,0:T(8,128)S(1)}, u32[]{:S(2)}, u32[]{:S(2)}) collective-permute-start(f32[64,5,64]{2,1,0:T(8,128)S(1)} %copy.16), channel_id=1, source_target_pairs={{0,16},{16,32},{32,48},{48,64},{64,80},{80,96},{96,112},{112,128},... | collective-permute-start | bytes 245768 | tf_op jit(solution)/shard_map/ppermute | solution.py:188
  8.8 9.0 %copy-start.7 = (s32[1,1,64]{2,1,0:T(1,128)S(1)}, s32[1,1,64]{2,1,0:T(1,128)}, u32[]{:S(2)}) copy-start(s32[1,1,64]{2,1,0:T(1,128)} %param.11) | copy-start | bytes 772
  9.8 28.0 %all-to-all-start = ((f32[16,80,128]{2,1,0:T(8,128)}), f32[16,80,128]{2,1,0:T(8,128)S(1)}, u32[]{:S(2)}, u32[]{:S(2)}) async-start(f32[16,80,128]{2,1,0:T(8,128)} %reshape.105), calls=%async_computation | async-start | bytes 1310720 | tf_op jit(solution)/shard_map/all_to_all | solution.py:197
  20.4 2.6 %copy-start.6 = (f32[2]{0:T(128)S(1)}, f32[2]{0:T(128)}, u32[]{:S(2)}) copy-start(f32[2]{0:T(128)} %constant.33.clone) | copy-start | bytes 28
  37.8 0.8 %copy-start.1 = (f32[16,80,128]{2,1,0:T(8,128)}, f32[16,80,128]{2,1,0:T(8,128)S(1)}, u32[]{:S(2)}) copy-start(f32[16,80,128]{2,1,0:T(8,128)S(1)} %all-to-all-done) | copy-start | bytes 1966084
  43.4 21.6 %collective-permute-start.1 = (f32[5,2,32,128]{3,2,1,0:T(8,128)}, f32[5,2,32,128]{3,2,1,0:T(8,128)S(1)}, u32[]{:S(2)}, u32[]{:S(2)}) collective-permute-start(f32[5,2,32,128]{3,2,1,0:T(8,128)} %get-tuple-element.11), channel_id=1, source_target_pairs={{0,16},{16,32},{32,48},{48,64},{64,80},{80,96},{96,112},{112,128},... | collective-permute-start | bytes 491528 | tf_op jit(solution)/shard_map/ppermute | solution.py:177
  47.4 17.6 %collective-permute-start.2 = (f32[5,2,32,128]{3,2,1,0:T(8,128)}, f32[5,2,32,128]{3,2,1,0:T(8,128)S(1)}, u32[]{:S(2)}, u32[]{:S(2)}) collective-permute-start(f32[5,2,32,128]{3,2,1,0:T(8,128)} %get-tuple-element.12), channel_id=1, source_target_pairs={{16,0},{32,16},{48,32},{64,48},{80,64},{96,80},{112,96},{128,112},... | collective-permute-start | bytes 491528 | tf_op jit(solution)/shard_map/ppermute | solution.py:177
  57.6 4.3 %collective-permute-start.3 = (f32[5,8,2,128]{3,2,1,0:T(2,128)}, f32[5,8,2,128]{3,2,1,0:T(2,128)S(1)}, u32[]{:S(2)}, u32[]{:S(2)}) collective-permute-start(f32[5,8,2,128]{3,2,1,0:T(2,128)} %get-tuple-element.13), channel_id=1, source_target_pairs={{0,1},{1,2},{2,3},{3,4},{4,5},{5,6},{6,7},{7,8},{8,9},{9,10},{10,1... | collective-permute-start | bytes 122888 | tf_op jit(solution)/shard_map/ppermute | solution.py:177
  59.5 5.5 %collective-permute-start.4 = (f32[5,8,2,128]{3,2,1,0:T(2,128)}, f32[5,8,2,128]{3,2,1,0:T(2,128)S(1)}, u32[]{:S(2)}, u32[]{:S(2)}) collective-permute-start(f32[5,8,2,128]{3,2,1,0:T(2,128)} %get-tuple-element.14), channel_id=1, source_target_pairs={{1,0},{2,1},{3,2},{4,3},{5,4},{6,5},{7,6},{8,7},{9,8},{10,9},{11,1... | collective-permute-start | bytes 122888 | tf_op jit(solution)/shard_map/ppermute | solution.py:177
  61.9 3.1 %copy-start.4 = (f32[5,8,2,128]{3,2,1,0:T(2,128)}, f32[5,8,2,128]{3,2,1,0:T(2,128)S(1)}, u32[]{:S(2)}) copy-start(f32[5,8,2,128]{3,2,1,0:T(2,128)S(1)} %collective-permute-done.3.yl_ref) | copy-start | bytes 122884
  65.0 0.6 copy-start.5
  65.0 0.7 copy-start.2
  65.0 0.7 %copy-start.3 = (f32[5,2,32,128]{3,2,1,0:T(8,128)}, f32[5,2,32,128]{3,2,1,0:T(8,128)S(1)}, u32[]{:S(2)}) copy-start(f32[5,2,32,128]{3,2,1,0:T(8,128)S(1)} %collective-permute-done.2.zh_ref) | copy-start | bytes 491524

commit v11 on v10

--- a/solution.py
+++ b/solution.py
@@ -121,14 +121,38 @@
     return cell + 0.5 * kernel_minmod(cell - below, above - cell)
 
 
-def advance_kernel(c_ref, u_ref, zl_ref, zh_ref, yl_ref, yh_ref, o_ref):
+def xterm_kernel(c_ref, u_ref, o_ref):
+    fields, zn, yn, xn = u_ref.shape
+    lane = lax.broadcasted_iota(jnp.int32, (yn, xn), 1)
+    for f in range(fields):
+        cx = c_ref[2, f]
+        for z in range(zn):
+            u = u_ref[f, z]
+            lower1 = jnp.where(lane >= 1, pltpu.roll(u, 1, 1), 0.0)
+            upper1 = jnp.where(lane < xn - 1, pltpu.roll(u, xn - 1, 1), 0.0)
+            gx = face(lower1, u, upper1)
+            gx_lo = jnp.where(lane >= 1, pltpu.roll(gx, 1, 1), 0.0)
+            o_ref[f, z] = cx * (gx - gx_lo)
+
+
+def xterm(courant, region):
+    vmem = pl.BlockSpec(memory_space=pltpu.VMEM)
+    return pl.pallas_call(
+        xterm_kernel,
+        in_specs=[pl.BlockSpec(memory_space=pltpu.SMEM), vmem],
+        out_specs=vmem,
+        out_shape=jax.ShapeDtypeStruct(region.shape, jnp.float32),
+        interpret=INTERPRET,
+    )(courant, region)
+
+
+def advance_kernel(c_ref, u_ref, zl_ref, zh_ref, yl_ref, yh_ref, tx_ref, o_ref):
     fields, zn, yn, xn = u_ref.shape
     lane = lax.broadcasted_iota(jnp.int32, (yn, xn), 1)
     row = lax.broadcasted_iota(jnp.int32, (yn, xn), 0)
     for f in range(fields):
         cz = c_ref[0, f]
         cy = c_ref[1, f]
-        cx = c_ref[2, f]
 
         def plane(j):
             if j < 2:
@@ -151,23 +175,18 @@
             gy_first = face(ylo[0:1], ylo[1:2], u[0:1])
             gy_lo = jnp.where(row == 0, gy_first, pltpu.roll(gy, 1, 0))
             ty = cy * (gy - gy_lo)
-            lower1 = jnp.where(lane >= 1, pltpu.roll(u, 1, 1), 0.0)
-            upper1 = jnp.where(lane < xn - 1, pltpu.roll(u, xn - 1, 1), 0.0)
-            gx = face(lower1, u, upper1)
-            gx_lo = jnp.where(lane >= 1, pltpu.roll(gx, 1, 1), 0.0)
-            tx = cx * (gx - gx_lo)
-            o_ref[f, z] = u - ((tz + ty) + tx)
-
-
-def advance(courant, region, zlo, zhi, ylo, yhi):
+            o_ref[f, z] = u - ((tz + ty) + tx_ref[f, z])
+
+
+def advance(courant, region, zlo, zhi, ylo, yhi, tx):
     vmem = pl.BlockSpec(memory_space=pltpu.VMEM)
     return pl.pallas_call(
         advance_kernel,
-        in_specs=[pl.BlockSpec(memory_space=pltpu.SMEM), vmem, vmem, vmem, vmem, vmem],
+        in_specs=[pl.BlockSpec(memory_space=pltpu.SMEM), vmem, vmem, vmem, vmem, vmem, vmem],
         out_specs=vmem,
         out_shape=jax.ShapeDtypeStruct(region.shape, jnp.float32),
         interpret=INTERPRET,
-    )(courant, region, zlo, zhi, ylo, yhi)
+    )(courant, region, zlo, zhi, ylo, yhi, tx)
 
 
 def exchange(top, bottom, axis):
@@ -210,7 +229,8 @@
 
     zlo, zhi = exchange(ztop, zbot, "slab")
     ylo, yhi = exchange(ytop, ybot, "tile")
-    return advance(courant, region, zlo, zhi, ylo, yhi)
+    tx = xterm(courant, region)
+    return advance(courant, region, zlo, zhi, ylo, yhi, tx)
 
 
 def solution(mesh):

time: 70.9 us -> 71.3 us (level)
  waiting for transfers between devices: 16.5 us -> 13.4 us
  Pallas kernels: 11.3 us -> 14.2 us
    pallas_call x0 -> x1, Pallas kernels: none -> 4.57 us  [xterm(): pl.pallas_call(xterm_kernel, in_specs=[pl.BlockSpec(memory_space=pltpu.SM...]
    ppermute x2, waiting for transfers between devices: 3.1 us -> 0.01 us  [exchange(): lax.ppermute(bottom, axis, backward)]
    pallas_call x1, Pallas kernels: 4.69 us -> 3.01 us  [advance(): pl.pallas_call(advance_kernel, in_specs=[pl.BlockSpec(memory_space=pltpu....]
  transfers between devices with their start and end apart: 6 -> 6, of which waited for: 3 -> 2; matrix products, arithmetic and copies ran while one was open for 13% -> 13% of each run, Pallas kernels for 3% -> 9%
where the time goes in v11:
time: 71.3 us; the launch traced here: 70.8 us
  starting transfers between devices  30.5 us (43%)
  Pallas kernels  14.2 us (20%)
  waiting for transfers between devices  13.4 us (19%)
  local copies, waits for them, and re-layouts  7.74 us (11%)
  other arithmetic  4.76 us (7%)
    ppermute x2, starting transfers between devices, exchange(): lax.ppermute(bottom, axis, backward)  12.5 us
    all_to_all x1, waiting for transfers between devices, local(): lax.all_to_all(outgoing, 'tile', split_axis=0, concat_axis=0, tiled=True)  12.2 us
    all_to_all x1, starting transfers between devices, local(): lax.all_to_all(outgoing, 'tile', split_axis=0, concat_axis=0, tiled=True)  8.07 us
    ppermute x2, starting transfers between devices, exchange(): lax.ppermute(top, axis, forward)  5.91 us
    pallas_call x1, Pallas kernels, assemble(): pl.pallas_call(assemble_kernel, out_shape=[jax.ShapeDtypeStruct((fields,...  4.8 us
    pallas_call x1, Pallas kernels, xterm(): pl.pallas_call(xterm_kernel, in_specs=[pl.BlockSpec(memory_space=pltpu.SM...  4.57 us
    ppermute x1, starting transfers between devices, local(): lax.ppermute(coarse_fine, 'slab', [(i, (i + 1) % slabs) for i in range(sl...  4 us
    unnamed x17, local copies, waits for them, and re-layouts  3.25 us
  transfers between devices with their start and end apart: 6, of which 2 were waited for; matrix products, arithmetic and copies ran while one was open for 13% of the time, Pallas kernels for 9%

profile of v11, /device:TPU:7, one launch (start us, length us, event | category | flops | bytes accessed | tf_op | source)
XLA Modules:
  0.0 70.8 jit_solution(4192910376442142818)
XLA Ops:
  0.0 1.1 %copy.16 = f32[64,5,64]{2,1,0:T(8,128)S(1)} copy(f32[64,5,64]{2,0,1:T(8,128)} %param.8) | data formatting | bytes 163840 | tf_op args[1]
  1.1 4.0 %collective-permute-start = (f32[64,5,64]{2,1,0:T(8,128)S(1)}, f32[64,5,64]{2,1,0:T(8,128)S(1)}, u32[]{:S(2)}, u32[]{:S(2)}) collective-permute-start(f32[64,5,64]{2,1,0:T(8,128)S(1)} %copy.16), channel_id=1, source_target_pairs={{0,16},{16,32},{32,48},{48,64},{64,80},{80,96},{96,112},{112,128},... | collective-permute-start | bytes 245768 | tf_op jit(solution)/shard_map/ppermute | solution.py:207
  5.1 0.9 %convert_reduce_fusion = s32[64]{0:T(128)S(1)} fusion(s32[64]{0:T(128)} %bitcast.25), kind=kLoop, calls=%fused_computation.24 | loop fusion | flops 20416 | bytes 512 | tf_op jit(solution)/shard_map/reduce_sum | solution.py:212
  6.0 0.7 bitcast_select_fusion
  6.7 0.1 select_reduce_fusion
  6.9 1.5 %gather_fusion = f32[64,5,512]{2,0,1:T(8,128)S(1)} fusion(f32[64,5,512]{2,0,1:T(8,128)S(1)} %copy-done, s32[1024]{0:T(1024)S(1)} %pad_clamp_fusion.1), kind=kCustom, calls=%fused_computation | custom fusion | bytes 1310976 | tf_op jit(solution)/shard_map/gather | solution.py:215
  8.4 0.4 copy.15
  8.8 1.0 %reshape.105 = f32[16,80,128]{2,1,0:T(8,128)} reshape(f32[64,5,512]{2,1,0:T(8,128)S(1)} %copy.15) | data formatting | bytes 1310720 | tf_op jit(solution)/shard_map/reshape | solution.py:215
  9.8 8.1 %all-to-all-start = ((f32[16,80,128]{2,1,0:T(8,128)}), f32[16,80,128]{2,1,0:T(8,128)S(1)}, u32[]{:S(2)}, u32[]{:S(2)}) async-start(f32[16,80,128]{2,1,0:T(8,128)} %reshape.105), calls=%async_computation | async-start | bytes 1310720 | tf_op jit(solution)/shard_map/all_to_all | solution.py:216
  17.9 0.1 broadcast_in_dim.13
  17.9 0.7 broadcast_in_dim_reshape.2.src_ref
  18.6 1.8 %shard_map.73.p_ref = bf16[1024,512]{1,0:T(8,128)(2,1)} custom-call(s32[1,512]{1,0:T(1,128)} %broadcast_in_dim_reshape.2.src_ref), custom_call_target="tpu_custom_call" | custom-call | tf_op jit(solution)/shard_map/pallas_call | solution.py:93
  20.4 1.2 %collective-permute-done = f32[64,5,64]{2,1,0:T(8,128)S(1)} collective-permute-done((f32[64,5,64]{2,1,0:T(8,128)S(1)}, f32[64,5,64]{2,1,0:T(8,128)S(1)}, u32[]{:S(2)}, u32[]{:S(2)}) %collective-permute-start) | collective-permute-done | bytes 81952 | tf_op jit(solution)/shard_map/ppermute | solution.py:207
  21.7 0.6 gather_fusion.1
  22.3 0.1 copy.17
  22.5 0.4 minimum_maximum_fusion.2
  23.0 0.1 broadcast_multiply_fusion.2
  23.1 0.1 broadcast_multiply_fusion.1
  23.3 0.2 broadcast_multiply_fusion
  23.5 0.2 broadcast_add_fusion
  23.7 1.9 %add_add_fusion = f32[5,4,2,4,2,4,2,64]{7,6,5,4,3,2,1,0:T(2,128)} fusion(f32[5,4,4,4,2,64]{5,4,3,2,1,0:T(2,128)S(1)} %broadcast_multiply_fusion, f32[5,4,2,4,2,4,64]{6,5,4,3,2,1,0:T(4,128)S(1)} %broadcast_add_fusion, f32[5,4,4,4,64]{4,3,2,1,0:T(4,128)S(1)} %bitcast.22), kind=kLoop, calls=%fused_computation.2 | loop fusion | flops 327680 | bytes 1228800 | tf_op jit(solution)/shard_map/add | solution.py:39
  25.6 12.2 %all-to-all-done = f32[16,80,128]{2,1,0:T(8,128)S(1)} async-done(((f32[16,80,128]{2,1,0:T(8,128)}), f32[16,80,128]{2,1,0:T(8,128)S(1)}, u32[]{:S(2)}, u32[]{:S(2)}) %all-to-all-start) | async-done | bytes 655392 | tf_op jit(solution)/shard_map/all_to_all | solution.py:216
  37.8 0.8 %copy-done.1 = f32[16,80,128]{2,1,0:T(8,128)} copy-done((f32[16,80,128]{2,1,0:T(8,128)}, f32[16,80,128]{2,1,0:T(8,128)S(1)}, u32[]{:S(2)}) %copy-start.1) | copy-done | bytes 655384
  38.6 4.8 %shard_map.74 = (f32[5,8,32,128]{3,2,1,0:T(8,128)}, f32[5,2,32,128]{3,2,1,0:T(8,128)}, f32[5,2,32,128]{3,2,1,0:T(8,128)}, f32[5,8,2,128]{3,2,1,0:T(2,128)}, f32[5,8,2,128]{3,2,1,0:T(2,128)}) custom-call(f32[1280,128]{1,0:T(8,128)} %bitcast.23, f32[5,512,64]{2,1,0:T(8,128)} %bitcast.17, bf16[1024,512]{1,0:T(8,128)(2,1)} %shard_map.73.p_ref), custom_call_target="tpu_custom_call" | custom-call | tf_op jit(solution)/shard_map/pallas_call | solution.py:102
  43.4 4.0 %collective-permute-start.1 = (f32[5,2,32,128]{3,2,1,0:T(8,128)}, f32[5,2,32,128]{3,2,1,0:T(8,128)S(1)}, u32[]{:S(2)}, u32[]{:S(2)}) collective-permute-start(f32[5,2,32,128]{3,2,1,0:T(8,128)} %get-tuple-element.11), channel_id=1, source_target_pairs={{0,16},{16,32},{32,48},{48,64},{64,80},{80,96},{96,112},{112,128},... | collective-permute-start | bytes 491528 | tf_op jit(solution)/shard_map/ppermute | solution.py:196
  47.4 10.1 %collective-permute-start.2 = (f32[5,2,32,128]{3,2,1,0:T(8,128)}, f32[5,2,32,128]{3,2,1,0:T(8,128)S(1)}, u32[]{:S(2)}, u32[]{:S(2)}) collective-permute-start(f32[5,2,32,128]{3,2,1,0:T(8,128)} %get-tuple-element.12), channel_id=1, source_target_pairs={{16,0},{32,16},{48,32},{64,48},{80,64},{96,80},{112,96},{128,112},... | collective-permute-start | bytes 491528 | tf_op jit(solution)/shard_map/ppermute | solution.py:196
  57.6 1.9 %collective-permute-start.3 = (f32[5,8,2,128]{3,2,1,0:T(2,128)}, f32[5,8,2,128]{3,2,1,0:T(2,128)S(1)}, u32[]{:S(2)}, u32[]{:S(2)}) collective-permute-start(f32[5,8,2,128]{3,2,1,0:T(2,128)} %get-tuple-element.13), channel_id=1, source_target_pairs={{0,1},{1,2},{2,3},{3,4},{4,5},{5,6},{6,7},{7,8},{8,9},{9,10},{10,1... | collective-permute-start | bytes 122888 | tf_op jit(solution)/shard_map/ppermute | solution.py:196
  59.5 2.4 %collective-permute-start.4 = (f32[5,8,2,128]{3,2,1,0:T(2,128)}, f32[5,8,2,128]{3,2,1,0:T(2,128)S(1)}, u32[]{:S(2)}, u32[]{:S(2)}) collective-permute-start(f32[5,8,2,128]{3,2,1,0:T(2,128)} %get-tuple-element.14), channel_id=1, source_target_pairs={{1,0},{2,1},{3,2},{4,3},{5,4},{6,5},{7,6},{8,7},{9,8},{10,9},{11,1... | collective-permute-start | bytes 122888 | tf_op jit(solution)/shard_map/ppermute | solution.py:196
  61.9 4.6 %shard_map.75.tx_ref = f32[5,8,32,128]{3,2,1,0:T(8,128)} custom-call(f32[3,5]{1,0:T(4,128)} %c_ref.3, f32[5,8,32,128]{3,2,1,0:T(8,128)} %get-tuple-element.10.u_ref), custom_call_target="tpu_custom_call" | custom-call | tf_op jit(solution)/shard_map/pallas_call | solution.py:140
  66.5 0.6 copy-done.4
  67.2 0.7 copy-done.3
  67.8 3.0 %shard_map.76 = f32[5,8,32,128]{3,2,1,0:T(8,128)} custom-call(f32[3,5]{1,0:T(4,128)} %c_ref.3, f32[5,8,32,128]{3,2,1,0:T(8,128)} %get-tuple-element.10.u_ref, f32[5,2,32,128]{3,2,1,0:T(8,128)} %copy-done.2, f32[5,2,32,128]{3,2,1,0:T(8,128)} %copy-done.3, f32[5,8,2,128]{3,2,1,0:T(2,128)} %copy-done.4, f32[5,8,2,128]{3,2,1,0:T(2,128)} %copy-done.5, ...), custom_call_target="tpu_custom_call" | custom-call | tf_op jit(solution)/shard_map/pallas_call | solution.py:183
  (24 shorter events, 0.2 us)
Async XLA Ops:
  0.0 6.8 %copy-start = (f32[64,5,512]{2,0,1:T(8,128)S(1)}, f32[64,5,512]{2,0,1:T(8,128)}, u32[]{:S(2)}) copy-start(f32[64,5,512]{2,0,1:T(8,128)} %param.7) | copy-start | bytes 1966084
  1.1 20.6 %collective-permute-start = (f32[64,5,64]{2,1,0:T(8,128)S(1)}, f32[64,5,64]{2,1,0:T(8,128)S(1)}, u32[]{:S(2)}, u32[]{:S(2)}) collective-permute-start(f32[64,5,64]{2,1,0:T(8,128)S(1)} %copy.16), channel_id=1, source_target_pairs={{0,16},{16,32},{32,48},{48,64},{64,80},{80,96},{96,112},{112,128},... | collective-permute-start | bytes 245768 | tf_op jit(solution)/shard_map/ppermute | solution.py:207
  8.8 9.0 %copy-start.7 = (s32[1,1,64]{2,1,0:T(1,128)S(1)}, s32[1,1,64]{2,1,0:T(1,128)}, u32[]{:S(2)}) copy-start(s32[1,1,64]{2,1,0:T(1,128)} %param.11) | copy-start | bytes 772
  9.8 28.0 %all-to-all-start = ((f32[16,80,128]{2,1,0:T(8,128)}), f32[16,80,128]{2,1,0:T(8,128)S(1)}, u32[]{:S(2)}, u32[]{:S(2)}) async-start(f32[16,80,128]{2,1,0:T(8,128)} %reshape.105), calls=%async_computation | async-start | bytes 1310720 | tf_op jit(solution)/shard_map/all_to_all | solution.py:216
  20.4 2.6 %copy-start.6 = (f32[2]{0:T(128)S(1)}, f32[2]{0:T(128)}, u32[]{:S(2)}) copy-start(f32[2]{0:T(128)} %constant.33.clone) | copy-start | bytes 28
  37.8 0.8 %copy-start.1 = (f32[16,80,128]{2,1,0:T(8,128)}, f32[16,80,128]{2,1,0:T(8,128)S(1)}, u32[]{:S(2)}) copy-start(f32[16,80,128]{2,1,0:T(8,128)S(1)} %all-to-all-done) | copy-start | bytes 1966084
  43.4 23.1 %collective-permute-start.1 = (f32[5,2,32,128]{3,2,1,0:T(8,128)}, f32[5,2,32,128]{3,2,1,0:T(8,128)S(1)}, u32[]{:S(2)}, u32[]{:S(2)}) collective-permute-start(f32[5,2,32,128]{3,2,1,0:T(8,128)} %get-tuple-element.11), channel_id=1, source_target_pairs={{0,16},{16,32},{32,48},{48,64},{64,80},{80,96},{96,112},{112,128},... | collective-permute-start | bytes 491528 | tf_op jit(solution)/shard_map/ppermute | solution.py:196
  47.4 19.1 %collective-permute-start.2 = (f32[5,2,32,128]{3,2,1,0:T(8,128)}, f32[5,2,32,128]{3,2,1,0:T(8,128)S(1)}, u32[]{:S(2)}, u32[]{:S(2)}) collective-permute-start(f32[5,2,32,128]{3,2,1,0:T(8,128)} %get-tuple-element.12), channel_id=1, source_target_pairs={{16,0},{32,16},{48,32},{64,48},{80,64},{96,80},{112,96},{128,112},... | collective-permute-start | bytes 491528 | tf_op jit(solution)/shard_map/ppermute | solution.py:196
  57.6 8.9 %collective-permute-start.3 = (f32[5,8,2,128]{3,2,1,0:T(2,128)}, f32[5,8,2,128]{3,2,1,0:T(2,128)S(1)}, u32[]{:S(2)}, u32[]{:S(2)}) collective-permute-start(f32[5,8,2,128]{3,2,1,0:T(2,128)} %get-tuple-element.13), channel_id=1, source_target_pairs={{0,1},{1,2},{2,3},{3,4},{4,5},{5,6},{6,7},{7,8},{8,9},{9,10},{10,1... | collective-permute-start | bytes 122888 | tf_op jit(solution)/shard_map/ppermute | solution.py:196
  59.5 7.0 %collective-permute-start.4 = (f32[5,8,2,128]{3,2,1,0:T(2,128)}, f32[5,8,2,128]{3,2,1,0:T(2,128)S(1)}, u32[]{:S(2)}, u32[]{:S(2)}) collective-permute-start(f32[5,8,2,128]{3,2,1,0:T(2,128)} %get-tuple-element.14), channel_id=1, source_target_pairs={{1,0},{2,1},{3,2},{4,3},{5,4},{6,5},{7,6},{8,7},{9,8},{10,9},{11,1... | collective-permute-start | bytes 122888 | tf_op jit(solution)/shard_map/ppermute | solution.py:196
  66.5 0.6 copy-start.4
  66.5 0.6 copy-start.5
  66.5 0.7 copy-start.2
  67.2 0.7 copy-start.3

commit v12 on v11

--- a/solution.py
+++ b/solution.py
@@ -50,8 +50,7 @@
     for f in range(fields):
         moved = jnp.concatenate(
             [arr_ref[pl.ds(f * quarters + q, blocks, stride=stride), :] for q in range(quarters)], axis=1)
-        a = jnp.concatenate([moved, jnp.zeros_like(moved)], axis=0)
-        at_ref[f * cells:(f + 1) * cells, :] = a.T
+        at_ref[f * cells:(f + 1) * cells, :blocks] = moved.T
         at_ref[f * cells:(f + 1) * cells, blocks:] = int_ref[f]
         parts.append(jnp.concatenate(
             [at_ref[pl.ds(f * cells + x, zy, stride=E), :] for x in range(E)], axis=1))
@@ -121,18 +120,30 @@
     return cell + 0.5 * kernel_minmod(cell - below, above - cell)
 
 
+def exact_shift(v, shift):
+    hi = v.astype(jnp.bfloat16)
+    rest = v - hi.astype(jnp.float32)
+    mid = rest.astype(jnp.bfloat16)
+    lo = (rest - mid.astype(jnp.float32)).astype(jnp.bfloat16)
+    n = v.shape[0]
+    res = jnp.dot(jnp.concatenate([hi, mid, lo], axis=0), shift, preferred_element_type=jnp.float32)
+    return (res[:n] + res[n:2 * n]) + res[2 * n:]
+
+
 def xterm_kernel(c_ref, u_ref, o_ref):
     fields, zn, yn, xn = u_ref.shape
-    lane = lax.broadcasted_iota(jnp.int32, (yn, xn), 1)
+    src = lax.broadcasted_iota(jnp.int32, (xn, 2 * xn), 0)
+    dst = lax.broadcasted_iota(jnp.int32, (xn, 2 * xn), 1)
+    both = jnp.where(((dst < xn) & (src == dst - 1)) | ((dst >= xn) & (src == dst - xn + 1)), 1.0, 0.0)
+    both = both.astype(jnp.bfloat16)
+    down = both[:, :xn]
     for f in range(fields):
         cx = c_ref[2, f]
-        for z in range(zn):
-            u = u_ref[f, z]
-            lower1 = jnp.where(lane >= 1, pltpu.roll(u, 1, 1), 0.0)
-            upper1 = jnp.where(lane < xn - 1, pltpu.roll(u, xn - 1, 1), 0.0)
-            gx = face(lower1, u, upper1)
-            gx_lo = jnp.where(lane >= 1, pltpu.roll(gx, 1, 1), 0.0)
-            o_ref[f, z] = cx * (gx - gx_lo)
+        u = u_ref[f].reshape(zn * yn, xn)
+        nb = exact_shift(u, both)
+        gx = face(nb[:, :xn], u, nb[:, xn:])
+        gx_lo = exact_shift(gx, down)
+        o_ref[f] = (cx * (gx - gx_lo)).reshape(zn, yn, xn)
 
 
 def xterm(courant, region):

time: 71.3 us -> 70.8 us (level)
  transfers between devices with their start and end apart: 6 -> 6, of which waited for: 2 -> 2; matrix products, arithmetic and copies ran while one was open for 13% -> 13% of each run, Pallas kernels for 9% -> 8%
where the time goes in v12:
time: 70.8 us; the launch traced here: 70.3 us
  starting transfers between devices  30.5 us (43%)
  Pallas kernels  13.7 us (19%)
  waiting for transfers between devices  13.4 us (19%)
  local copies, waits for them, and re-layouts  7.74 us (11%)
  other arithmetic  4.76 us (7%)
    ppermute x2, starting transfers between devices, exchange(): lax.ppermute(bottom, axis, backward)  12.5 us
    all_to_all x1, waiting for transfers between devices, local(): lax.all_to_all(outgoing, 'tile', split_axis=0, concat_axis=0, tiled=True)  12.2 us
    all_to_all x1, starting transfers between devices, local(): lax.all_to_all(outgoing, 'tile', split_axis=0, concat_axis=0, tiled=True)  8.07 us
    ppermute x2, starting transfers between devices, exchange(): lax.ppermute(top, axis, forward)  5.91 us
    pallas_call x1, Pallas kernels, assemble(): pl.pallas_call(assemble_kernel, out_shape=[jax.ShapeDtypeStruct((fields,...  4.8 us
    pallas_call x1, Pallas kernels, xterm(): pl.pallas_call(xterm_kernel, in_specs=[pl.BlockSpec(memory_space=pltpu.SM...  4.05 us
    ppermute x1, starting transfers between devices, local(): lax.ppermute(coarse_fine, 'slab', [(i, (i + 1) % slabs) for i in range(sl...  4 us
    unnamed x17, local copies, waits for them, and re-layouts  3.25 us
  transfers between devices with their start and end apart: 6, of which 2 were waited for; matrix products, arithmetic and copies ran while one was open for 13% of the time, Pallas kernels for 8%

profile of v12, /device:TPU:7, one launch (start us, length us, event | category | flops | bytes accessed | tf_op | source)
XLA Modules:
  0.0 70.3 jit_solution(15972101639471382014)
XLA Ops:
  0.0 1.1 %copy.16 = f32[64,5,64]{2,1,0:T(8,128)S(1)} copy(f32[64,5,64]{2,0,1:T(8,128)} %param.8) | data formatting | bytes 163840 | tf_op args[1]
  1.1 4.0 %collective-permute-start = (f32[64,5,64]{2,1,0:T(8,128)S(1)}, f32[64,5,64]{2,1,0:T(8,128)S(1)}, u32[]{:S(2)}, u32[]{:S(2)}) collective-permute-start(f32[64,5,64]{2,1,0:T(8,128)S(1)} %copy.16), channel_id=1, source_target_pairs={{0,16},{16,32},{32,48},{48,64},{64,80},{80,96},{96,112},{112,128},... | collective-permute-start | bytes 245768 | tf_op jit(solution)/shard_map/ppermute | solution.py:218
  5.1 0.9 %convert_reduce_fusion = s32[64]{0:T(128)S(1)} fusion(s32[64]{0:T(128)} %bitcast.25), kind=kLoop, calls=%fused_computation.24 | loop fusion | flops 20416 | bytes 512 | tf_op jit(solution)/shard_map/reduce_sum | solution.py:223
  6.0 0.7 bitcast_select_fusion
  6.7 0.1 select_reduce_fusion
  6.9 1.5 %gather_fusion = f32[64,5,512]{2,0,1:T(8,128)S(1)} fusion(f32[64,5,512]{2,0,1:T(8,128)S(1)} %copy-done, s32[1024]{0:T(1024)S(1)} %pad_clamp_fusion.1), kind=kCustom, calls=%fused_computation | custom fusion | bytes 1310976 | tf_op jit(solution)/shard_map/gather | solution.py:226
  8.4 0.4 copy.15
  8.8 1.0 %reshape.105 = f32[16,80,128]{2,1,0:T(8,128)} reshape(f32[64,5,512]{2,1,0:T(8,128)S(1)} %copy.15) | data formatting | bytes 1310720 | tf_op jit(solution)/shard_map/reshape | solution.py:226
  9.8 8.1 %all-to-all-start = ((f32[16,80,128]{2,1,0:T(8,128)}), f32[16,80,128]{2,1,0:T(8,128)S(1)}, u32[]{:S(2)}, u32[]{:S(2)}) async-start(f32[16,80,128]{2,1,0:T(8,128)} %reshape.105), calls=%async_computation | async-start | bytes 1310720 | tf_op jit(solution)/shard_map/all_to_all | solution.py:227
  17.9 0.1 broadcast_in_dim.13
  17.9 0.7 broadcast_in_dim_reshape.2.src_ref
  18.6 1.8 %shard_map.73.p_ref = bf16[1024,512]{1,0:T(8,128)(2,1)} custom-call(s32[1,512]{1,0:T(1,128)} %broadcast_in_dim_reshape.2.src_ref), custom_call_target="tpu_custom_call" | custom-call | tf_op jit(solution)/shard_map/pallas_call | solution.py:92
  20.4 1.2 %collective-permute-done = f32[64,5,64]{2,1,0:T(8,128)S(1)} collective-permute-done((f32[64,5,64]{2,1,0:T(8,128)S(1)}, f32[64,5,64]{2,1,0:T(8,128)S(1)}, u32[]{:S(2)}, u32[]{:S(2)}) %collective-permute-start) | collective-permute-done | bytes 81952 | tf_op jit(solution)/shard_map/ppermute | solution.py:218
  21.7 0.6 gather_fusion.1
  22.3 0.1 copy.17
  22.5 0.4 minimum_maximum_fusion.2
  23.0 0.1 broadcast_multiply_fusion.2
  23.1 0.1 broadcast_multiply_fusion.1
  23.3 0.2 broadcast_multiply_fusion
  23.5 0.2 broadcast_add_fusion
  23.7 1.9 %add_add_fusion = f32[5,4,2,4,2,4,2,64]{7,6,5,4,3,2,1,0:T(2,128)} fusion(f32[5,4,4,4,2,64]{5,4,3,2,1,0:T(2,128)S(1)} %broadcast_multiply_fusion, f32[5,4,2,4,2,4,64]{6,5,4,3,2,1,0:T(4,128)S(1)} %broadcast_add_fusion, f32[5,4,4,4,64]{4,3,2,1,0:T(4,128)S(1)} %bitcast.22), kind=kLoop, calls=%fused_computation.2 | loop fusion | flops 327680 | bytes 1228800 | tf_op jit(solution)/shard_map/add | solution.py:39
  25.6 12.2 %all-to-all-done = f32[16,80,128]{2,1,0:T(8,128)S(1)} async-done(((f32[16,80,128]{2,1,0:T(8,128)}), f32[16,80,128]{2,1,0:T(8,128)S(1)}, u32[]{:S(2)}, u32[]{:S(2)}) %all-to-all-start) | async-done | bytes 655392 | tf_op jit(solution)/shard_map/all_to_all | solution.py:227
  37.8 0.8 %copy-done.1 = f32[16,80,128]{2,1,0:T(8,128)} copy-done((f32[16,80,128]{2,1,0:T(8,128)}, f32[16,80,128]{2,1,0:T(8,128)S(1)}, u32[]{:S(2)}) %copy-start.1) | copy-done | bytes 655384
  38.6 4.8 %shard_map.74 = (f32[5,8,32,128]{3,2,1,0:T(8,128)}, f32[5,2,32,128]{3,2,1,0:T(8,128)}, f32[5,2,32,128]{3,2,1,0:T(8,128)}, f32[5,8,2,128]{3,2,1,0:T(2,128)}, f32[5,8,2,128]{3,2,1,0:T(2,128)}) custom-call(f32[1280,128]{1,0:T(8,128)} %bitcast.23, f32[5,512,64]{2,1,0:T(8,128)} %bitcast.17, bf16[1024,512]{1,0:T(8,128)(2,1)} %shard_map.73.p_ref), custom_call_target="tpu_custom_call" | custom-call | tf_op jit(solution)/shard_map/pallas_call | solution.py:101
  43.4 4.0 %collective-permute-start.1 = (f32[5,2,32,128]{3,2,1,0:T(8,128)}, f32[5,2,32,128]{3,2,1,0:T(8,128)S(1)}, u32[]{:S(2)}, u32[]{:S(2)}) collective-permute-start(f32[5,2,32,128]{3,2,1,0:T(8,128)} %get-tuple-element.11), channel_id=1, source_target_pairs={{0,16},{16,32},{32,48},{48,64},{64,80},{80,96},{96,112},{112,128},... | collective-permute-start | bytes 491528 | tf_op jit(solution)/shard_map/ppermute | solution.py:207
  47.4 10.1 %collective-permute-start.2 = (f32[5,2,32,128]{3,2,1,0:T(8,128)}, f32[5,2,32,128]{3,2,1,0:T(8,128)S(1)}, u32[]{:S(2)}, u32[]{:S(2)}) collective-permute-start(f32[5,2,32,128]{3,2,1,0:T(8,128)} %get-tuple-element.12), channel_id=1, source_target_pairs={{16,0},{32,16},{48,32},{64,48},{80,64},{96,80},{112,96},{128,112},... | collective-permute-start | bytes 491528 | tf_op jit(solution)/shard_map/ppermute | solution.py:207
  57.6 1.9 %collective-permute-start.3 = (f32[5,8,2,128]{3,2,1,0:T(2,128)}, f32[5,8,2,128]{3,2,1,0:T(2,128)S(1)}, u32[]{:S(2)}, u32[]{:S(2)}) collective-permute-start(f32[5,8,2,128]{3,2,1,0:T(2,128)} %get-tuple-element.13), channel_id=1, source_target_pairs={{0,1},{1,2},{2,3},{3,4},{4,5},{5,6},{6,7},{7,8},{8,9},{9,10},{10,1... | collective-permute-start | bytes 122888 | tf_op jit(solution)/shard_map/ppermute | solution.py:207
  59.5 2.4 %collective-permute-start.4 = (f32[5,8,2,128]{3,2,1,0:T(2,128)}, f32[5,8,2,128]{3,2,1,0:T(2,128)S(1)}, u32[]{:S(2)}, u32[]{:S(2)}) collective-permute-start(f32[5,8,2,128]{3,2,1,0:T(2,128)} %get-tuple-element.14), channel_id=1, source_target_pairs={{1,0},{2,1},{3,2},{4,3},{5,4},{6,5},{7,6},{8,7},{9,8},{10,9},{11,1... | collective-permute-start | bytes 122888 | tf_op jit(solution)/shard_map/ppermute | solution.py:207
  61.9 4.0 %shard_map.75.tx_ref = f32[5,8,32,128]{3,2,1,0:T(8,128)} custom-call(f32[3,5]{1,0:T(4,128)} %c_ref.3, f32[5,8,32,128]{3,2,1,0:T(8,128)} %get-tuple-element.10.u_ref), custom_call_target="tpu_custom_call" | custom-call | tf_op jit(solution)/shard_map/pallas_call | solution.py:151
  66.0 0.6 copy-done.4
  66.6 0.7 copy-done.3
  67.3 3.0 %shard_map.76 = f32[5,8,32,128]{3,2,1,0:T(8,128)} custom-call(f32[3,5]{1,0:T(4,128)} %c_ref.3, f32[5,8,32,128]{3,2,1,0:T(8,128)} %get-tuple-element.10.u_ref, f32[5,2,32,128]{3,2,1,0:T(8,128)} %copy-done.2, f32[5,2,32,128]{3,2,1,0:T(8,128)} %copy-done.3, f32[5,8,2,128]{3,2,1,0:T(2,128)} %copy-done.4, f32[5,8,2,128]{3,2,1,0:T(2,128)} %copy-done.5, ...), custom_call_target="tpu_custom_call" | custom-call | tf_op jit(solution)/shard_map/pallas_call | solution.py:194
  (24 shorter events, 0.2 us)
Async XLA Ops:
  0.0 6.8 %copy-start = (f32[64,5,512]{2,0,1:T(8,128)S(1)}, f32[64,5,512]{2,0,1:T(8,128)}, u32[]{:S(2)}) copy-start(f32[64,5,512]{2,0,1:T(8,128)} %param.7) | copy-start | bytes 1966084
  1.1 20.6 %collective-permute-start = (f32[64,5,64]{2,1,0:T(8,128)S(1)}, f32[64,5,64]{2,1,0:T(8,128)S(1)}, u32[]{:S(2)}, u32[]{:S(2)}) collective-permute-start(f32[64,5,64]{2,1,0:T(8,128)S(1)} %copy.16), channel_id=1, source_target_pairs={{0,16},{16,32},{32,48},{48,64},{64,80},{80,96},{96,112},{112,128},... | collective-permute-start | bytes 245768 | tf_op jit(solution)/shard_map/ppermute | solution.py:218
  8.8 9.0 %copy-start.7 = (s32[1,1,64]{2,1,0:T(1,128)S(1)}, s32[1,1,64]{2,1,0:T(1,128)}, u32[]{:S(2)}) copy-start(s32[1,1,64]{2,1,0:T(1,128)} %param.11) | copy-start | bytes 772
  9.8 28.0 %all-to-all-start = ((f32[16,80,128]{2,1,0:T(8,128)}), f32[16,80,128]{2,1,0:T(8,128)S(1)}, u32[]{:S(2)}, u32[]{:S(2)}) async-start(f32[16,80,128]{2,1,0:T(8,128)} %reshape.105), calls=%async_computation | async-start | bytes 1310720 | tf_op jit(solution)/shard_map/all_to_all | solution.py:227
  20.4 2.6 %copy-start.6 = (f32[2]{0:T(128)S(1)}, f32[2]{0:T(128)}, u32[]{:S(2)}) copy-start(f32[2]{0:T(128)} %constant.33.clone) | copy-start | bytes 28
  37.8 0.8 %copy-start.1 = (f32[16,80,128]{2,1,0:T(8,128)}, f32[16,80,128]{2,1,0:T(8,128)S(1)}, u32[]{:S(2)}) copy-start(f32[16,80,128]{2,1,0:T(8,128)S(1)} %all-to-all-done) | copy-start | bytes 1966084
  43.4 22.5 %collective-permute-start.1 = (f32[5,2,32,128]{3,2,1,0:T(8,128)}, f32[5,2,32,128]{3,2,1,0:T(8,128)S(1)}, u32[]{:S(2)}, u32[]{:S(2)}) collective-permute-start(f32[5,2,32,128]{3,2,1,0:T(8,128)} %get-tuple-element.11), channel_id=1, source_target_pairs={{0,16},{16,32},{32,48},{48,64},{64,80},{80,96},{96,112},{112,128},... | collective-permute-start | bytes 491528 | tf_op jit(solution)/shard_map/ppermute | solution.py:207
  47.4 18.6 %collective-permute-start.2 = (f32[5,2,32,128]{3,2,1,0:T(8,128)}, f32[5,2,32,128]{3,2,1,0:T(8,128)S(1)}, u32[]{:S(2)}, u32[]{:S(2)}) collective-permute-start(f32[5,2,32,128]{3,2,1,0:T(8,128)} %get-tuple-element.12), channel_id=1, source_target_pairs={{16,0},{32,16},{48,32},{64,48},{80,64},{96,80},{112,96},{128,112},... | collective-permute-start | bytes 491528 | tf_op jit(solution)/shard_map/ppermute | solution.py:207
  57.6 8.4 %collective-permute-start.3 = (f32[5,8,2,128]{3,2,1,0:T(2,128)}, f32[5,8,2,128]{3,2,1,0:T(2,128)S(1)}, u32[]{:S(2)}, u32[]{:S(2)}) collective-permute-start(f32[5,8,2,128]{3,2,1,0:T(2,128)} %get-tuple-element.13), channel_id=1, source_target_pairs={{0,1},{1,2},{2,3},{3,4},{4,5},{5,6},{6,7},{7,8},{8,9},{9,10},{10,1... | collective-permute-start | bytes 122888 | tf_op jit(solution)/shard_map/ppermute | solution.py:207
  59.5 6.5 %collective-permute-start.4 = (f32[5,8,2,128]{3,2,1,0:T(2,128)}, f32[5,8,2,128]{3,2,1,0:T(2,128)S(1)}, u32[]{:S(2)}, u32[]{:S(2)}) collective-permute-start(f32[5,8,2,128]{3,2,1,0:T(2,128)} %get-tuple-element.14), channel_id=1, source_target_pairs={{1,0},{2,1},{3,2},{4,3},{5,4},{6,5},{7,6},{8,7},{9,8},{10,9},{11,1... | collective-permute-start | bytes 122888 | tf_op jit(solution)/shard_map/ppermute | solution.py:207
  66.0 0.6 copy-start.4
  66.0 0.6 copy-start.5
  66.0 0.7 copy-start.2
  66.6 0.7 copy-start.3

commit v13 on v12

--- a/solution.py
+++ b/solution.py
@@ -56,12 +56,10 @@
             [at_ref[pl.ds(f * cells + x, zy, stride=E), :] for x in range(E)], axis=1))
     w = jnp.concatenate(parts, axis=0)
     hi = w.astype(jnp.bfloat16)
-    rest = w - hi.astype(jnp.float32)
-    mid = rest.astype(jnp.bfloat16)
-    lo = (rest - mid.astype(jnp.float32)).astype(jnp.bfloat16)
-    res = jnp.dot(jnp.concatenate([hi, mid, lo], axis=0), p_ref[...], preferred_element_type=jnp.float32)
+    mid = (w - hi.astype(jnp.float32)).astype(jnp.bfloat16)
+    res = jnp.dot(jnp.concatenate([hi, mid], axis=0), p_ref[...], preferred_element_type=jnp.float32)
     n = fields * zy
-    out = (res[:n] + res[n:2 * n]) + res[2 * n:]
+    out = res[:n] + res[n:]
     width = o_ref.shape[3]
     count = o_ref.shape[2] // E
     for f in range(fields):

time: 70.8 us -> 70.4 us (level)
  no operation moved by 1% of the time
where the time goes in v13:
time: 70.4 us; the launch traced here: 70 us
  starting transfers between devices  30.5 us (43%)
  waiting for transfers between devices  13.4 us (19%)
  Pallas kernels  13.3 us (19%)
  local copies, waits for them, and re-layouts  7.74 us (11%)
  other arithmetic  4.76 us (7%)
    ppermute x2, starting transfers between devices, exchange(): lax.ppermute(bottom, axis, backward)  12.5 us
    all_to_all x1, waiting for transfers between devices, local(): lax.all_to_all(outgoing, 'tile', split_axis=0, concat_axis=0, tiled=True)  12.2 us
    all_to_all x1, starting transfers between devices, local(): lax.all_to_all(outgoing, 'tile', split_axis=0, concat_axis=0, tiled=True)  8.07 us
    ppermute x2, starting transfers between devices, exchange(): lax.ppermute(top, axis, forward)  5.9 us
    pallas_call x1, Pallas kernels, assemble(): pl.pallas_call(assemble_kernel, out_shape=[jax.ShapeDtypeStruct((fields,...  4.45 us
    pallas_call x1, Pallas kernels, xterm(): pl.pallas_call(xterm_kernel, in_specs=[pl.BlockSpec(memory_space=pltpu.SM...  4.04 us
    ppermute x1, starting transfers between devices, local(): lax.ppermute(coarse_fine, 'slab', [(i, (i + 1) % slabs) for i in range(sl...  4 us
    unnamed x17, local copies, waits for them, and re-layouts  3.25 us
  transfers between devices with their start and end apart: 6, of which 2 were waited for; matrix products, arithmetic and copies ran while one was open for 13% of the time, Pallas kernels for 8%

profile of v13, /device:TPU:7, one launch (start us, length us, event | category | flops | bytes accessed | tf_op | source)
XLA Modules:
  0.0 70.0 jit_solution(18242896449458538720)
XLA Ops:
  0.0 1.1 %copy.16 = f32[64,5,64]{2,1,0:T(8,128)S(1)} copy(f32[64,5,64]{2,0,1:T(8,128)} %param.8) | data formatting | bytes 163840 | tf_op args[1]
  1.1 4.0 %collective-permute-start = (f32[64,5,64]{2,1,0:T(8,128)S(1)}, f32[64,5,64]{2,1,0:T(8,128)S(1)}, u32[]{:S(2)}, u32[]{:S(2)}) collective-permute-start(f32[64,5,64]{2,1,0:T(8,128)S(1)} %copy.16), channel_id=1, source_target_pairs={{0,16},{16,32},{32,48},{48,64},{64,80},{80,96},{96,112},{112,128},... | collective-permute-start | bytes 245768 | tf_op jit(solution)/shard_map/ppermute | solution.py:216
  5.1 0.9 %convert_reduce_fusion = s32[64]{0:T(128)S(1)} fusion(s32[64]{0:T(128)} %bitcast.25), kind=kLoop, calls=%fused_computation.24 | loop fusion | flops 20416 | bytes 512 | tf_op jit(solution)/shard_map/reduce_sum | solution.py:221
  6.0 0.7 bitcast_select_fusion
  6.7 0.1 select_reduce_fusion
  6.9 1.5 %gather_fusion = f32[64,5,512]{2,0,1:T(8,128)S(1)} fusion(f32[64,5,512]{2,0,1:T(8,128)S(1)} %copy-done, s32[1024]{0:T(1024)S(1)} %pad_clamp_fusion.1), kind=kCustom, calls=%fused_computation | custom fusion | bytes 1310976 | tf_op jit(solution)/shard_map/gather | solution.py:224
  8.4 0.4 copy.15
  8.8 1.0 %reshape.105 = f32[16,80,128]{2,1,0:T(8,128)} reshape(f32[64,5,512]{2,1,0:T(8,128)S(1)} %copy.15) | data formatting | bytes 1310720 | tf_op jit(solution)/shard_map/reshape | solution.py:224
  9.8 8.1 %all-to-all-start = ((f32[16,80,128]{2,1,0:T(8,128)}), f32[16,80,128]{2,1,0:T(8,128)S(1)}, u32[]{:S(2)}, u32[]{:S(2)}) async-start(f32[16,80,128]{2,1,0:T(8,128)} %reshape.105), calls=%async_computation | async-start | bytes 1310720 | tf_op jit(solution)/shard_map/all_to_all | solution.py:225
  17.9 0.1 broadcast_in_dim.13
  17.9 0.7 broadcast_in_dim_reshape.2.src_ref
  18.6 1.8 %shard_map.73.p_ref = bf16[1024,512]{1,0:T(8,128)(2,1)} custom-call(s32[1,512]{1,0:T(1,128)} %broadcast_in_dim_reshape.2.src_ref), custom_call_target="tpu_custom_call" | custom-call | tf_op jit(solution)/shard_map/pallas_call | solution.py:90
  20.4 1.2 %collective-permute-done = f32[64,5,64]{2,1,0:T(8,128)S(1)} collective-permute-done((f32[64,5,64]{2,1,0:T(8,128)S(1)}, f32[64,5,64]{2,1,0:T(8,128)S(1)}, u32[]{:S(2)}, u32[]{:S(2)}) %collective-permute-start) | collective-permute-done | bytes 81952 | tf_op jit(solution)/shard_map/ppermute | solution.py:216
  21.7 0.6 gather_fusion.1
  22.3 0.1 copy.17
  22.5 0.4 minimum_maximum_fusion.2
  23.0 0.1 broadcast_multiply_fusion.2
  23.1 0.1 broadcast_multiply_fusion.1
  23.3 0.2 broadcast_multiply_fusion
  23.5 0.2 broadcast_add_fusion
  23.7 1.9 %add_add_fusion = f32[5,4,2,4,2,4,2,64]{7,6,5,4,3,2,1,0:T(2,128)} fusion(f32[5,4,4,4,2,64]{5,4,3,2,1,0:T(2,128)S(1)} %broadcast_multiply_fusion, f32[5,4,2,4,2,4,64]{6,5,4,3,2,1,0:T(4,128)S(1)} %broadcast_add_fusion, f32[5,4,4,4,64]{4,3,2,1,0:T(4,128)S(1)} %bitcast.22), kind=kLoop, calls=%fused_computation.2 | loop fusion | flops 327680 | bytes 1228800 | tf_op jit(solution)/shard_map/add | solution.py:39
  25.6 12.2 %all-to-all-done = f32[16,80,128]{2,1,0:T(8,128)S(1)} async-done(((f32[16,80,128]{2,1,0:T(8,128)}), f32[16,80,128]{2,1,0:T(8,128)S(1)}, u32[]{:S(2)}, u32[]{:S(2)}) %all-to-all-start) | async-done | bytes 655392 | tf_op jit(solution)/shard_map/all_to_all | solution.py:225
  37.8 0.8 %copy-done.1 = f32[16,80,128]{2,1,0:T(8,128)} copy-done((f32[16,80,128]{2,1,0:T(8,128)}, f32[16,80,128]{2,1,0:T(8,128)S(1)}, u32[]{:S(2)}) %copy-start.1) | copy-done | bytes 655384
  38.6 4.4 %shard_map.74 = (f32[5,8,32,128]{3,2,1,0:T(8,128)}, f32[5,2,32,128]{3,2,1,0:T(8,128)}, f32[5,2,32,128]{3,2,1,0:T(8,128)}, f32[5,8,2,128]{3,2,1,0:T(2,128)}, f32[5,8,2,128]{3,2,1,0:T(2,128)}) custom-call(f32[1280,128]{1,0:T(8,128)} %bitcast.23, f32[5,512,64]{2,1,0:T(8,128)} %bitcast.17, bf16[1024,512]{1,0:T(8,128)(2,1)} %shard_map.73.p_ref), custom_call_target="tpu_custom_call" | custom-call | tf_op jit(solution)/shard_map/pallas_call | solution.py:99
  43.1 4.0 %collective-permute-start.1 = (f32[5,2,32,128]{3,2,1,0:T(8,128)}, f32[5,2,32,128]{3,2,1,0:T(8,128)S(1)}, u32[]{:S(2)}, u32[]{:S(2)}) collective-permute-start(f32[5,2,32,128]{3,2,1,0:T(8,128)} %get-tuple-element.11), channel_id=1, source_target_pairs={{0,16},{16,32},{32,48},{48,64},{64,80},{80,96},{96,112},{112,128},... | collective-permute-start | bytes 491528 | tf_op jit(solution)/shard_map/ppermute | solution.py:205
  47.1 10.1 %collective-permute-start.2 = (f32[5,2,32,128]{3,2,1,0:T(8,128)}, f32[5,2,32,128]{3,2,1,0:T(8,128)S(1)}, u32[]{:S(2)}, u32[]{:S(2)}) collective-permute-start(f32[5,2,32,128]{3,2,1,0:T(8,128)} %get-tuple-element.12), channel_id=1, source_target_pairs={{16,0},{32,16},{48,32},{64,48},{80,64},{96,80},{112,96},{128,112},... | collective-permute-start | bytes 491528 | tf_op jit(solution)/shard_map/ppermute | solution.py:205
  57.2 1.9 %collective-permute-start.3 = (f32[5,8,2,128]{3,2,1,0:T(2,128)}, f32[5,8,2,128]{3,2,1,0:T(2,128)S(1)}, u32[]{:S(2)}, u32[]{:S(2)}) collective-permute-start(f32[5,8,2,128]{3,2,1,0:T(2,128)} %get-tuple-element.13), channel_id=1, source_target_pairs={{0,1},{1,2},{2,3},{3,4},{4,5},{5,6},{6,7},{7,8},{8,9},{9,10},{10,1... | collective-permute-start | bytes 122888 | tf_op jit(solution)/shard_map/ppermute | solution.py:205
  59.1 2.4 %collective-permute-start.4 = (f32[5,8,2,128]{3,2,1,0:T(2,128)}, f32[5,8,2,128]{3,2,1,0:T(2,128)S(1)}, u32[]{:S(2)}, u32[]{:S(2)}) collective-permute-start(f32[5,8,2,128]{3,2,1,0:T(2,128)} %get-tuple-element.14), channel_id=1, source_target_pairs={{1,0},{2,1},{3,2},{4,3},{5,4},{6,5},{7,6},{8,7},{9,8},{10,9},{11,1... | collective-permute-start | bytes 122888 | tf_op jit(solution)/shard_map/ppermute | solution.py:205
  61.5 4.0 %shard_map.75.tx_ref = f32[5,8,32,128]{3,2,1,0:T(8,128)} custom-call(f32[3,5]{1,0:T(4,128)} %c_ref.3, f32[5,8,32,128]{3,2,1,0:T(8,128)} %get-tuple-element.10.u_ref), custom_call_target="tpu_custom_call" | custom-call | tf_op jit(solution)/shard_map/pallas_call | solution.py:149
  65.6 0.6 copy-done.4
  66.3 0.7 copy-done.3
  66.9 3.0 %shard_map.76 = f32[5,8,32,128]{3,2,1,0:T(8,128)} custom-call(f32[3,5]{1,0:T(4,128)} %c_ref.3, f32[5,8,32,128]{3,2,1,0:T(8,128)} %get-tuple-element.10.u_ref, f32[5,2,32,128]{3,2,1,0:T(8,128)} %copy-done.2, f32[5,2,32,128]{3,2,1,0:T(8,128)} %copy-done.3, f32[5,8,2,128]{3,2,1,0:T(2,128)} %copy-done.4, f32[5,8,2,128]{3,2,1,0:T(2,128)} %copy-done.5, ...), custom_call_target="tpu_custom_call" | custom-call | tf_op jit(solution)/shard_map/pallas_call | solution.py:192
  (24 shorter events, 0.2 us)
Async XLA Ops:
  0.0 6.8 %copy-start = (f32[64,5,512]{2,0,1:T(8,128)S(1)}, f32[64,5,512]{2,0,1:T(8,128)}, u32[]{:S(2)}) copy-start(f32[64,5,512]{2,0,1:T(8,128)} %param.7) | copy-start | bytes 1966084
  1.1 20.6 %collective-permute-start = (f32[64,5,64]{2,1,0:T(8,128)S(1)}, f32[64,5,64]{2,1,0:T(8,128)S(1)}, u32[]{:S(2)}, u32[]{:S(2)}) collective-permute-start(f32[64,5,64]{2,1,0:T(8,128)S(1)} %copy.16), channel_id=1, source_target_pairs={{0,16},{16,32},{32,48},{48,64},{64,80},{80,96},{96,112},{112,128},... | collective-permute-start | bytes 245768 | tf_op jit(solution)/shard_map/ppermute | solution.py:216
  8.8 9.0 %copy-start.7 = (s32[1,1,64]{2,1,0:T(1,128)S(1)}, s32[1,1,64]{2,1,0:T(1,128)}, u32[]{:S(2)}) copy-start(s32[1,1,64]{2,1,0:T(1,128)} %param.11) | copy-start | bytes 772
  9.8 28.0 %all-to-all-start = ((f32[16,80,128]{2,1,0:T(8,128)}), f32[16,80,128]{2,1,0:T(8,128)S(1)}, u32[]{:S(2)}, u32[]{:S(2)}) async-start(f32[16,80,128]{2,1,0:T(8,128)} %reshape.105), calls=%async_computation | async-start | bytes 1310720 | tf_op jit(solution)/shard_map/all_to_all | solution.py:225
  20.4 2.6 %copy-start.6 = (f32[2]{0:T(128)S(1)}, f32[2]{0:T(128)}, u32[]{:S(2)}) copy-start(f32[2]{0:T(128)} %constant.33.clone) | copy-start | bytes 28
  37.8 0.8 %copy-start.1 = (f32[16,80,128]{2,1,0:T(8,128)}, f32[16,80,128]{2,1,0:T(8,128)S(1)}, u32[]{:S(2)}) copy-start(f32[16,80,128]{2,1,0:T(8,128)S(1)} %all-to-all-done) | copy-start | bytes 1966084
  43.1 22.5 %collective-permute-start.1 = (f32[5,2,32,128]{3,2,1,0:T(8,128)}, f32[5,2,32,128]{3,2,1,0:T(8,128)S(1)}, u32[]{:S(2)}, u32[]{:S(2)}) collective-permute-start(f32[5,2,32,128]{3,2,1,0:T(8,128)} %get-tuple-element.11), channel_id=1, source_target_pairs={{0,16},{16,32},{32,48},{48,64},{64,80},{80,96},{96,112},{112,128},... | collective-permute-start | bytes 491528 | tf_op jit(solution)/shard_map/ppermute | solution.py:205
  47.1 18.6 %collective-permute-start.2 = (f32[5,2,32,128]{3,2,1,0:T(8,128)}, f32[5,2,32,128]{3,2,1,0:T(8,128)S(1)}, u32[]{:S(2)}, u32[]{:S(2)}) collective-permute-start(f32[5,2,32,128]{3,2,1,0:T(8,128)} %get-tuple-element.12), channel_id=1, source_target_pairs={{16,0},{32,16},{48,32},{64,48},{80,64},{96,80},{112,96},{128,112},... | collective-permute-start | bytes 491528 | tf_op jit(solution)/shard_map/ppermute | solution.py:205
  57.2 8.4 %collective-permute-start.3 = (f32[5,8,2,128]{3,2,1,0:T(2,128)}, f32[5,8,2,128]{3,2,1,0:T(2,128)S(1)}, u32[]{:S(2)}, u32[]{:S(2)}) collective-permute-start(f32[5,8,2,128]{3,2,1,0:T(2,128)} %get-tuple-element.13), channel_id=1, source_target_pairs={{0,1},{1,2},{2,3},{3,4},{4,5},{5,6},{6,7},{7,8},{8,9},{9,10},{10,1... | collective-permute-start | bytes 122888 | tf_op jit(solution)/shard_map/ppermute | solution.py:205
  59.1 6.5 %collective-permute-start.4 = (f32[5,8,2,128]{3,2,1,0:T(2,128)}, f32[5,8,2,128]{3,2,1,0:T(2,128)S(1)}, u32[]{:S(2)}, u32[]{:S(2)}) collective-permute-start(f32[5,8,2,128]{3,2,1,0:T(2,128)} %get-tuple-element.14), channel_id=1, source_target_pairs={{1,0},{2,1},{3,2},{4,3},{5,4},{6,5},{7,6},{8,7},{9,8},{10,9},{11,1... | collective-permute-start | bytes 122888 | tf_op jit(solution)/shard_map/ppermute | solution.py:205
  65.6 0.6 copy-start.4
  65.6 0.6 copy-start.5
  65.6 0.7 copy-start.2
  66.3 0.7 copy-start.3

commit v14 on v13

--- a/solution.py
+++ b/solution.py
@@ -120,12 +120,10 @@
 
 def exact_shift(v, shift):
     hi = v.astype(jnp.bfloat16)
-    rest = v - hi.astype(jnp.float32)
-    mid = rest.astype(jnp.bfloat16)
-    lo = (rest - mid.astype(jnp.float32)).astype(jnp.bfloat16)
+    mid = (v - hi.astype(jnp.float32)).astype(jnp.bfloat16)
     n = v.shape[0]
-    res = jnp.dot(jnp.concatenate([hi, mid, lo], axis=0), shift, preferred_element_type=jnp.float32)
-    return (res[:n] + res[n:2 * n]) + res[2 * n:]
+    res = jnp.dot(jnp.concatenate([hi, mid], axis=0), shift, preferred_element_type=jnp.float32)
+    return res[:n] + res[n:]
 
 
 def xterm_kernel(c_ref, u_ref, o_ref):

time: 70.4 us -> 69.9 us (level)
  no operation moved by 1% of the time
where the time goes in v14:
time: 69.9 us; the launch traced here: 69.4 us
  starting transfers between devices  30.5 us (44%)
  waiting for transfers between devices  13.4 us (19%)
  Pallas kernels  12.8 us (18%)
  local copies, waits for them, and re-layouts  7.74 us (11%)
  other arithmetic  4.76 us (7%)
    ppermute x2, starting transfers between devices, exchange(): lax.ppermute(bottom, axis, backward)  12.5 us
    all_to_all x1, waiting for transfers between devices, local(): lax.all_to_all(outgoing, 'tile', split_axis=0, concat_axis=0, tiled=True)  12.2 us
    all_to_all x1, starting transfers between devices, local(): lax.all_to_all(outgoing, 'tile', split_axis=0, concat_axis=0, tiled=True)  8.07 us
    ppermute x2, starting transfers between devices, exchange(): lax.ppermute(top, axis, forward)  5.9 us
    pallas_call x1, Pallas kernels, assemble(): pl.pallas_call(assemble_kernel, out_shape=[jax.ShapeDtypeStruct((fields,...  4.45 us
    ppermute x1, starting transfers between devices, local(): lax.ppermute(coarse_fine, 'slab', [(i, (i + 1) % slabs) for i in range(sl...  4 us
    pallas_call x1, Pallas kernels, xterm(): pl.pallas_call(xterm_kernel, in_specs=[pl.BlockSpec(memory_space=pltpu.SM...  3.53 us
    unnamed x17, local copies, waits for them, and re-layouts  3.25 us
  transfers between devices with their start and end apart: 6, of which 2 were waited for; matrix products, arithmetic and copies ran while one was open for 13% of the time, Pallas kernels for 8%

profile of v14, /device:TPU:7, one launch (start us, length us, event | category | flops | bytes accessed | tf_op | source)
XLA Modules:
  0.0 69.4 jit_solution(3012705827495718390)
XLA Ops:
  0.0 1.1 %copy.16 = f32[64,5,64]{2,1,0:T(8,128)S(1)} copy(f32[64,5,64]{2,0,1:T(8,128)} %param.8) | data formatting | bytes 163840 | tf_op args[1]
  1.1 4.0 %collective-permute-start = (f32[64,5,64]{2,1,0:T(8,128)S(1)}, f32[64,5,64]{2,1,0:T(8,128)S(1)}, u32[]{:S(2)}, u32[]{:S(2)}) collective-permute-start(f32[64,5,64]{2,1,0:T(8,128)S(1)} %copy.16), channel_id=1, source_target_pairs={{0,16},{16,32},{32,48},{48,64},{64,80},{80,96},{96,112},{112,128},... | collective-permute-start | bytes 245768 | tf_op jit(solution)/shard_map/ppermute | solution.py:214
  5.1 0.9 %convert_reduce_fusion = s32[64]{0:T(128)S(1)} fusion(s32[64]{0:T(128)} %bitcast.25), kind=kLoop, calls=%fused_computation.24 | loop fusion | flops 20416 | bytes 512 | tf_op jit(solution)/shard_map/reduce_sum | solution.py:219
  6.0 0.7 bitcast_select_fusion
  6.7 0.1 select_reduce_fusion
  6.9 1.5 %gather_fusion = f32[64,5,512]{2,0,1:T(8,128)S(1)} fusion(f32[64,5,512]{2,0,1:T(8,128)S(1)} %copy-done, s32[1024]{0:T(1024)S(1)} %pad_clamp_fusion.1), kind=kCustom, calls=%fused_computation | custom fusion | bytes 1310976 | tf_op jit(solution)/shard_map/gather | solution.py:222
  8.4 0.4 copy.15
  8.8 1.0 %reshape.105 = f32[16,80,128]{2,1,0:T(8,128)} reshape(f32[64,5,512]{2,1,0:T(8,128)S(1)} %copy.15) | data formatting | bytes 1310720 | tf_op jit(solution)/shard_map/reshape | solution.py:222
  9.8 8.1 %all-to-all-start = ((f32[16,80,128]{2,1,0:T(8,128)}), f32[16,80,128]{2,1,0:T(8,128)S(1)}, u32[]{:S(2)}, u32[]{:S(2)}) async-start(f32[16,80,128]{2,1,0:T(8,128)} %reshape.105), calls=%async_computation | async-start | bytes 1310720 | tf_op jit(solution)/shard_map/all_to_all | solution.py:223
  17.9 0.1 broadcast_in_dim.13
  17.9 0.7 broadcast_in_dim_reshape.2.src_ref
  18.6 1.8 %shard_map.73.p_ref = bf16[1024,512]{1,0:T(8,128)(2,1)} custom-call(s32[1,512]{1,0:T(1,128)} %broadcast_in_dim_reshape.2.src_ref), custom_call_target="tpu_custom_call" | custom-call | tf_op jit(solution)/shard_map/pallas_call | solution.py:90
  20.4 1.2 %collective-permute-done = f32[64,5,64]{2,1,0:T(8,128)S(1)} collective-permute-done((f32[64,5,64]{2,1,0:T(8,128)S(1)}, f32[64,5,64]{2,1,0:T(8,128)S(1)}, u32[]{:S(2)}, u32[]{:S(2)}) %collective-permute-start) | collective-permute-done | bytes 81952 | tf_op jit(solution)/shard_map/ppermute | solution.py:214
  21.7 0.6 gather_fusion.1
  22.3 0.1 copy.17
  22.5 0.4 minimum_maximum_fusion.2
  23.0 0.1 broadcast_multiply_fusion.2
  23.1 0.1 broadcast_multiply_fusion.1
  23.3 0.2 broadcast_multiply_fusion
  23.5 0.2 broadcast_add_fusion
  23.7 1.9 %add_add_fusion = f32[5,4,2,4,2,4,2,64]{7,6,5,4,3,2,1,0:T(2,128)} fusion(f32[5,4,4,4,2,64]{5,4,3,2,1,0:T(2,128)S(1)} %broadcast_multiply_fusion, f32[5,4,2,4,2,4,64]{6,5,4,3,2,1,0:T(4,128)S(1)} %broadcast_add_fusion, f32[5,4,4,4,64]{4,3,2,1,0:T(4,128)S(1)} %bitcast.22), kind=kLoop, calls=%fused_computation.2 | loop fusion | flops 327680 | bytes 1228800 | tf_op jit(solution)/shard_map/add | solution.py:39
  25.6 12.2 %all-to-all-done = f32[16,80,128]{2,1,0:T(8,128)S(1)} async-done(((f32[16,80,128]{2,1,0:T(8,128)}), f32[16,80,128]{2,1,0:T(8,128)S(1)}, u32[]{:S(2)}, u32[]{:S(2)}) %all-to-all-start) | async-done | bytes 655392 | tf_op jit(solution)/shard_map/all_to_all | solution.py:223
  37.8 0.8 %copy-done.1 = f32[16,80,128]{2,1,0:T(8,128)} copy-done((f32[16,80,128]{2,1,0:T(8,128)}, f32[16,80,128]{2,1,0:T(8,128)S(1)}, u32[]{:S(2)}) %copy-start.1) | copy-done | bytes 655384
  38.6 4.4 %shard_map.74 = (f32[5,8,32,128]{3,2,1,0:T(8,128)}, f32[5,2,32,128]{3,2,1,0:T(8,128)}, f32[5,2,32,128]{3,2,1,0:T(8,128)}, f32[5,8,2,128]{3,2,1,0:T(2,128)}, f32[5,8,2,128]{3,2,1,0:T(2,128)}) custom-call(f32[1280,128]{1,0:T(8,128)} %bitcast.23, f32[5,512,64]{2,1,0:T(8,128)} %bitcast.17, bf16[1024,512]{1,0:T(8,128)(2,1)} %shard_map.73.p_ref), custom_call_target="tpu_custom_call" | custom-call | tf_op jit(solution)/shard_map/pallas_call | solution.py:99
  43.1 4.0 %collective-permute-start.1 = (f32[5,2,32,128]{3,2,1,0:T(8,128)}, f32[5,2,32,128]{3,2,1,0:T(8,128)S(1)}, u32[]{:S(2)}, u32[]{:S(2)}) collective-permute-start(f32[5,2,32,128]{3,2,1,0:T(8,128)} %get-tuple-element.11), channel_id=1, source_target_pairs={{0,16},{16,32},{32,48},{48,64},{64,80},{80,96},{96,112},{112,128},... | collective-permute-start | bytes 491528 | tf_op jit(solution)/shard_map/ppermute | solution.py:203
  47.1 10.1 %collective-permute-start.2 = (f32[5,2,32,128]{3,2,1,0:T(8,128)}, f32[5,2,32,128]{3,2,1,0:T(8,128)S(1)}, u32[]{:S(2)}, u32[]{:S(2)}) collective-permute-start(f32[5,2,32,128]{3,2,1,0:T(8,128)} %get-tuple-element.12), channel_id=1, source_target_pairs={{16,0},{32,16},{48,32},{64,48},{80,64},{96,80},{112,96},{128,112},... | collective-permute-start | bytes 491528 | tf_op jit(solution)/shard_map/ppermute | solution.py:203
  57.2 1.9 %collective-permute-start.3 = (f32[5,8,2,128]{3,2,1,0:T(2,128)}, f32[5,8,2,128]{3,2,1,0:T(2,128)S(1)}, u32[]{:S(2)}, u32[]{:S(2)}) collective-permute-start(f32[5,8,2,128]{3,2,1,0:T(2,128)} %get-tuple-element.13), channel_id=1, source_target_pairs={{0,1},{1,2},{2,3},{3,4},{4,5},{5,6},{6,7},{7,8},{8,9},{9,10},{10,1... | collective-permute-start | bytes 122888 | tf_op jit(solution)/shard_map/ppermute | solution.py:203
  59.1 2.4 %collective-permute-start.4 = (f32[5,8,2,128]{3,2,1,0:T(2,128)}, f32[5,8,2,128]{3,2,1,0:T(2,128)S(1)}, u32[]{:S(2)}, u32[]{:S(2)}) collective-permute-start(f32[5,8,2,128]{3,2,1,0:T(2,128)} %get-tuple-element.14), channel_id=1, source_target_pairs={{1,0},{2,1},{3,2},{4,3},{5,4},{6,5},{7,6},{8,7},{9,8},{10,9},{11,1... | collective-permute-start | bytes 122888 | tf_op jit(solution)/shard_map/ppermute | solution.py:203
  61.5 3.5 %shard_map.75.tx_ref = f32[5,8,32,128]{3,2,1,0:T(8,128)} custom-call(f32[3,5]{1,0:T(4,128)} %c_ref.3, f32[5,8,32,128]{3,2,1,0:T(8,128)} %get-tuple-element.10.u_ref), custom_call_target="tpu_custom_call" | custom-call | tf_op jit(solution)/shard_map/pallas_call | solution.py:147
  65.1 0.6 copy-done.4
  65.8 0.7 copy-done.3
  66.4 3.0 %shard_map.76 = f32[5,8,32,128]{3,2,1,0:T(8,128)} custom-call(f32[3,5]{1,0:T(4,128)} %c_ref.3, f32[5,8,32,128]{3,2,1,0:T(8,128)} %get-tuple-element.10.u_ref, f32[5,2,32,128]{3,2,1,0:T(8,128)} %copy-done.2, f32[5,2,32,128]{3,2,1,0:T(8,128)} %copy-done.3, f32[5,8,2,128]{3,2,1,0:T(2,128)} %copy-done.4, f32[5,8,2,128]{3,2,1,0:T(2,128)} %copy-done.5, ...), custom_call_target="tpu_custom_call" | custom-call | tf_op jit(solution)/shard_map/pallas_call | solution.py:190
  (24 shorter events, 0.2 us)
Async XLA Ops:
  0.0 6.8 %copy-start = (f32[64,5,512]{2,0,1:T(8,128)S(1)}, f32[64,5,512]{2,0,1:T(8,128)}, u32[]{:S(2)}) copy-start(f32[64,5,512]{2,0,1:T(8,128)} %param.7) | copy-start | bytes 1966084
  1.1 20.6 %collective-permute-start = (f32[64,5,64]{2,1,0:T(8,128)S(1)}, f32[64,5,64]{2,1,0:T(8,128)S(1)}, u32[]{:S(2)}, u32[]{:S(2)}) collective-permute-start(f32[64,5,64]{2,1,0:T(8,128)S(1)} %copy.16), channel_id=1, source_target_pairs={{0,16},{16,32},{32,48},{48,64},{64,80},{80,96},{96,112},{112,128},... | collective-permute-start | bytes 245768 | tf_op jit(solution)/shard_map/ppermute | solution.py:214
  8.8 9.0 %copy-start.7 = (s32[1,1,64]{2,1,0:T(1,128)S(1)}, s32[1,1,64]{2,1,0:T(1,128)}, u32[]{:S(2)}) copy-start(s32[1,1,64]{2,1,0:T(1,128)} %param.11) | copy-start | bytes 772
  9.8 28.0 %all-to-all-start = ((f32[16,80,128]{2,1,0:T(8,128)}), f32[16,80,128]{2,1,0:T(8,128)S(1)}, u32[]{:S(2)}, u32[]{:S(2)}) async-start(f32[16,80,128]{2,1,0:T(8,128)} %reshape.105), calls=%async_computation | async-start | bytes 1310720 | tf_op jit(solution)/shard_map/all_to_all | solution.py:223
  20.4 2.6 %copy-start.6 = (f32[2]{0:T(128)S(1)}, f32[2]{0:T(128)}, u32[]{:S(2)}) copy-start(f32[2]{0:T(128)} %constant.33.clone) | copy-start | bytes 28
  37.8 0.8 %copy-start.1 = (f32[16,80,128]{2,1,0:T(8,128)}, f32[16,80,128]{2,1,0:T(8,128)S(1)}, u32[]{:S(2)}) copy-start(f32[16,80,128]{2,1,0:T(8,128)S(1)} %all-to-all-done) | copy-start | bytes 1966084
  43.1 22.0 %collective-permute-start.1 = (f32[5,2,32,128]{3,2,1,0:T(8,128)}, f32[5,2,32,128]{3,2,1,0:T(8,128)S(1)}, u32[]{:S(2)}, u32[]{:S(2)}) collective-permute-start(f32[5,2,32,128]{3,2,1,0:T(8,128)} %get-tuple-element.11), channel_id=1, source_target_pairs={{0,16},{16,32},{32,48},{48,64},{64,80},{80,96},{96,112},{112,128},... | collective-permute-start | bytes 491528 | tf_op jit(solution)/shard_map/ppermute | solution.py:203
  47.1 18.1 %collective-permute-start.2 = (f32[5,2,32,128]{3,2,1,0:T(8,128)}, f32[5,2,32,128]{3,2,1,0:T(8,128)S(1)}, u32[]{:S(2)}, u32[]{:S(2)}) collective-permute-start(f32[5,2,32,128]{3,2,1,0:T(8,128)} %get-tuple-element.12), channel_id=1, source_target_pairs={{16,0},{32,16},{48,32},{64,48},{80,64},{96,80},{112,96},{128,112},... | collective-permute-start | bytes 491528 | tf_op jit(solution)/shard_map/ppermute | solution.py:203
  57.2 7.9 %collective-permute-start.3 = (f32[5,8,2,128]{3,2,1,0:T(2,128)}, f32[5,8,2,128]{3,2,1,0:T(2,128)S(1)}, u32[]{:S(2)}, u32[]{:S(2)}) collective-permute-start(f32[5,8,2,128]{3,2,1,0:T(2,128)} %get-tuple-element.13), channel_id=1, source_target_pairs={{0,1},{1,2},{2,3},{3,4},{4,5},{5,6},{6,7},{7,8},{8,9},{9,10},{10,1... | collective-permute-start | bytes 122888 | tf_op jit(solution)/shard_map/ppermute | solution.py:203
  59.1 6.0 %collective-permute-start.4 = (f32[5,8,2,128]{3,2,1,0:T(2,128)}, f32[5,8,2,128]{3,2,1,0:T(2,128)S(1)}, u32[]{:S(2)}, u32[]{:S(2)}) collective-permute-start(f32[5,8,2,128]{3,2,1,0:T(2,128)} %get-tuple-element.14), channel_id=1, source_target_pairs={{1,0},{2,1},{3,2},{4,3},{5,4},{6,5},{7,6},{8,7},{9,8},{10,9},{11,1... | collective-permute-start | bytes 122888 | tf_op jit(solution)/shard_map/ppermute | solution.py:203
  65.1 0.6 copy-start.4
  65.1 0.6 copy-start.5
  65.1 0.7 copy-start.2
  65.8 0.7 copy-start.3
